TPU v7x, 256 devices: a whole 4x4x8 slice. The times are simulated.
256 devices in a mesh: dp: 4 (over y), seq: 16 (over z, core), tensor: 4 (over x).
Axes of the slice: x: 4, y: 4, z: 8, core: 2. Of those that a mesh axis runs over, the one named last changes fastest.
Arguments:
- queries: bfloat16 [16384, 8192], P(('dp', 'seq'), 'tensor'), parts along dimension 0, may hold values from -110 to 110
- keys_values: bfloat16 [16384, 2, 1024], P(('dp', 'seq'), None, 'tensor'), parts along dimension 0, may hold values from -4.5 to 4.5
- out_weight: bfloat16 [8192, 8192], P('tensor', 'seq'), may hold values from -0.1875 to 0.1875
- residual: bfloat16 [16384, 8192], P(('dp', 'tensor'), 'seq'), parts along dimension 0, may hold values from -3 to 3
- segments: int32 [16384], P('dp'), parts along dimension 0, may hold values from 0 to 3, never falling along the last dimension, each value on 1 to 2048 neighbouring positions
Outputs:
- layer_out: bfloat16 [16384, 8192], P(('dp', 'tensor'), 'seq'), parts along dimension 0
There are 4 independent parts, one for each index of `dp`. A program takes and returns all parts, laid end to end along the dimension named above; an argument that names none is the same for every part. Nothing has to cross between parts.
Inputs may be any that keep to these rules, and one draw needn't show every extreme that they name: `segments`: segment numbers never fall along the tokens.
All inputs are finite; a program needn't handle non-finite values.
Results may differ from a plain program's by a relative error of at most 0.0085.
Values may be sent and summed in bfloat16 or wider, within the bound.
No kernel may reach another device: no remote copies, remote signals or barrier semaphores. Data moves between devices by JAX's collectives and lax.ppermute only.
A program may use at most 128 MiB of HBM per device.

v0:
```python
import jax
import jax.numpy as jnp
import numpy as np
from jax import lax
from jax.sharding import PartitionSpec as P

H = 64
KVH = 8
HD = 128
L = 4096


def attend(query_all, pair_all, segments, heads_dev, kv_dev, group_size):
    all_rows = query_all.shape[0]
    seq_count = all_rows // L
    block_rows = min(512, L)
    head_map = np.array([0 // group_size], dtype=np.int32)
    query_four = query_all.reshape(seq_count, L, heads_dev, HD)
    key_heads = pair_all[:, 0, :].reshape(seq_count, L, kv_dev, HD)[:, :, head_map, :]
    value_heads = pair_all[:, 1, :].reshape(seq_count, L, kv_dev, HD)[:, :, head_map, :]
    doc_ids = segments.reshape(seq_count, L)
    score_scale = HD ** (-0.5)
    outputs = []
    for block_index in range(L // block_rows):
        first_row = block_index * block_rows
        key_end = first_row + block_rows
        query_block = query_four[:, first_row:key_end]
        raw_scores = (
            jnp.einsum(
                "sqhd,skhd->shqk",
                query_block,
                key_heads[:, :key_end],
                preferred_element_type=jnp.float32,
            )
            * score_scale
        )
        query_pos = first_row + jnp.arange(block_rows)[:, None]
        key_pos = jnp.arange(key_end)[None, :]
        same_doc = doc_ids[:, first_row:key_end, None] == doc_ids[:, None, :key_end]
        allowed = (key_pos <= query_pos)[None, None, :, :] & same_doc[:, None, :, :]
        masked = jnp.where(allowed, raw_scores, -1e30)
        highest = jnp.max(masked, axis=-1, keepdims=True)
        exponents = jnp.where(allowed, jnp.exp(masked - highest), 0.0)
        weights = (exponents / jnp.sum(exponents, axis=-1, keepdims=True)).astype(jnp.bfloat16)
        blended = jnp.einsum(
            "shqk,skhd->sqhd", weights, value_heads[:, :key_end], preferred_element_type=jnp.float32
        )
        outputs.append(blended.astype(jnp.bfloat16))
    return jnp.concatenate(outputs, axis=1).reshape(all_rows, heads_dev * HD)


def on_device(queries, keys_values, out_weight, residual, segments):
    n_seq = lax.axis_size("seq")
    tok_dev = queries.shape[0]
    heads_ten = queries.shape[1] // HD
    heads_dev = heads_ten // n_seq
    kv_ten = keys_values.shape[2] // HD
    group_size = H // KVH
    kv_dev = max(1, heads_dev // group_size)
    table = np.array(
        [
            target * heads_dev // group_size + member
            for target in range(n_seq)
            for member in range(kv_dev)
        ],
        dtype=np.int32,
    )
    picked = keys_values.reshape(tok_dev, 2, kv_ten, HD)[:, :, table, :].reshape(
        tok_dev, 2, n_seq * kv_dev * HD
    )
    query_slab = queries.reshape(tok_dev, 1, heads_ten * HD)
    query_all, pair_all = (
        lax.all_to_all(query_slab, "seq", split_axis=2, concat_axis=0, tiled=True),
        lax.all_to_all(picked, "seq", split_axis=2, concat_axis=0, tiled=True),
    )
    query_all = query_all.reshape(query_all.shape[0], heads_dev * HD)
    heads_out = attend(query_all, pair_all, segments, heads_dev, kv_dev, group_size)
    gathered = lax.all_gather(heads_out, "seq", axis=1, tiled=True)
    summed = lax.psum_scatter(
        jnp.dot(gathered, out_weight, preferred_element_type=jnp.float32),
        "tensor",
        scatter_dimension=0,
        tiled=True,
    )
    return (residual.astype(jnp.float32) + summed).astype(jnp.bfloat16)


def solution(mesh):
    placed = (
        P(("dp", "seq"), "tensor"),
        P(("dp", "seq"), None, "tensor"),
        P("tensor", "seq"),
        P(("dp", "tensor"), "seq"),
        P("dp"),
    )
    return jax.shard_map(
        on_device, mesh=mesh, in_specs=placed, out_specs=P(("dp", "tensor"), "seq"), check_vma=False
    )
```

profile of v0, /device:TPU:1, one launch (start us, length us, event | category | flops | bytes accessed | tf_op | source)
XLA Modules:
  0.0 371.0 jit_solution(6181886769436137936)
XLA Ops:
  6.5 0.0 copy-start
  6.5 6.1 %copy.31 = bf16[256,1,2048]{0,1,2:T(2,128)(2,1)} copy(bf16[256,1,2048]{2,0,1:T(8,128)(2,1)} %bitcast.269) | data formatting | bytes 2097152 | tf_op jit(solution)/shard_map/reshape | solution.py:71
  12.6 0.5 broadcast.241
  13.1 0.0 copy-start.5
  13.1 11.6 %reduce.38 = bf16[2048,256]{1,0:T(8,128)(2,1)S(1)} reduce(bf16[2048,1,256]{2,1,0:T(2,128)(2,1)} %bitcast.264, bf16[]{:T(256)} %broadcast.241), dimensions={1}, to_apply=%bitcast.225.reduce_sub_computation | reduce | bytes 2097154
  24.8 1.1 reshape.549
  25.9 10.0 %all-to-all-start.1 = ((bf16[16,2,16384]{2,1,0:T(2,128)(2,1)}), bf16[16,2,16384]{2,1,0:T(2,128)(2,1)S(1)}, u32[]{:S(2)}, u32[]{:S(2)}) async-start(bf16[16,2,16384]{2,1,0:T(2,128)(2,1)} %reshape.549), calls=%async_computation.1 | async-start | bytes 2097152 | tf_op jit(solution)/shard_map/all_to_all | solution.py:73
  35.9 1.8 copy.25
  37.7 1.1 copy.26
  38.8 0.0 copy-done.5
  38.8 2.1 gather_fusion
  40.9 3.9 %copy.27 = bf16[256,2,16,128]{0,3,2,1:T(8,128)(2,1)} copy(bf16[256,2,16,128]{3,0,1,2:T(8,128)(2,1)} %bitcast.265) | data formatting | bytes 4194304 | tf_op jit(solution)/shard_map/gather | solution.py:68
  44.9 0.0 copy-start.4
  44.9 5.8 %copy.28 = bf16[256,2,2048]{0,1,2:T(2,128)(2,1)} copy(bf16[256,2,2048]{0,2,1:T(8,128)(2,1)} %bitcast.266) | data formatting | bytes 4194304 | tf_op jit(solution)/shard_map/reshape | solution.py:68
  50.7 13.2 %all-to-all-done.1 = bf16[16,2,16384]{2,1,0:T(2,128)(2,1)S(1)} async-done(((bf16[16,2,16384]{2,1,0:T(2,128)(2,1)}), bf16[16,2,16384]{2,1,0:T(2,128)(2,1)S(1)}, u32[]{:S(2)}, u32[]{:S(2)}) %all-to-all-start.1) | async-done | bytes 1048608 | tf_op jit(solution)/shard_map/all_to_all | solution.py:73
  63.9 4.3 %all-to-all-start = ((bf16[256,2,2048]{0,1,2:T(2,128)(2,1)}), bf16[256,2,2048]{0,1,2:T(2,128)(2,1)}, u32[]{:S(2)}, u32[]{:S(2)}) async-start(bf16[256,2,2048]{0,1,2:T(2,128)(2,1)} %copy.28), calls=%async_computation | async-start | bytes 4194304 | tf_op jit(solution)/shard_map/all_to_all | solution.py:74
  68.2 0.6 all-gather.3.cloned.1.call-start
  68.8 0.0 copy-done.4
  69.0 3.5 reshape.550
  72.5 1.8 copy.33
  74.3 1.3 copy.32
  75.6 40.8 %all-to-all-done = bf16[256,2,2048]{0,1,2:T(2,128)(2,1)} async-done(((bf16[256,2,2048]{0,1,2:T(2,128)(2,1)}), bf16[256,2,2048]{0,1,2:T(2,128)(2,1)}, u32[]{:S(2)}, u32[]{:S(2)}) %all-to-all-start) | async-done | bytes 2097184 | tf_op jit(solution)/shard_map/all_to_all | solution.py:74
  116.4 3.2 copy.29
  119.5 0.0 copy-start.2
  119.6 4.0 %copy.30 = bf16[16,256,2,128]{3,1,0,2:T(8,128)(2,1)} copy(bf16[16,256,2,128]{1,3,0,2:T(8,128)(2,1)} %bitcast.267) | data formatting | bytes 4194304 | tf_op jit(solution)/shard_map/all_to_all | solution.py:74
  123.6 1.7 slice_bitcast_fusion.1
  125.3 0.0 copy-done.2
  125.3 0.4 fusion.84
  125.7 0.2 fusion.59
  125.9 1.1 fusion.36
  127.0 0.6 fusion.25
  127.6 0.7 fusion.51
  128.3 1.8 fusion.38
  130.1 0.9 fusion.85
  131.0 1.3 fusion.24
  132.3 1.9 fusion.48
  134.2 1.1 fusion.12
  135.3 1.5 fusion.21
  136.8 2.6 fusion.46
  139.4 1.3 fusion.86
  140.7 2.0 fusion.14
  142.8 2.6 fusion.44
  145.4 1.5 fusion.6
  146.9 2.2 fusion.15
  149.1 3.6 fusion.42
  152.8 1.8 fusion.87
  154.5 2.9 fusion.8
  157.4 0.0 copy-start.1
  157.4 3.4 fusion.40
  160.8 0.0 copy-done.1
  160.8 1.9 fusion.3
  162.8 2.9 fusion.9
  165.7 4.6 %fusion.50 = bf16[1,4096,1,128]{1,3,2,0:T(8,128)(2,1)} fusion(bf16[1,4096,1,128]{1,3,2,0:T(8,128)(2,1)} %fusion.40, f32[4096,512]{1,0:T(8,128)S(1)} %get-tuple-element.30, f32[512]{0:T(512)S(1)} %fusion.9, f32[512]{0:T(512)S(1)} %get-tuple-element.29, s32[512]{0:T(512)S(1)} %bitcast.300, s32[512]{0:T(512)S(1)} %iota_add_fusion, s32[4096]{0:T(1024)S(1)} %copy-done.4, ...), kind=kOutput, calls=%fused_computation.83 | convolution fusion | flops 555810816 | bytes 9592832 | tf_op jit(solution)/shard_map/shqk,skhd->sqhd/dot_general | solution.py:45
  170.3 0.0 all-gather.3.cloned.1.call-update
  170.3 0.0 reduce-scatter.2.cloned.1.call-start
  170.4 94.6 %all-gather.3.cloned.1.call-done = bf16[1,4096,1,2048]{1,3,2,0:T(8,128)(2,1)} async-done(((bf16[1,4096,1,128]{1,3,2,0:T(8,128)(2,1)}), bf16[1,4096,1,2048]{1,3,2,0:T(8,128)(2,1)}) %all-gather.3.cloned.1.call-update) | async-done | bytes 16777232 | tf_op jit(solution)/shard_map/all_gather | solution.py:78
  264.9 0.0 copy-done
  264.9 14.7 %fusion = f32[4096,512]{1,0:T(8,128)} fusion(bf16[2048,512]{1,0:T(8,128)(2,1)S(1)} %copy-done, bf16[1,4096,1,2048]{1,3,2,0:T(8,128)(2,1)} %all-gather.3.cloned.1.call-done), kind=kOutput, calls=%fused_computation.1 | convolution fusion | flops 8589934592 | bytes 27262976 | tf_op jit(solution)/shard_map/dot_general | solution.py:80
  279.7 0.0 copy-start.3
  279.7 0.0 reduce-scatter.2.cloned.1.call-update
  279.7 81.3 %reduce-scatter.2.cloned.1.call-done = f32[1024,512]{1,0:T(8,128)} async-done(((f32[4096,512]{1,0:T(8,128)}), f32[1024,512]{1,0:T(8,128)}) %reduce-scatter.2.cloned.1.call-update) | async-done | bytes 2097168 | tf_op jit(solution)/shard_map/reduce_scatter | solution.py:79
  361.0 0.0 copy-done.3
  361.0 2.9 add_convert_fusion
  (15 shorter events, 0.1 us)
Async XLA Ops:
  6.5 258.4 %copy-start = (bf16[2048,512]{1,0:T(8,128)(2,1)S(1)}, bf16[2048,512]{1,0:T(8,128)(2,1)}, u32[]{:S(2)}) copy-start(bf16[2048,512]{1,0:T(8,128)(2,1)} %param.12) | copy-start | bytes 6291460
  13.1 25.7 %copy-start.5 = (s32[16]{0:T(128)S(1)}, s32[16]{0:T(128)}, u32[]{:S(2)}) copy-start(s32[16]{0:T(128)} %constant.15) | copy-start | bytes 196
  25.9 38.0 %all-to-all-start.1 = ((bf16[16,2,16384]{2,1,0:T(2,128)(2,1)}), bf16[16,2,16384]{2,1,0:T(2,128)(2,1)S(1)}, u32[]{:S(2)}, u32[]{:S(2)}) async-start(bf16[16,2,16384]{2,1,0:T(2,128)(2,1)} %reshape.549), calls=%async_computation.1 | async-start | bytes 2097152 | tf_op jit(solution)/shard_map/all_to_all | solution.py:73
  44.9 23.9 %copy-start.4 = (s32[4096]{0:T(1024)S(1)}, s32[4096]{0:T(1024)}, u32[]{:S(2)}) copy-start(s32[4096]{0:T(1024)} %param.14) | copy-start | bytes 49156
  63.9 52.5 %all-to-all-start = ((bf16[256,2,2048]{0,1,2:T(2,128)(2,1)}), bf16[256,2,2048]{0,1,2:T(2,128)(2,1)}, u32[]{:S(2)}, u32[]{:S(2)}) async-start(bf16[256,2,2048]{0,1,2:T(2,128)(2,1)} %copy.28), calls=%async_computation | async-start | bytes 4194304 | tf_op jit(solution)/shard_map/all_to_all | solution.py:74
  68.2 196.7 %all-gather.3.cloned.1.call-start = ((), (), s32[]{:S(2)}) async-start(), calls=%async_computation.4 | async-start | bytes 17825792 | tf_op jit(solution)/shard_map/all_gather | solution.py:78
  119.5 5.7 %copy-start.2 = (bf16[16,256,1,128]{3,1,0,2:T(8,128)(2,1)S(1)}, bf16[16,256,1,128]{3,1,0,2:T(8,128)(2,1)}, u32[]{:S(2)}) copy-start(bf16[16,256,1,128]{3,1,0,2:T(8,128)(2,1)} %copy.32) | copy-start | bytes 3145732
  157.4 3.4 copy-start.1
  170.3 190.7 %reduce-scatter.2.cloned.1.call-start = ((), (), s32[]{:S(2)}) async-start(), calls=%async_computation.3 | async-start | bytes 10485760 | tf_op jit(solution)/shard_map/reduce_scatter | solution.py:79
  279.7 81.3 %copy-start.3 = (bf16[1024,512]{1,0:T(8,128)(2,1)S(1)}, bf16[1024,512]{1,0:T(8,128)(2,1)}, u32[]{:S(2)}) copy-start(bf16[1024,512]{1,0:T(8,128)(2,1)} %param.13) | copy-start | bytes 3145732
Sparse Core Ops, SparseCore 0:
  170.4 94.4 all-gather.2
  279.8 81.1 reduce-scatter.1
where the time goes:
time: 376 us; the launch traced here: 371 us
  waiting for transfers between devices  230 us (61%)
  matrix products  45.8 us (12%)
  local copies, waits for them, and re-layouts  38 us (10%)
  other arithmetic  28.4 us (8%)
  starting transfers between devices  14.9 us (4%)
  between operations  13.9 us (4%)
    all_gather x1, waiting for transfers between devices, on_device(): gathered = lax.all_gather(heads_out, 'seq', axis=1, tiled=True)  94.6 us
    reduce_scatter x1, waiting for transfers between devices, on_device(): lax.psum_scatter(jnp.dot(gathered, out_weight, preferred_element_type=jnp...  81.3 us
    all_to_all x1, waiting for transfers between devices, on_device(): lax.all_to_all(picked, 'seq', split_axis=2, concat_axis=0, tiled=True)  40.8 us
    dot_general x8, matrix products, attend(): jnp.einsum('shqk,skhd->sqhd', weights, value_heads[:, :key_end], preferre...  21.7 us
    dot_general x1, matrix products, on_device(): jnp.dot(gathered, out_weight, preferred_element_type=jnp.float32)  14.7 us
    reduce_sum x8, other arithmetic, attend(): jnp.sum(exponents, axis=-1, keepdims=True)  13.8 us
    all_to_all x1, waiting for transfers between devices, on_device(): lax.all_to_all(query_slab, 'seq', split_axis=2, concat_axis=0, tiled=True)  13.2 us
    unnamed x1, other arithmetic  11.6 us
  transfers between devices with their start and end apart: 4, of which 4 were waited for; matrix products, arithmetic and copies ran while one was open for 6% of the time, Pallas kernels for 0%

commit v1 on v0

v1 whole, which is shorter than its diff:
```python
import jax
import jax.numpy as jnp
import numpy as np
from jax import lax
from jax.sharding import PartitionSpec as P

H = 64
KVH = 8
HD = 128
L = 4096
CHUNKS = 4


def attend_rows(query_head, key_head, value_head, doc_ids, first_row, rows):
    key_end = first_row + rows
    query_block = query_head[first_row:key_end]
    raw_scores = (
        jnp.einsum(
            "qd,kd->qk",
            query_block,
            key_head[:key_end],
            preferred_element_type=jnp.float32,
        )
        * HD ** (-0.5)
    )
    query_pos = first_row + jnp.arange(rows)[:, None]
    key_pos = jnp.arange(key_end)[None, :]
    same_doc = doc_ids[first_row:key_end, None] == doc_ids[None, :key_end]
    allowed = (key_pos <= query_pos) & same_doc
    masked = jnp.where(allowed, raw_scores, -1e30)
    highest = jnp.max(masked, axis=-1, keepdims=True)
    exponents = jnp.where(allowed, jnp.exp(masked - highest), 0.0)
    weights = (exponents / jnp.sum(exponents, axis=-1, keepdims=True)).astype(jnp.bfloat16)
    blended = jnp.einsum(
        "qk,kd->qd", weights, value_head[:key_end], preferred_element_type=jnp.float32
    )
    return blended.astype(jnp.bfloat16)


def on_device(queries, keys_values, out_weight, residual, segments):
    n_seq = lax.axis_size("seq")
    n_ten = lax.axis_size("tensor")
    seq_idx = lax.axis_index("seq")
    tok_dev = queries.shape[0]
    heads_ten = queries.shape[1] // HD
    heads_dev = heads_ten // n_seq
    assert heads_dev == 1
    group_size = H // KVH
    query_slab = queries.reshape(tok_dev, 1, heads_ten * HD)
    query_all = lax.all_to_all(query_slab, "seq", split_axis=2, concat_axis=0, tiled=True)
    query_head = query_all.reshape(query_all.shape[0], HD)
    rows_all = query_head.shape[0]
    assert rows_all == L
    pair_all = lax.all_gather(keys_values, "seq", axis=0, tiled=True)
    kv_local = seq_idx // group_size
    pair_head = lax.dynamic_slice_in_dim(pair_all, kv_local * HD, HD, axis=2)
    key_head = pair_head[:, 0, :]
    value_head = pair_head[:, 1, :]
    doc_ids = segments
    out_rows = rows_all // n_ten
    block_rows = out_rows // CHUNKS
    pieces = []
    for chunk in range(CHUNKS):
        blocks = [
            attend_rows(query_head, key_head, value_head, doc_ids, part * out_rows + chunk * block_rows, block_rows)
            for part in range(n_ten)
        ]
        chunk_heads = jnp.concatenate(blocks, axis=0)
        gathered = lax.all_gather(chunk_heads, "seq", axis=1, tiled=True)
        projected = jnp.dot(gathered, out_weight, preferred_element_type=jnp.float32)
        pieces.append(lax.psum_scatter(projected, "tensor", scatter_dimension=0, tiled=True))
    summed = jnp.concatenate(pieces, axis=0)
    return (residual.astype(jnp.float32) + summed).astype(jnp.bfloat16)


def solution(mesh):
    placed = (
        P(("dp", "seq"), "tensor"),
        P(("dp", "seq"), None, "tensor"),
        P("tensor", "seq"),
        P(("dp", "tensor"), "seq"),
        P("dp"),
    )
    return jax.shard_map(
        on_device, mesh=mesh, in_specs=placed, out_specs=P(("dp", "tensor"), "seq"), check_vma=False
    )
```

time: 376 us -> 439 us (1.17)
  waiting for transfers between devices: 230 us -> 299 us
  local copies, waits for them, and re-layouts: 38 us -> 15.3 us
  matrix products: 45.8 us -> 62.3 us
  other arithmetic: 28.4 us -> 33.2 us
    reduce_scatter x1 -> x4, waiting for transfers between devices: 81.3 us -> 130 us  [on_device(): lax.psum_scatter(projected, 'tensor', scatter_dimension=0, tiled=True)]
    all_to_all x1 -> x0, waiting for transfers between devices: 40.8 us -> none  [on_device(): lax.all_to_all(picked, 'seq', split_axis=2, concat_axis=0, tiled=True)]
    all_gather x1 -> x5, waiting for transfers between devices: 94.6 us -> 134 us  [the longest x4 134 us: on_device(): gathered = lax.all_gather(chunk_heads, 'seq', axis=1, tiled=True)]
    all_to_all x1, waiting for transfers between devices: 13.2 us -> 34.6 us  [on_device(): lax.all_to_all(query_slab, 'seq', split_axis=2, concat_axis=0, tiled=True)]
    dot_general x1 -> x4, matrix products: 14.7 us -> 23.4 us  [on_device(): jnp.dot(gathered, out_weight, preferred_element_type=jnp.float32)]
    all_to_all x3 -> x0, local copies, waits for them, and re-layouts: 8.51 us -> none  [the longest x2 7.2 us: on_device(): lax.all_to_all(picked, 'seq', split_axis=2, concat_axis=0, tiled=True)]
    gather x3 -> x0, local copies, waits for them, and re-layouts: 7.72 us -> none  [the longest x2 6.04 us: on_device(): keys_values.reshape(tok_dev, 2, kv_ten, HD)[:, :, table, :]]
    dot_general x16 -> x32, matrix products: 31.1 us -> 38.8 us  [the longest x16 21 us: attend_rows(): jnp.einsum('qk,kd->qd', weights, value_head[:key_end], preferred_element_...]
  transfers between devices with their start and end apart: 4 -> 10, of which waited for: 4 -> 9; matrix products, arithmetic and copies ran while one was open for 6% -> 21% of each run, Pallas kernels for 0% -> 0%
where the time goes in v1:
time: 439 us; the launch traced here: 435 us
  waiting for transfers between devices  299 us (68%)
  matrix products  62.3 us (14%)
  other arithmetic  33.2 us (8%)
  local copies, waits for them, and re-layouts  15.3 us (3%)
  between operations  13.9 us (3%)
  starting transfers between devices  11.6 us (3%)
    all_gather x4, waiting for transfers between devices, on_device(): gathered = lax.all_gather(chunk_heads, 'seq', axis=1, tiled=True)  134 us
    reduce_scatter x4, waiting for transfers between devices, on_device(): lax.psum_scatter(projected, 'tensor', scatter_dimension=0, tiled=True)  130 us
    all_to_all x1, waiting for transfers between devices, on_device(): lax.all_to_all(query_slab, 'seq', split_axis=2, concat_axis=0, tiled=True)  34.6 us
    dot_general x4, matrix products, on_device(): jnp.dot(gathered, out_weight, preferred_element_type=jnp.float32)  23.4 us
    dot_general x16, matrix products, attend_rows(): jnp.einsum('qk,kd->qd', weights, value_head[:key_end], preferred_element_...  21 us
    dot_general x16, matrix products, attend_rows(): jnp.einsum('qd,kd->qk', query_block, key_head[:key_end], preferred_elemen...  17.8 us
    reduce_sum x16, other arithmetic, attend_rows(): jnp.sum(exponents, axis=-1, keepdims=True)  15.8 us
    unnamed x1, other arithmetic  11.6 us
  transfers between devices with their start and end apart: 10, of which 9 were waited for; matrix products, arithmetic and copies ran while one was open for 21% of the time, Pallas kernels for 0%

profile of v1, /device:TPU:1, one launch (start us, length us, event | category | flops | bytes accessed | tf_op | source)
XLA Modules:
  0.0 435.5 jit_solution(1249033622516324133)
XLA Ops:
  6.5 1.8 copy.43
  8.4 5.9 %copy.44 = bf16[256,1,2048]{0,1,2:T(2,128)(2,1)} copy(bf16[256,1,2048]{2,0,1:T(8,128)(2,1)} %bitcast.316) | data formatting | bytes 2097152 | tf_op jit(solution)/shard_map/reshape | solution.py:49
  14.8 11.6 %reduce = bf16[2048,256]{1,0:T(8,128)(2,1)S(1)} reduce(bf16[2048,1,256]{2,1,0:T(2,128)(2,1)} %bitcast.306, bf16[]{:T(256)} %broadcast.172), dimensions={1}, to_apply=%bitcast.228.reduce_sub_computation | reduce | bytes 2097154
  26.5 1.1 reshape.191
  27.6 10.0 %all-to-all-start = ((bf16[16,2,16384]{2,1,0:T(2,128)(2,1)}), bf16[16,2,16384]{2,1,0:T(2,128)(2,1)S(1)}, u32[]{:S(2)}, u32[]{:S(2)}) async-start(bf16[16,2,16384]{2,1,0:T(2,128)(2,1)} %reshape.191), calls=%async_computation | async-start | bytes 2097152 | tf_op jit(solution)/shard_map/all_to_all | solution.py:50
  38.0 34.6 %all-to-all-done = bf16[16,2,16384]{2,1,0:T(2,128)(2,1)S(1)} async-done(((bf16[16,2,16384]{2,1,0:T(2,128)(2,1)}), bf16[16,2,16384]{2,1,0:T(2,128)(2,1)S(1)}, u32[]{:S(2)}, u32[]{:S(2)}) %all-to-all-start) | async-done | bytes 1048608 | tf_op jit(solution)/shard_map/all_to_all | solution.py:50
  72.5 3.5 reshape.192
  76.0 1.8 copy.61
  77.8 3.2 fusion.130
  81.0 1.9 fusion.30
  83.1 0.9 fusion.131
  84.0 1.4 fusion.39
  85.5 0.6 fusion.132
  86.1 0.7 fusion.52
  87.6 2.3 fusion.65
  89.8 1.7 fusion.69
  91.6 1.1 convolution_convert_fusion.1
  92.7 0.6 convolution_convert_fusion.2
  93.3 0.7 pad_maximum_fusion.3
  94.4 1.3 fusion.137
  96.0 1.6 convolution_convert_fusion.4
  98.0 0.6 fusion.136
  98.5 1.0 fusion.59
  99.5 0.8 fusion.135
  100.3 1.3 fusion.41
  101.7 1.1 fusion.134
  102.8 1.8 fusion.32
  104.6 1.0 convolution_convert_fusion.3
  105.6 1.6 fusion.68
  107.2 2.2 fusion.64
  109.3 0.7 pad_maximum_fusion.2
  110.7 1.3 fusion.141
  112.2 1.5 fusion.140
  114.7 0.8 fusion.139
  115.5 1.2 fusion.45
  116.7 1.0 fusion.138
  117.7 0.9 convolution_convert_fusion
  118.6 1.8 fusion.33
  120.4 1.4 fusion.67
  121.8 2.0 fusion.63
  123.8 0.7 pad_maximum_fusion.1
  124.8 1.2 fusion.145
  126.2 1.4 fusion.144
  128.4 0.7 fusion.143
  129.1 1.1 fusion.48
  130.2 1.0 fusion.142
  131.2 0.7 convolution_convert_fusion.6
  131.9 1.6 fusion.35
  133.5 1.3 fusion.66
  134.8 1.9 fusion.70
  136.8 0.7 pad_maximum_fusion
  137.6 4.4 %all-gather.14.cloned.1.call-done = bf16[1024,2048]{1,0:T(8,128)(2,1)} async-done(((bf16[1024,128]{1,0:T(8,128)(2,1)}), bf16[1024,2048]{1,0:T(8,128)(2,1)}) %all-gather.14.cloned.1.call-update) | async-done | bytes 4194320 | tf_op jit(solution)/shard_map/all_gather | solution.py:69
  141.9 5.9 %fusion.149 = f32[1024,512]{1,0:T(8,128)} fusion(bf16[1024,2048]{1,0:T(8,128)(2,1)} %all-gather.14.cloned.1.call-done, bf16[2048,512]{1,0:T(8,128)(2,1)S(1)} %copy-done), kind=kOutput, calls=%fused_computation.289 | convolution fusion | flops 2147483648 | bytes 8388608 | tf_op jit(solution)/shard_map/dot_general | solution.py:70
  147.9 43.4 %all-gather.12.cloned.1.call-done = bf16[1024,2048]{1,0:T(8,128)(2,1)} async-done(((bf16[1024,128]{1,0:T(8,128)(2,1)}), bf16[1024,2048]{1,0:T(8,128)(2,1)}) %all-gather.12.cloned.1.call-update) | async-done | bytes 4194320 | tf_op jit(solution)/shard_map/all_gather | solution.py:69
  191.2 5.9 %fusion.148 = f32[1024,512]{1,0:T(8,128)} fusion(bf16[1024,2048]{1,0:T(8,128)(2,1)} %all-gather.12.cloned.1.call-done, bf16[2048,512]{1,0:T(8,128)(2,1)S(1)} %copy-done), kind=kOutput, calls=%fused_computation.288 | convolution fusion | flops 2147483648 | bytes 8388608 | tf_op jit(solution)/shard_map/dot_general | solution.py:70
  197.4 43.1 %all-gather.10.cloned.1.call-done = bf16[1024,2048]{1,0:T(8,128)(2,1)} async-done(((bf16[1024,128]{1,0:T(8,128)(2,1)}), bf16[1024,2048]{1,0:T(8,128)(2,1)}) %all-gather.10.cloned.1.call-update) | async-done | bytes 4194320 | tf_op jit(solution)/shard_map/all_gather | solution.py:69
  240.4 5.9 %fusion.147 = f32[1024,512]{1,0:T(8,128)} fusion(bf16[1024,2048]{1,0:T(8,128)(2,1)} %all-gather.10.cloned.1.call-done, bf16[2048,512]{1,0:T(8,128)(2,1)S(1)} %copy-done), kind=kOutput, calls=%fused_computation.287 | convolution fusion | flops 2147483648 | bytes 8388608 | tf_op jit(solution)/shard_map/dot_general | solution.py:70
  246.4 43.3 %all-gather.8.cloned.1.call-done = bf16[1024,2048]{1,0:T(8,128)(2,1)} async-done(((bf16[1024,128]{1,0:T(8,128)(2,1)}), bf16[1024,2048]{1,0:T(8,128)(2,1)}) %all-gather.8.cloned.1.call-update) | async-done | bytes 4194320 | tf_op jit(solution)/shard_map/all_gather | solution.py:69
  289.6 5.8 %fusion.146 = f32[1024,512]{1,0:T(8,128)} fusion(bf16[1024,2048]{1,0:T(8,128)(2,1)} %all-gather.8.cloned.1.call-done, bf16[2048,512]{1,0:T(8,128)(2,1)S(1)} %copy-done), kind=kOutput, calls=%fused_computation.286 | convolution fusion | flops 2147483648 | bytes 8388608 | tf_op jit(solution)/shard_map/dot_general | solution.py:70
  295.5 26.6 %reduce-scatter.11.cloned.1.call-done = f32[256,512]{1,0:T(8,128)} async-done(((f32[1024,512]{1,0:T(8,128)}), f32[256,512]{1,0:T(8,128)}) %reduce-scatter.11.cloned.1.call-update) | async-done | bytes 524304 | tf_op jit(solution)/shard_map/reduce_scatter | solution.py:71
  322.1 34.6 %reduce-scatter.9.cloned.1.call-done = f32[256,512]{1,0:T(8,128)} async-done(((f32[1024,512]{1,0:T(8,128)}), f32[256,512]{1,0:T(8,128)}) %reduce-scatter.9.cloned.1.call-update) | async-done | bytes 524304 | tf_op jit(solution)/shard_map/reduce_scatter | solution.py:71
  356.7 34.6 %reduce-scatter.7.cloned.1.call-done = f32[256,512]{1,0:T(8,128)} async-done(((f32[1024,512]{1,0:T(8,128)}), f32[256,512]{1,0:T(8,128)}) %reduce-scatter.7.cloned.1.call-update) | async-done | bytes 524304 | tf_op jit(solution)/shard_map/reduce_scatter | solution.py:71
  391.3 34.6 %reduce-scatter.5.cloned.1.call-done = f32[256,512]{1,0:T(8,128)} async-done(((f32[1024,512]{1,0:T(8,128)}), f32[256,512]{1,0:T(8,128)}) %reduce-scatter.5.cloned.1.call-update) | async-done | bytes 524304 | tf_op jit(solution)/shard_map/reduce_scatter | solution.py:71
  425.9 2.8 fusion.36
  (69 shorter events, 6.1 us)
Async XLA Ops:
  6.5 135.4 %copy-start = (bf16[2048,512]{1,0:T(8,128)(2,1)S(1)}, bf16[2048,512]{1,0:T(8,128)(2,1)}, u32[]{:S(2)}) copy-start(bf16[2048,512]{1,0:T(8,128)(2,1)} %param.7) | copy-start | bytes 6291460
  6.5 71.3 %all-gather.6.cloned.1.call-start = ((), (), s32[]{:S(2)}) async-start(), calls=%async_computation.5 | async-start | bytes 4456448 | tf_op jit(solution)/shard_map/all_gather | solution.py:54
  26.5 11.4 %copy-start.1 = (s32[4096]{0:T(1024)S(1)}, s32[4096]{0:T(1024)}, u32[]{:S(2)}) copy-start(s32[4096]{0:T(1024)} %param.9) | copy-start | bytes 49156
  27.6 44.9 %all-to-all-start = ((bf16[16,2,16384]{2,1,0:T(2,128)(2,1)}), bf16[16,2,16384]{2,1,0:T(2,128)(2,1)S(1)}, u32[]{:S(2)}, u32[]{:S(2)}) async-start(bf16[16,2,16384]{2,1,0:T(2,128)(2,1)} %reshape.191), calls=%async_computation | async-start | bytes 2097152 | tf_op jit(solution)/shard_map/all_to_all | solution.py:50
  37.6 104.4 %all-gather.14.cloned.1.call-start = ((), (), s32[]{:S(2)}) async-start(), calls=%async_computation.12 | async-start | bytes 4456448 | tf_op jit(solution)/shard_map/all_gather | solution.py:69
  81.0 2.2 copy-start.3
  94.0 97.2 %all-gather.12.cloned.1.call-start = ((), (), s32[]{:S(2)}) async-start(), calls=%async_computation.10 | async-start | bytes 4456448 | tf_op jit(solution)/shard_map/all_gather | solution.py:69
  95.7 2.3 copy-start.4
  110.1 130.3 %all-gather.10.cloned.1.call-start = ((), (), s32[]{:S(2)}) async-start(), calls=%async_computation.8 | async-start | bytes 4456448 | tf_op jit(solution)/shard_map/all_gather | solution.py:69
  110.7 3.6 copy-start.5
  124.5 165.1 %all-gather.8.cloned.1.call-start = ((), (), s32[]{:S(2)}) async-start(), calls=%async_computation.6 | async-start | bytes 4456448 | tf_op jit(solution)/shard_map/all_gather | solution.py:69
  124.8 3.3 copy-start.6
  137.5 184.6 %reduce-scatter.11.cloned.1.call-start = ((), (), s32[]{:S(2)}) async-start(), calls=%async_computation.13 | async-start | bytes 2621440 | tf_op jit(solution)/shard_map/reduce_scatter | solution.py:71
  147.8 208.9 %reduce-scatter.9.cloned.1.call-start = ((), (), s32[]{:S(2)}) async-start(), calls=%async_computation.11 | async-start | bytes 2621440 | tf_op jit(solution)/shard_map/reduce_scatter | solution.py:71
  197.1 194.2 %reduce-scatter.7.cloned.1.call-start = ((), (), s32[]{:S(2)}) async-start(), calls=%async_computation.9 | async-start | bytes 2621440 | tf_op jit(solution)/shard_map/reduce_scatter | solution.py:71
  246.3 179.6 %copy-start.2 = (bf16[1024,512]{1,0:T(8,128)(2,1)S(1)}, bf16[1024,512]{1,0:T(8,128)(2,1)}, u32[]{:S(2)}) copy-start(bf16[1024,512]{1,0:T(8,128)(2,1)} %param.8) | copy-start | bytes 3145732
  246.3 179.5 %reduce-scatter.5.cloned.1.call-start = ((), (), s32[]{:S(2)}) async-start(), calls=%async_computation.7 | async-start | bytes 2621440 | tf_op jit(solution)/shard_map/reduce_scatter | solution.py:71
Sparse Core Ops, SparseCore 0:
  9.2 64.9 all-gather.5
  94.2 47.7 all-gather.13
  143.7 47.5 all-gather.11
  192.8 47.5 all-gather.9
  242.0 47.5 all-gather.7
  292.0 30.0 reduce-scatter.10
  324.7 31.9 reduce-scatter.8
  359.2 31.9 reduce-scatter.6
  393.8 32.0 reduce-scatter.4

commit v2 on v0

v2 whole, which is shorter than its diff:
```python
import jax
import jax.numpy as jnp
import numpy as np
from jax import lax
from jax.sharding import PartitionSpec as P

H = 64
KVH = 8
HD = 128
L = 4096


def attend(query_head, key_head, value_head, doc_ids):
    rows_all = query_head.shape[0]
    block_rows = min(512, rows_all)
    score_scale = HD ** (-0.5)
    outputs = []
    for block_index in range(rows_all // block_rows):
        first_row = block_index * block_rows
        key_end = first_row + block_rows
        raw_scores = (
            jnp.einsum(
                "qd,kd->qk",
                query_head[first_row:key_end],
                key_head[:key_end],
                preferred_element_type=jnp.float32,
            )
            * score_scale
        )
        query_pos = first_row + jnp.arange(block_rows)[:, None]
        key_pos = jnp.arange(key_end)[None, :]
        same_doc = doc_ids[first_row:key_end, None] == doc_ids[None, :key_end]
        allowed = (key_pos <= query_pos) & same_doc
        masked = jnp.where(allowed, raw_scores, -1e30)
        highest = jnp.max(masked, axis=-1, keepdims=True)
        exponents = jnp.where(allowed, jnp.exp(masked - highest), 0.0)
        weights = (exponents / jnp.sum(exponents, axis=-1, keepdims=True)).astype(jnp.bfloat16)
        blended = jnp.einsum(
            "qk,kd->qd", weights, value_head[:key_end], preferred_element_type=jnp.float32
        )
        outputs.append(blended.astype(jnp.bfloat16))
    return jnp.concatenate(outputs, axis=0)


def on_device(queries, keys_values, out_weight, residual, segments):
    n_seq = lax.axis_size("seq")
    seq_idx = lax.axis_index("seq")
    tok_dev = queries.shape[0]
    heads_ten = queries.shape[1] // HD
    assert heads_ten == n_seq
    group_size = H // KVH
    head_major = jnp.transpose(queries.reshape(tok_dev, heads_ten, HD), (1, 0, 2))
    query_parts = lax.all_to_all(head_major, "seq", split_axis=0, concat_axis=0, tiled=True)
    query_head = query_parts.reshape(n_seq * tok_dev, HD)
    assert query_head.shape[0] == L
    pair_all = lax.all_gather(keys_values, "seq", axis=0, tiled=True)
    pair_head = lax.dynamic_slice_in_dim(pair_all, (seq_idx // group_size) * HD, HD, axis=2)
    heads_out = attend(query_head, pair_head[:, 0, :], pair_head[:, 1, :], segments)
    gathered = lax.all_gather(heads_out, "seq", axis=1, tiled=True)
    summed = lax.psum_scatter(
        jnp.dot(gathered, out_weight, preferred_element_type=jnp.float32),
        "tensor",
        scatter_dimension=0,
        tiled=True,
    )
    return (residual.astype(jnp.float32) + summed).astype(jnp.bfloat16)


def solution(mesh):
    placed = (
        P(("dp", "seq"), "tensor"),
        P(("dp", "seq"), None, "tensor"),
        P("tensor", "seq"),
        P(("dp", "tensor"), "seq"),
        P("dp"),
    )
    return jax.shard_map(
        on_device, mesh=mesh, in_specs=placed, out_specs=P(("dp", "tensor"), "seq"), check_vma=False
    )
```

time: 376 us -> 330 us (0.88); the launches traced: 371 us -> 330 us
  local copies, waits for them, and re-layouts: 38 us -> 14.5 us
  waiting for transfers between devices: 230 us -> 219 us
  other arithmetic: 28.4 us -> 22.3 us
  starting transfers between devices: 14.9 us -> 10.1 us
  matrix products: 45.8 us -> 49.9 us
    all_to_all x2 -> x1, waiting for transfers between devices: 54 us -> 29.6 us  [on_device(): lax.all_to_all(head_major, 'seq', split_axis=0, concat_axis=0, tiled=True)]
    reshape x3 -> x0, local copies, waits for them, and re-layouts: 13 us -> none  [the longest x2 6.92 us: on_device(): keys_values.reshape(tok_dev, 2, kv_ten, HD)[:, :, table, :]]
    unnamed x1 -> x0, other arithmetic: 11.6 us -> none
    slice x7 -> x14, local copies, waits for them, and re-layouts: 0.1 us -> 9.32 us  [the longest x9 6.33 us: attend(): query_head[first_row:key_end]]
    all_to_all x3 -> x0, local copies, waits for them, and re-layouts: 8.51 us -> none  [the longest x2 7.2 us: on_device(): lax.all_to_all(picked, 'seq', split_axis=2, concat_axis=0, tiled=True)]
    all_gather x0 -> x1, waiting for transfers between devices: none -> 8.22 us  [on_device(): pair_all = lax.all_gather(keys_values, 'seq', axis=0, tiled=True)]
    gather x3 -> x0, local copies, waits for them, and re-layouts: 7.72 us -> none  [the longest x2 6.04 us: on_device(): keys_values.reshape(tok_dev, 2, kv_ten, HD)[:, :, table, :]]
    all_gather x1, waiting for transfers between devices: 94.6 us -> 101 us  [on_device(): gathered = lax.all_gather(heads_out, 'seq', axis=1, tiled=True)]
  transfers between devices with their start and end apart: 4 -> 4, of which waited for: 4 -> 4; matrix products, arithmetic and copies ran while one was open for 6% -> 5% of each run, Pallas kernels for 0% -> 0%
where the time goes in v2:
time: 330 us
  waiting for transfers between devices  219 us (66%)
  matrix products  49.9 us (15%)
  other arithmetic  22.3 us (7%)
  local copies, waits for them, and re-layouts  14.5 us (4%)
  between operations  13.6 us (4%)
  starting transfers between devices  10.1 us (3%)
    all_gather x1, waiting for transfers between devices, on_device(): gathered = lax.all_gather(heads_out, 'seq', axis=1, tiled=True)  101 us
    reduce_scatter x1, waiting for transfers between devices, on_device(): lax.psum_scatter(jnp.dot(gathered, out_weight, preferred_element_type=jnp...  80.9 us
    all_to_all x1, waiting for transfers between devices, on_device(): lax.all_to_all(head_major, 'seq', split_axis=0, concat_axis=0, tiled=True)  29.6 us
    dot_general x8, matrix products, attend(): jnp.einsum('qk,kd->qd', weights, value_head[:key_end], preferred_element_...  22.2 us
    reduce_sum x8, other arithmetic, attend(): jnp.sum(exponents, axis=-1, keepdims=True)  15.3 us
    dot_general x1, matrix products, on_device(): jnp.dot(gathered, out_weight, preferred_element_type=jnp.float32)  14.4 us
    dot_general x8, matrix products, attend(): jnp.einsum('qd,kd->qk', query_head[first_row:key_end], key_head[:key_end]...  13.3 us
    all_to_all x1, starting transfers between devices, on_device(): lax.all_to_all(head_major, 'seq', split_axis=0, concat_axis=0, tiled=True)  9.97 us
  transfers between devices with their start and end apart: 4, of which 4 were waited for; matrix products, arithmetic and copies ran while one was open for 5% of the time, Pallas kernels for 0%

profile of v2, /device:TPU:1, one launch (start us, length us, event | category | flops | bytes accessed | tf_op | source)
XLA Modules:
  0.0 329.7 jit_solution(3992154205988510510)
XLA Ops:
  6.5 1.8 copy.7
  8.4 0.0 all-gather.3.cloned.1.call-update
  8.4 2.3 copy.8
  10.7 10.0 %all-to-all-start = ((bf16[16,256,128]{1,2,0:T(8,128)(2,1)}), bf16[16,256,128]{1,2,0:T(8,128)(2,1)S(1)}, u32[]{:S(2)}, u32[]{:S(2)}) async-start(bf16[16,256,128]{1,2,0:T(8,128)(2,1)} %bitcast.154), calls=%async_computation | async-start | bytes 2097152 | tf_op jit(solution)/shard_map/all_to_all | solution.py:53
  20.6 0.0 all-gather.5.cloned.1.call-start
  20.7 0.6 slice.203
  21.3 0.6 slice.219
  21.9 0.6 slice.211
  22.5 0.6 slice.235
  23.1 0.6 slice.227
  23.7 0.6 iota_add_fusion.5
  24.3 0.6 iota_add_fusion.4
  24.8 0.6 iota_add_fusion.3
  25.4 0.6 iota_add_fusion.2
  26.0 0.6 iota_add_fusion.1
  26.6 0.6 iota_add_fusion
  27.2 0.6 fusion.86
  27.8 29.6 %all-to-all-done = bf16[16,256,128]{1,2,0:T(8,128)(2,1)S(1)} async-done(((bf16[16,256,128]{1,2,0:T(8,128)(2,1)}), bf16[16,256,128]{1,2,0:T(8,128)(2,1)S(1)}, u32[]{:S(2)}, u32[]{:S(2)}) %all-to-all-start) | async-done | bytes 1048608 | tf_op jit(solution)/shard_map/all_to_all | solution.py:53
  57.4 0.8 fusion.85
  58.2 1.0 copy.16
  59.3 1.0 copy.15
  60.3 1.0 copy.14
  61.3 1.0 copy.13
  62.4 1.0 copy.12
  63.4 0.1 copy.11
  63.5 0.1 copy.10
  63.6 0.1 copy.9
  63.8 8.2 %all-gather.3.cloned.1.call-done = bf16[4096,2,256]{2,0,1:T(8,128)(2,1)} async-done(((bf16[256,2,256]{2,0,1:T(8,128)(2,1)}), bf16[4096,2,256]{2,0,1:T(8,128)(2,1)}) %all-gather.3.cloned.1.call-update) | async-done | bytes 4194320 | tf_op jit(solution)/shard_map/all_gather | solution.py:56
  72.0 1.4 fusion.87
  73.4 1.0 fusion.45
  74.4 1.6 fusion.23
  76.0 1.4 fusion.41
  77.5 0.9 fusion.88
  78.3 1.5 fusion.22
  79.9 1.1 fusion.10
  81.0 1.5 fusion.19
  82.4 0.0 copy-done.5
  82.4 0.0 copy-done.13
  82.5 0.0 copy-done.19
  82.5 1.3 fusion.89
  83.8 1.9 fusion.12
  85.7 1.5 fusion.4
  87.2 2.2 fusion.13
  89.5 1.8 fusion.90
  91.3 2.7 fusion.6
  94.0 3.8 %fusion.1 = (f32[512]{0:T(512)S(1)}, f32[4096,512]{1,0:T(8,128)S(1)}) fusion(s32[512]{0:T(512)S(1)} %copy-done.10, s32[512]{0:T(512)S(1)} %copy-done.16, s32[4096]{0:T(1024)S(1)} %copy-done.3, bf16[512,128]{1,0:T(8,128)(2,1)S(1)} %bitcast.158, bf16[4096,2,256]{2,0,1:T(8,128)(2,1)} %all-gather.3.cloned.1.call-done, s32[]{:T(128)S(6)} %select_n.65), kind=kOutput, calls=%fused_computation.5 | convolution fusion | flops 549453312 | bytes 9590788 | tf_op jit(solution)/shard_map/qd,kd->qk/dot_general | solution.py:22
  97.8 3.1 fusion.7
  101.0 1.4 fusion.28
  102.4 2.2 fusion.29
  104.6 2.4 fusion.39
  107.0 3.4 %fusion.38 = bf16[4096,128]{1,0:T(8,128)(2,1)S(1)} fusion(bf16[4096,128]{1,0:T(8,128)(2,1)S(1)} %fusion.39, f32[2048,512]{1,0:T(8,128)S(1)} %get-tuple-element.28, f32[512]{0:T(512)S(1)} %fusion.19, f32[512]{0:T(512)S(1)} %get-tuple-element.27, s32[512]{0:T(512)S(1)} %copy-done.14, s32[512]{0:T(512)S(1)} %copy-done.20, s32[2048]{0:T(1024)S(1)} %copy-done.6, ...), kind=kOutput, calls=%fused_computation.70 | convolution fusion | flops 277938176 | bytes 4866056 | tf_op jit(solution)/shard_map/qk,kd->qd/dot_general | solution.py:38
  110.4 2.2 fusion.37
  112.6 3.1 fusion.36
  115.7 3.5 %fusion.35 = bf16[4096,128]{1,0:T(8,128)(2,1)S(1)} fusion(bf16[4096,128]{1,0:T(8,128)(2,1)S(1)} %fusion.36, f32[512,3584]{0,1:T(8,128)S(1)} %get-tuple-element.34, f32[512]{0:T(512)S(1)} %fusion.6, f32[512]{0:T(512)S(1)} %get-tuple-element.33, s32[512]{0:T(512)S(1)} %copy-done.11, s32[512]{0:T(512)S(1)} %copy-done.17, s32[3584]{0:T(1024)S(1)} %bitcast.157, ...), kind=kOutput, calls=%fused_computation.67 | convolution fusion | flops 482672640 | bytes 8413192 | tf_op jit(solution)/shard_map/qk,kd->qd/dot_general | solution.py:38
  119.2 4.1 %fusion.40 = bf16[4096,128]{1,0:T(8,128)(2,1)S(1)} fusion(bf16[4096,128]{1,0:T(8,128)(2,1)S(1)} %fusion.35, f32[4096,512]{1,0:T(8,128)S(1)} %get-tuple-element.36, f32[512]{0:T(512)S(1)} %fusion.7, f32[512]{0:T(512)S(1)} %get-tuple-element.35, s32[512]{0:T(512)S(1)} %copy-done.10, s32[512]{0:T(512)S(1)} %copy-done.16, s32[4096]{0:T(1024)S(1)} %copy-done.3, ...), kind=kOutput, calls=%fused_computation.72 | convolution fusion | flops 555810816 | bytes 9592840 | tf_op jit(solution)/shard_map/qk,kd->qd/dot_general | solution.py:38
  123.3 0.0 copy-start.1
  123.3 1.0 copy-done.1
  124.2 0.0 all-gather.5.cloned.1.call-update
  124.3 0.0 reduce-scatter.2.cloned.1.call-start
  124.3 100.7 %all-gather.5.cloned.1.call-done = bf16[4096,2048]{1,0:T(8,128)(2,1)} async-done(((bf16[4096,128]{1,0:T(8,128)(2,1)}), bf16[4096,2048]{1,0:T(8,128)(2,1)}) %all-gather.5.cloned.1.call-update) | async-done | bytes 16777232 | tf_op jit(solution)/shard_map/all_gather | solution.py:59
  225.0 14.4 %fusion.91 = f32[4096,512]{1,0:T(8,128)} fusion(bf16[4096,2048]{1,0:T(8,128)(2,1)} %all-gather.5.cloned.1.call-done, bf16[2048,512]{1,0:T(8,128)(2,1)S(1)} %copy-done), kind=kOutput, calls=%fused_computation.149 | convolution fusion | flops 8589934592 | bytes 27262976 | tf_op jit(solution)/shard_map/dot_general | solution.py:61
  239.4 0.0 reduce-scatter.2.cloned.1.call-update
  239.4 80.9 %reduce-scatter.2.cloned.1.call-done = f32[1024,512]{1,0:T(8,128)} async-done(((f32[4096,512]{1,0:T(8,128)}), f32[1024,512]{1,0:T(8,128)}) %reduce-scatter.2.cloned.1.call-update) | async-done | bytes 2097168 | tf_op jit(solution)/shard_map/reduce_scatter | solution.py:60
  320.3 2.9 add_convert_fusion
  (48 shorter events, 0.1 us)
Async XLA Ops:
  6.5 218.4 %copy-start = (bf16[2048,512]{1,0:T(8,128)(2,1)S(1)}, bf16[2048,512]{1,0:T(8,128)(2,1)}, u32[]{:S(2)}) copy-start(bf16[2048,512]{1,0:T(8,128)(2,1)} %param.7) | copy-start | bytes 6291460
  6.5 14.1 %copy-start.3 = (s32[4096]{0:T(1024)S(1)}, s32[4096]{0:T(1024)}, u32[]{:S(2)}) copy-start(s32[4096]{0:T(1024)} %param.9) | copy-start | bytes 49156
  6.5 65.5 %all-gather.3.cloned.1.call-start = ((), (), s32[]{:S(2)}) async-start(), calls=%async_computation.2 | async-start | bytes 4456448 | tf_op jit(solution)/shard_map/all_gather | solution.py:56
  10.7 46.7 %all-to-all-start = ((bf16[16,256,128]{1,2,0:T(8,128)(2,1)}), bf16[16,256,128]{1,2,0:T(8,128)(2,1)S(1)}, u32[]{:S(2)}, u32[]{:S(2)}) async-start(bf16[16,256,128]{1,2,0:T(8,128)(2,1)} %bitcast.154), calls=%async_computation | async-start | bytes 2097152 | tf_op jit(solution)/shard_map/all_to_all | solution.py:53
  20.6 204.3 %all-gather.5.cloned.1.call-start = ((), (), s32[]{:S(2)}) async-start(), calls=%async_computation.3 | async-start | bytes 17825792 | tf_op jit(solution)/shard_map/all_gather | solution.py:59
  72.0 5.4 %copy-start.7 = (s32[1536]{0:T(1024)S(1)}, s32[1536]{0:T(1024)}, u32[]{:S(2)}) copy-start(s32[1536]{0:T(1024)} %slice.211) | copy-start | bytes 18436
  72.0 5.4 %copy-start.15 = (s32[512]{0:T(512)S(1)}, s32[512]{0:T(512)}, u32[]{:S(2)}) copy-start(s32[512]{0:T(512)} %get-tuple-element.18) | copy-start | bytes 6148
  72.0 5.4 %copy-start.21 = (s32[512]{0:T(512)S(1)}, s32[512]{0:T(512)}, u32[]{:S(2)}) copy-start(s32[512]{0:T(512)} %iota_add_fusion.5) | copy-start | bytes 6148
  72.0 5.5 %copy-start.24 = (bf16[4096,2,256]{2,0,1:T(8,128)(2,1)S(1)}, bf16[4096,2,256]{2,0,1:T(8,128)(2,1)}, u32[]{:S(2)}) copy-start(bf16[4096,2,256]{2,0,1:T(8,128)(2,1)} %all-gather.3.cloned.1.call-done) | copy-start | bytes 12582916
  77.5 2.4 copy-start.6
  77.5 2.4 copy-start.14
  77.5 2.4 copy-start.20
  79.9 2.6 copy-start.5
  79.9 2.6 copy-start.13
  79.9 2.6 copy-start.19
  83.8 1.9 copy-start.4
  83.8 1.9 copy-start.12
  83.8 1.9 copy-start.18
  87.2 2.2 copy-start.11
  87.2 2.2 copy-start.17
  91.2 2.7 copy-start.10
  91.3 2.7 copy-start.16
  97.8 3.2 copy-start.8
  100.9 1.5 copy-start.9
  100.9 1.5 copy-start.22
  101.0 1.5 copy-start.23
  107.0 3.4 %copy-start.25 = (bf16[4096,2,256]{2,0,1:T(8,128)(2,1)S(1)}, bf16[4096,2,256]{2,0,1:T(8,128)(2,1)}, u32[]{:S(2)}) copy-start(bf16[4096,2,256]{2,0,1:T(8,128)(2,1)} %all-gather.3.cloned.1.call-done) | copy-start | bytes 12582916
  123.3 1.0 copy-start.1
  124.3 196.0 %reduce-scatter.2.cloned.1.call-start = ((), (), s32[]{:S(2)}) async-start(), calls=%async_computation.4 | async-start | bytes 10485760 | tf_op jit(solution)/shard_map/reduce_scatter | solution.py:60
  239.4 80.9 %copy-start.2 = (bf16[1024,512]{1,0:T(8,128)(2,1)S(1)}, bf16[1024,512]{1,0:T(8,128)(2,1)}, u32[]{:S(2)}) copy-start(bf16[1024,512]{1,0:T(8,128)(2,1)} %param.8) | copy-start | bytes 3145732
Sparse Core Ops, SparseCore 0:
  9.2 62.7 all-gather.2
  124.4 100.5 all-gather.4
  239.5 80.7 reduce-scatter.1

commit v3 on v2

--- a/solution.py
+++ b/solution.py
@@ -58,7 +58,7 @@
     heads_out = attend(query_head, pair_head[:, 0, :], pair_head[:, 1, :], segments)
     gathered = lax.all_gather(heads_out, "seq", axis=1, tiled=True)
     summed = lax.psum_scatter(
-        jnp.dot(gathered, out_weight, preferred_element_type=jnp.float32),
+        jnp.dot(gathered, out_weight, preferred_element_type=jnp.float32).astype(jnp.bfloat16),
         "tensor",
         scatter_dimension=0,
         tiled=True,

time: 330 us -> 295 us (0.89)
  waiting for transfers between devices: 219 us -> 186 us
    reduce_scatter x1, waiting for transfers between devices: 80.9 us -> 47.2 us  [on_device(): lax.psum_scatter(jnp.dot(gathered, out_weight, preferred_element_type=jnp...]
where the time goes in v3:
time: 295 us
  waiting for transfers between devices  186 us (63%)
  matrix products  49.2 us (17%)
  other arithmetic  21.9 us (7%)
  local copies, waits for them, and re-layouts  14.5 us (5%)
  between operations  13.6 us (5%)
  starting transfers between devices  10.1 us (3%)
    all_gather x1, waiting for transfers between devices, on_device(): gathered = lax.all_gather(heads_out, 'seq', axis=1, tiled=True)  101 us
    reduce_scatter x1, waiting for transfers between devices, on_device(): lax.psum_scatter(jnp.dot(gathered, out_weight, preferred_element_type=jnp...  47.2 us
    all_to_all x1, waiting for transfers between devices, on_device(): lax.all_to_all(head_major, 'seq', split_axis=0, concat_axis=0, tiled=True)  29.6 us
    dot_general x8, matrix products, attend(): jnp.einsum('qk,kd->qd', weights, value_head[:key_end], preferred_element_...  22.2 us
    reduce_sum x8, other arithmetic, attend(): jnp.sum(exponents, axis=-1, keepdims=True)  15.3 us
    dot_general x1, matrix products, on_device(): jnp.dot(gathered, out_weight, preferred_element_type=jnp.float32)  13.7 us
    dot_general x8, matrix products, attend(): jnp.einsum('qd,kd->qk', query_head[first_row:key_end], key_head[:key_end]...  13.3 us
    all_to_all x1, starting transfers between devices, on_device(): lax.all_to_all(head_major, 'seq', split_axis=0, concat_axis=0, tiled=True)  9.97 us
  transfers between devices with their start and end apart: 4, of which 4 were waited for; matrix products, arithmetic and copies ran while one was open for 5% of the time, Pallas kernels for 0%

profile of v3, /device:TPU:1, one launch (start us, length us, event | category | flops | bytes accessed | tf_op | source)
XLA Modules:
  0.0 294.9 jit_solution(4038347070746041483)
XLA Ops:
  6.5 0.0 copy-start
  6.5 1.8 copy.7
  8.4 0.0 all-gather.3.cloned.1.call-update
  8.4 2.3 copy.8
  10.7 10.0 %all-to-all-start = ((bf16[16,256,128]{1,2,0:T(8,128)(2,1)}), bf16[16,256,128]{1,2,0:T(8,128)(2,1)S(1)}, u32[]{:S(2)}, u32[]{:S(2)}) async-start(bf16[16,256,128]{1,2,0:T(8,128)(2,1)} %bitcast.154), calls=%async_computation | async-start | bytes 2097152 | tf_op jit(solution)/shard_map/all_to_all | solution.py:53
  20.6 0.0 all-gather.5.cloned.1.call-start
  20.7 0.6 slice.203
  21.3 0.6 slice.219
  21.9 0.6 slice.211
  22.5 0.6 slice.235
  23.1 0.6 slice.227
  23.7 0.6 iota_add_fusion.5
  24.3 0.6 iota_add_fusion.4
  24.8 0.6 iota_add_fusion.3
  25.4 0.6 iota_add_fusion.2
  26.0 0.6 iota_add_fusion.1
  26.6 0.6 iota_add_fusion
  27.2 0.6 fusion.86
  27.8 29.6 %all-to-all-done = bf16[16,256,128]{1,2,0:T(8,128)(2,1)S(1)} async-done(((bf16[16,256,128]{1,2,0:T(8,128)(2,1)}), bf16[16,256,128]{1,2,0:T(8,128)(2,1)S(1)}, u32[]{:S(2)}, u32[]{:S(2)}) %all-to-all-start) | async-done | bytes 1048608 | tf_op jit(solution)/shard_map/all_to_all | solution.py:53
  57.4 0.8 fusion.85
  58.2 1.0 copy.16
  59.3 1.0 copy.15
  60.3 1.0 copy.14
  61.3 1.0 copy.13
  62.4 1.0 copy.12
  63.4 0.1 copy.11
  63.5 0.1 copy.10
  63.6 0.1 copy.9
  63.8 8.2 %all-gather.3.cloned.1.call-done = bf16[4096,2,256]{2,0,1:T(8,128)(2,1)} async-done(((bf16[256,2,256]{2,0,1:T(8,128)(2,1)}), bf16[4096,2,256]{2,0,1:T(8,128)(2,1)}) %all-gather.3.cloned.1.call-update) | async-done | bytes 4194320 | tf_op jit(solution)/shard_map/all_gather | solution.py:56
  72.0 1.4 fusion.87
  73.4 1.0 fusion.45
  74.4 1.6 fusion.23
  76.0 1.4 fusion.41
  77.4 0.0 copy-done.7
  77.4 0.0 copy-done.15
  77.5 0.9 fusion.88
  78.3 1.5 fusion.22
  79.9 1.1 fusion.10
  81.0 1.5 fusion.19
  82.5 1.3 fusion.89
  83.8 1.9 fusion.12
  85.7 1.5 fusion.4
  87.2 2.2 fusion.13
  89.5 1.8 fusion.90
  91.3 2.7 fusion.6
  94.0 3.8 %fusion.1 = (f32[512]{0:T(512)S(1)}, f32[4096,512]{1,0:T(8,128)S(1)}) fusion(s32[512]{0:T(512)S(1)} %copy-done.10, s32[512]{0:T(512)S(1)} %copy-done.16, s32[4096]{0:T(1024)S(1)} %copy-done.3, bf16[512,128]{1,0:T(8,128)(2,1)S(1)} %bitcast.158, bf16[4096,2,256]{2,0,1:T(8,128)(2,1)} %all-gather.3.cloned.1.call-done, s32[]{:T(128)S(6)} %select_n.65), kind=kOutput, calls=%fused_computation.5 | convolution fusion | flops 549453312 | bytes 9590788 | tf_op jit(solution)/shard_map/qd,kd->qk/dot_general | solution.py:22
  97.8 3.1 %fusion.7 = f32[512]{0:T(512)S(1)} fusion(f32[4096,512]{1,0:T(8,128)S(1)} %get-tuple-element.36, f32[512]{0:T(512)S(1)} %get-tuple-element.35, s32[512]{0:T(512)S(1)} %copy-done.10, s32[512]{0:T(512)S(1)} %copy-done.16, s32[4096]{0:T(1024)S(1)} %copy-done.3), kind=kLoop, calls=%fused_computation.24 | loop fusion | flops 16776704 | bytes 8413184 | tf_op jit(solution)/shard_map/reduce_sum | solution.py:37
  101.0 1.4 fusion.28
  102.4 2.2 fusion.29
  104.6 2.4 fusion.39
  107.0 3.4 %fusion.38 = bf16[4096,128]{1,0:T(8,128)(2,1)S(1)} fusion(bf16[4096,128]{1,0:T(8,128)(2,1)S(1)} %fusion.39, f32[2048,512]{1,0:T(8,128)S(1)} %get-tuple-element.28, f32[512]{0:T(512)S(1)} %fusion.19, f32[512]{0:T(512)S(1)} %get-tuple-element.27, s32[512]{0:T(512)S(1)} %copy-done.14, s32[512]{0:T(512)S(1)} %copy-done.20, s32[2048]{0:T(1024)S(1)} %copy-done.6, ...), kind=kOutput, calls=%fused_computation.71 | convolution fusion | flops 277938176 | bytes 4866056 | tf_op jit(solution)/shard_map/qk,kd->qd/dot_general | solution.py:38
  110.4 2.2 fusion.37
  112.6 3.1 %fusion.36 = bf16[4096,128]{1,0:T(8,128)(2,1)S(1)} fusion(bf16[4096,128]{1,0:T(8,128)(2,1)S(1)} %fusion.37, f32[3072,512]{1,0:T(8,128)S(1)} %get-tuple-element.32, f32[512]{0:T(512)S(1)} %fusion.13, f32[512]{0:T(512)S(1)} %get-tuple-element.31, s32[512]{0:T(512)S(1)} %copy-done.12, s32[512]{0:T(512)S(1)} %copy-done.18, s32[3072]{0:T(1024)S(1)} %copy-done.4, ...), kind=kOutput, calls=%fused_computation.69 | convolution fusion | flops 416874496 | bytes 7229448 | tf_op jit(solution)/shard_map/qk,kd->qd/dot_general | solution.py:38
  115.7 3.5 %fusion.35 = bf16[4096,128]{1,0:T(8,128)(2,1)S(1)} fusion(bf16[4096,128]{1,0:T(8,128)(2,1)S(1)} %fusion.36, f32[512,3584]{0,1:T(8,128)S(1)} %get-tuple-element.34, f32[512]{0:T(512)S(1)} %fusion.6, f32[512]{0:T(512)S(1)} %get-tuple-element.33, s32[512]{0:T(512)S(1)} %copy-done.11, s32[512]{0:T(512)S(1)} %copy-done.17, s32[3584]{0:T(1024)S(1)} %bitcast.157, ...), kind=kOutput, calls=%fused_computation.68 | convolution fusion | flops 482672640 | bytes 8413192 | tf_op jit(solution)/shard_map/qk,kd->qd/dot_general | solution.py:38
  119.2 4.1 %fusion.40 = bf16[4096,128]{1,0:T(8,128)(2,1)S(1)} fusion(bf16[4096,128]{1,0:T(8,128)(2,1)S(1)} %fusion.35, f32[4096,512]{1,0:T(8,128)S(1)} %get-tuple-element.36, f32[512]{0:T(512)S(1)} %fusion.7, f32[512]{0:T(512)S(1)} %get-tuple-element.35, s32[512]{0:T(512)S(1)} %copy-done.10, s32[512]{0:T(512)S(1)} %copy-done.16, s32[4096]{0:T(1024)S(1)} %copy-done.3, ...), kind=kOutput, calls=%fused_computation.73 | convolution fusion | flops 555810816 | bytes 9592840 | tf_op jit(solution)/shard_map/qk,kd->qd/dot_general | solution.py:38
  123.3 0.0 copy-start.2
  123.3 1.0 copy-done.2
  124.2 0.0 all-gather.5.cloned.1.call-update
  124.3 0.0 reduce-scatter.2.cloned.1.call-start
  124.3 100.7 %all-gather.5.cloned.1.call-done = bf16[4096,2048]{1,0:T(8,128)(2,1)} async-done(((bf16[4096,128]{1,0:T(8,128)(2,1)}), bf16[4096,2048]{1,0:T(8,128)(2,1)}) %all-gather.5.cloned.1.call-update) | async-done | bytes 16777232 | tf_op jit(solution)/shard_map/all_gather | solution.py:59
  225.0 13.7 %convolution_convert_fusion = bf16[4096,512]{1,0:T(8,128)(2,1)} fusion(bf16[4096,2048]{1,0:T(8,128)(2,1)} %all-gather.5.cloned.1.call-done, bf16[2048,512]{1,0:T(8,128)(2,1)S(1)} %copy-done), kind=kOutput, calls=%fused_computation.16 | convolution fusion | flops 8592031744 | bytes 23068672 | tf_op jit(solution)/shard_map/dot_general | solution.py:61
  238.7 0.0 reduce-scatter.2.cloned.1.call-update
  238.7 47.2 %reduce-scatter.2.cloned.1.call-done = bf16[1024,512]{1,0:T(8,128)(2,1)} async-done(((bf16[4096,512]{1,0:T(8,128)(2,1)}), bf16[1024,512]{1,0:T(8,128)(2,1)}) %reduce-scatter.2.cloned.1.call-update) | async-done | bytes 1048592 | tf_op jit(solution)/shard_map/reduce_scatter | solution.py:60
  285.9 2.5 add_convert_fusion
  (48 shorter events, 0.1 us)
Async XLA Ops:
  6.5 218.4 %copy-start = (bf16[2048,512]{1,0:T(8,128)(2,1)S(1)}, bf16[2048,512]{1,0:T(8,128)(2,1)}, u32[]{:S(2)}) copy-start(bf16[2048,512]{1,0:T(8,128)(2,1)} %param.7) | copy-start | bytes 6291460
  6.5 14.1 %copy-start.3 = (s32[4096]{0:T(1024)S(1)}, s32[4096]{0:T(1024)}, u32[]{:S(2)}) copy-start(s32[4096]{0:T(1024)} %param.9) | copy-start | bytes 49156
  6.5 65.5 %all-gather.3.cloned.1.call-start = ((), (), s32[]{:S(2)}) async-start(), calls=%async_computation.2 | async-start | bytes 4456448 | tf_op jit(solution)/shard_map/all_gather | solution.py:56
  10.7 46.7 %all-to-all-start = ((bf16[16,256,128]{1,2,0:T(8,128)(2,1)}), bf16[16,256,128]{1,2,0:T(8,128)(2,1)S(1)}, u32[]{:S(2)}, u32[]{:S(2)}) async-start(bf16[16,256,128]{1,2,0:T(8,128)(2,1)} %bitcast.154), calls=%async_computation | async-start | bytes 2097152 | tf_op jit(solution)/shard_map/all_to_all | solution.py:53
  20.6 204.3 %all-gather.5.cloned.1.call-start = ((), (), s32[]{:S(2)}) async-start(), calls=%async_computation.3 | async-start | bytes 17825792 | tf_op jit(solution)/shard_map/all_gather | solution.py:59
  72.0 5.4 %copy-start.7 = (s32[1536]{0:T(1024)S(1)}, s32[1536]{0:T(1024)}, u32[]{:S(2)}) copy-start(s32[1536]{0:T(1024)} %slice.211) | copy-start | bytes 18436
  72.0 5.4 %copy-start.15 = (s32[512]{0:T(512)S(1)}, s32[512]{0:T(512)}, u32[]{:S(2)}) copy-start(s32[512]{0:T(512)} %get-tuple-element.18) | copy-start | bytes 6148
  72.0 5.4 %copy-start.21 = (s32[512]{0:T(512)S(1)}, s32[512]{0:T(512)}, u32[]{:S(2)}) copy-start(s32[512]{0:T(512)} %iota_add_fusion.5) | copy-start | bytes 6148
  72.0 5.5 %copy-start.24 = (bf16[4096,2,256]{2,0,1:T(8,128)(2,1)S(1)}, bf16[4096,2,256]{2,0,1:T(8,128)(2,1)}, u32[]{:S(2)}) copy-start(bf16[4096,2,256]{2,0,1:T(8,128)(2,1)} %all-gather.3.cloned.1.call-done) | copy-start | bytes 12582916
  77.5 2.4 copy-start.6
  77.5 2.4 copy-start.14
  77.5 2.4 copy-start.20
  79.9 2.6 copy-start.5
  79.9 2.6 copy-start.13
  79.9 2.6 copy-start.19
  83.8 1.9 copy-start.4
  83.8 1.9 copy-start.12
  83.8 1.9 copy-start.18
  87.2 2.2 copy-start.11
  87.2 2.2 copy-start.17
  91.2 2.7 copy-start.10
  91.3 2.7 copy-start.16
  97.8 3.2 %copy-start.8 = (s32[512]{0:T(512)S(1)}, s32[512]{0:T(512)}, u32[]{:S(2)}) copy-start(s32[512]{0:T(512)} %get-tuple-element.20) | copy-start | bytes 6148
  100.9 1.5 copy-start.9
  100.9 1.5 copy-start.22
  101.0 1.5 copy-start.23
  107.0 3.4 %copy-start.25 = (bf16[4096,2,256]{2,0,1:T(8,128)(2,1)S(1)}, bf16[4096,2,256]{2,0,1:T(8,128)(2,1)}, u32[]{:S(2)}) copy-start(bf16[4096,2,256]{2,0,1:T(8,128)(2,1)} %all-gather.3.cloned.1.call-done) | copy-start | bytes 12582916
  123.3 1.0 copy-start.2
  124.3 161.7 %reduce-scatter.2.cloned.1.call-start = ((), (), s32[]{:S(2)}) async-start(), calls=%async_computation.4 | async-start | bytes 5242880 | tf_op jit(solution)/shard_map/reduce_scatter | solution.py:60
  238.7 47.2 %copy-start.1 = (bf16[1024,512]{1,0:T(8,128)(2,1)S(1)}, bf16[1024,512]{1,0:T(8,128)(2,1)}, u32[]{:S(2)}) copy-start(bf16[1024,512]{1,0:T(8,128)(2,1)} %param.8) | copy-start | bytes 3145732
Sparse Core Ops, SparseCore 0:
  9.2 62.7 all-gather.2
  124.4 100.5 all-gather.4
  238.9 47.0 reduce-scatter.1

commit v4 on v3

v4 whole, which is shorter than its diff:
```python
import functools
import jax
import jax.numpy as jnp
import numpy as np
from jax import lax
from jax.experimental import pallas as pl
from jax.experimental.pallas import tpu as pltpu
from jax.sharding import PartitionSpec as P

H = 64
KVH = 8
HD = 128
L = 4096


def flash_kernel(starts_ref, q_ref, k_ref, v_ref, segq_ref, segk_ref, o_ref, *, bq, bk):
    qi = pl.program_id(0)
    q = q_ref[...]
    seg_q = segq_ref[...]
    row_pos = qi * bq + lax.broadcasted_iota(jnp.int32, (bq, bk), 0)

    def body(kb, carry):
        m_prev, l_prev, acc_prev = carry
        start = pl.multiple_of(kb * bk, bk)
        k_blk = k_ref[pl.ds(start, bk), :]
        v_blk = v_ref[pl.ds(start, bk), :]
        seg_k = segk_ref[:, pl.ds(start, bk)]
        scores = lax.dot_general(
            q, k_blk, (((1,), (1,)), ((), ())), preferred_element_type=jnp.float32
        ) * (HD ** -0.5)
        col_pos = start + lax.broadcasted_iota(jnp.int32, (bq, bk), 1)
        allowed = (col_pos <= row_pos) & (seg_q == seg_k)
        masked = jnp.where(allowed, scores, -1e30)
        m_new = jnp.maximum(m_prev, jnp.max(masked, axis=1, keepdims=True))
        alpha = jnp.exp(m_prev - m_new)
        probs = jnp.where(allowed, jnp.exp(masked - m_new), 0.0)
        l_new = alpha * l_prev + jnp.sum(probs, axis=1, keepdims=True)
        acc_new = alpha * acc_prev + jnp.dot(
            probs.astype(jnp.bfloat16), v_blk, preferred_element_type=jnp.float32
        )
        return m_new, l_new, acc_new

    init = (
        jnp.full((bq, 1), -1e30, jnp.float32),
        jnp.zeros((bq, 1), jnp.float32),
        jnp.zeros((bq, HD), jnp.float32),
    )
    last = (qi * bq + bq - 1) // bk
    _, l_fin, acc_fin = lax.fori_loop(starts_ref[qi], last + 1, body, init)
    o_ref[...] = (acc_fin / l_fin).astype(o_ref.dtype)


def flash(query_head, key_head, value_head, segments, bq=512, bk=512):
    rows = query_head.shape[0]
    n_q = rows // bq
    first_docs = segments[::bq]
    starts = (jnp.searchsorted(segments, first_docs, side="left") // bk).astype(jnp.int32)
    seg_col = segments.reshape(rows, 1)
    seg_row = segments.reshape(1, rows)
    kernel = functools.partial(flash_kernel, bq=bq, bk=bk)
    return pl.pallas_call(
        kernel,
        out_shape=jax.ShapeDtypeStruct((rows, HD), jnp.bfloat16),
        grid_spec=pltpu.PrefetchScalarGridSpec(
            num_scalar_prefetch=1,
            grid=(n_q,),
            in_specs=[
                pl.BlockSpec((bq, HD), lambda i, s: (i, 0)),
                pl.BlockSpec((rows, HD), lambda i, s: (0, 0)),
                pl.BlockSpec((rows, HD), lambda i, s: (0, 0)),
                pl.BlockSpec((bq, 1), lambda i, s: (i, 0)),
                pl.BlockSpec((1, rows), lambda i, s: (0, 0)),
            ],
            out_specs=pl.BlockSpec((bq, HD), lambda i, s: (i, 0)),
        ),
        compiler_params=pltpu.CompilerParams(dimension_semantics=("arbitrary",)),
    )(starts, query_head, key_head, value_head, seg_col, seg_row)


def on_device(queries, keys_values, out_weight, residual, segments):
    n_seq = lax.axis_size("seq")
    seq_idx = lax.axis_index("seq")
    tok_dev = queries.shape[0]
    heads_ten = queries.shape[1] // HD
    assert heads_ten == n_seq
    group_size = H // KVH
    head_major = jnp.transpose(queries.reshape(tok_dev, heads_ten, HD), (1, 0, 2))
    query_parts = lax.all_to_all(head_major, "seq", split_axis=0, concat_axis=0, tiled=True)
    query_head = query_parts.reshape(n_seq * tok_dev, HD)
    assert query_head.shape[0] == L
    pair_all = lax.all_gather(keys_values, "seq", axis=0, tiled=True)
    pair_head = lax.dynamic_slice_in_dim(pair_all, (seq_idx // group_size) * HD, HD, axis=2)
    heads_out = flash(query_head, pair_head[:, 0, :], pair_head[:, 1, :], segments)
    gathered = lax.all_gather(heads_out, "seq", axis=1, tiled=True)
    summed = lax.psum_scatter(
        jnp.dot(gathered, out_weight, preferred_element_type=jnp.float32).astype(jnp.bfloat16),
        "tensor",
        scatter_dimension=0,
        tiled=True,
    )
    return (residual.astype(jnp.float32) + summed).astype(jnp.bfloat16)


def solution(mesh):
    placed = (
        P(("dp", "seq"), "tensor"),
        P(("dp", "seq"), None, "tensor"),
        P("tensor", "seq"),
        P(("dp", "tensor"), "seq"),
        P("dp"),
    )
    return jax.shard_map(
        on_device, mesh=mesh, in_specs=placed, out_specs=P(("dp", "tensor"), "seq"), check_vma=False
    )
```

time: 295 us -> 275 us (0.932)
  matrix products: 49.2 us -> 13.8 us
  Pallas kernels: 0 us -> 22.5 us
  other arithmetic: 21.9 us -> 3.37 us
  waiting for transfers between devices: 186 us -> 191 us
  local copies, waits for them, and re-layouts: 14.5 us -> 18.7 us
    dot_general x16 -> x0, matrix products: 35.5 us -> none  [the longest x8 22.2 us: attend(): jnp.einsum('qk,kd->qd', weights, value_head[:key_end], preferred_element_...]
    all_gather x1, waiting for transfers between devices: 8.22 us -> 39.5 us  [on_device(): pair_all = lax.all_gather(keys_values, 'seq', axis=0, tiled=True)]
    all_to_all x1, waiting for transfers between devices: 29.6 us -> 0.01 us  [on_device(): lax.all_to_all(head_major, 'seq', split_axis=0, concat_axis=0, tiled=True)]
    pallas_call x0 -> x1, Pallas kernels: none -> 22.5 us  [flash(): pl.pallas_call(kernel, out_shape=jax.ShapeDtypeStruct((rows, HD), jnp.bfl...]
    reduce_sum x8 -> x0, other arithmetic: 15.3 us -> none  [attend(): jnp.sum(exponents, axis=-1, keepdims=True)]
    slice x14 -> x1, local copies, waits for them, and re-layouts: 9.32 us -> 0.09 us  [flash(): first_docs = segments[::bq]]
    gather x0 -> x13, local copies, waits for them, and re-layouts: none -> 8.27 us  [flash(): jnp.searchsorted(segments, first_docs, side='left') // bk]
    all_gather x1, waiting for transfers between devices: 101 us -> 105 us  [on_device(): gathered = lax.all_gather(heads_out, 'seq', axis=1, tiled=True)]
  transfers between devices with their start and end apart: 4 -> 4, of which waited for: 4 -> 3; matrix products, arithmetic and copies ran while one was open for 5% -> 6% of each run, Pallas kernels for 0% -> 0%
where the time goes in v4:
time: 275 us; the launch traced here: 273 us
  waiting for transfers between devices  191 us (69%)
  Pallas kernels  22.5 us (8%)
  local copies, waits for them, and re-layouts  18.7 us (7%)
  matrix products  13.8 us (5%)
  between operations  13.2 us (5%)
  starting transfers between devices  10.1 us (4%)
  other arithmetic  3.37 us (1%)
    all_gather x1, waiting for transfers between devices, on_device(): gathered = lax.all_gather(heads_out, 'seq', axis=1, tiled=True)  105 us
    reduce_scatter x1, waiting for transfers between devices, on_device(): lax.psum_scatter(jnp.dot(gathered, out_weight, preferred_element_type=jnp...  47.2 us
    all_gather x1, waiting for transfers between devices, on_device(): pair_all = lax.all_gather(keys_values, 'seq', axis=0, tiled=True)  39.5 us
    pallas_call x1, Pallas kernels, flash(): pl.pallas_call(kernel, out_shape=jax.ShapeDtypeStruct((rows, HD), jnp.bfl...  22.5 us
    dot_general x1, matrix products, on_device(): jnp.dot(gathered, out_weight, preferred_element_type=jnp.float32)  13.8 us
    all_to_all x1, starting transfers between devices, on_device(): lax.all_to_all(head_major, 'seq', split_axis=0, concat_axis=0, tiled=True)  9.97 us
    gather x13, local copies, waits for them, and re-layouts, flash(): jnp.searchsorted(segments, first_docs, side='left') // bk  8.27 us
  transfers between devices with their start and end apart: 4, of which 3 were waited for; matrix products, arithmetic and copies ran while one was open for 6% of the time, Pallas kernels for 0%

profile of v4, /device:TPU:1, one launch (start us, length us, event | category | flops | bytes accessed | tf_op | source)
XLA Modules:
  0.0 273.3 jit_solution(854307086787822246)
XLA Ops:
  6.5 0.0 copy-start
  6.5 0.0 copy-start.1
  6.5 0.0 all-gather.3.cloned.1.call-start
  6.5 1.8 copy.9
  8.4 0.0 all-gather.3.cloned.1.call-update
  8.4 2.5 bitcast_bitcast_fusion
  10.9 10.0 %all-to-all-start = ((bf16[16,256,128]{2,1,0:T(8,128)(2,1)}), bf16[16,256,128]{2,1,0:T(8,128)(2,1)S(1)}, u32[]{:S(2)}, u32[]{:S(2)}) async-start(bf16[16,256,128]{2,1,0:T(8,128)(2,1)} %bitcast_bitcast_fusion), calls=%async_computation | async-start | bytes 2097152 | tf_op jit(solution)/shard_map/all_to_all | solution.py:88
  20.8 0.0 all-gather.5.cloned.1.call-start
  20.9 0.0 copy-done.1
  20.9 0.1 slice.9
  21.0 9.0 %while.24 = (s32[]{:T(128)}, u32[8]{0:T(128)S(1)}, u32[8]{0:T(128)S(1)}, s32[4096]{0:T(1024)S(1)}, s32[8]{0:T(128)S(1)}, /*index=5*/s32[]{:T(128)}, s32[]{:T(128)}, s32[]{}) while((s32[]{:T(128)}, u32[8]{0:T(128)S(1)}, u32[8]{0:T(128)S(1)}, s32[4096]{0:T(1024)S(1)}, s32[8]{0:T(128)S(1)}, /*index=5*/s32[]{:T(128)}, s32[]{:T(128)}, ...), condition=%wide.region_1.2_spmd.clone, body=%wide.region_0.1_spmd.clone.sunk | while | flops 1132 | bytes 4620 | solution.py:57
  21.0 0.6 gather_fusion
  21.7 0.6 gather_fusion
  22.4 0.6 gather_fusion
  23.1 0.6 gather_fusion
  23.8 0.6 gather_fusion
  24.5 0.6 gather_fusion
  25.2 0.6 gather_fusion
  25.9 0.6 gather_fusion
  26.6 0.6 gather_fusion
  27.3 0.6 gather_fusion
  28.0 0.6 gather_fusion
  28.7 0.6 gather_fusion
  29.4 0.6 gather_fusion
  30.0 2.0 copy.10.segq_ref
  32.0 0.5 and_select_fusion.starts_ref
  32.6 39.5 %all-gather.3.cloned.1.call-done = bf16[4096,2,256]{2,0,1:T(8,128)(2,1)} async-done(((bf16[256,2,256]{2,0,1:T(8,128)(2,1)}), bf16[4096,2,256]{2,0,1:T(8,128)(2,1)}) %all-gather.3.cloned.1.call-update) | async-done | bytes 4194320 | tf_op jit(solution)/shard_map/all_gather | solution.py:91
  72.1 3.0 %dynamic-slice_bitcast_fusion = (bf16[4096,128]{1,0:T(8,128)(2,1)}, bf16[4096,128]{1,0:T(8,128)(2,1)}) fusion(bf16[4096,2,256]{2,0,1:T(8,128)(2,1)} %all-gather.3.cloned.1.call-done, s32[]{:T(128)S(6)} %add.26, s32[]{:T(128)S(6)} %select_n.27), kind=kLoop, calls=%fused_computation.10 | loop fusion | bytes 4194312 | tf_op jit(solution)/shard_map/squeeze | solution.py:93
  75.1 0.0 all-to-all-done
  75.1 0.0 copy-start.2
  75.1 1.0 copy-done.2
  76.1 22.5 %shard_map.55 = bf16[4096,128]{1,0:T(8,128)(2,1)} custom-call(s32[8]{0:T(128)} %and_select_fusion.starts_ref, bf16[4096,128]{1,0:T(8,128)(2,1)} %bitcast.18, bf16[4096,128]{1,0:T(8,128)(2,1)} %get-tuple-element.102.k_ref, bf16[4096,128]{1,0:T(8,128)(2,1)} %get-tuple-element.101.v_ref, s32[4096,1]{1,0:T(8,128)} %copy.10.segq_ref, s32[1,4096]{1,0:T(1,128)S(1)} %bitcast.17), custom_call_target="tpu_custom_call" | custom-call | tf_op jit(solution)/shard_map/pallas_call | solution.py:61
  98.6 0.0 all-gather.5.cloned.1.call-update
  98.6 0.0 reduce-scatter.2.cloned.1.call-start
  98.6 104.7 %all-gather.5.cloned.1.call-done = bf16[4096,2048]{1,0:T(8,128)(2,1)} async-done(((bf16[4096,128]{1,0:T(8,128)(2,1)}), bf16[4096,2048]{1,0:T(8,128)(2,1)}) %all-gather.5.cloned.1.call-update) | async-done | bytes 16777232 | tf_op jit(solution)/shard_map/all_gather | solution.py:94
  203.3 0.0 copy-done
  203.3 13.8 %convolution_convert_fusion = bf16[4096,512]{1,0:T(8,128)(2,1)} fusion(bf16[4096,2048]{1,0:T(8,128)(2,1)} %all-gather.5.cloned.1.call-done, bf16[2048,512]{1,0:T(8,128)(2,1)S(1)} %copy-done), kind=kOutput, calls=%fused_computation.7 | convolution fusion | flops 8592031744 | bytes 23068672 | tf_op jit(solution)/shard_map/dot_general | solution.py:96
  217.1 0.0 copy-start.3
  217.1 0.0 reduce-scatter.2.cloned.1.call-update
  217.1 47.2 %reduce-scatter.2.cloned.1.call-done = bf16[1024,512]{1,0:T(8,128)(2,1)} async-done(((bf16[4096,512]{1,0:T(8,128)(2,1)}), bf16[1024,512]{1,0:T(8,128)(2,1)}) %reduce-scatter.2.cloned.1.call-update) | async-done | bytes 1048592 | tf_op jit(solution)/shard_map/reduce_scatter | solution.py:95
  264.3 0.0 copy-done.3
  264.3 2.5 add_convert_fusion
  (41 shorter events, 0.4 us)
Async XLA Ops:
  6.5 196.8 %copy-start = (bf16[2048,512]{1,0:T(8,128)(2,1)S(1)}, bf16[2048,512]{1,0:T(8,128)(2,1)}, u32[]{:S(2)}) copy-start(bf16[2048,512]{1,0:T(8,128)(2,1)} %param.9) | copy-start | bytes 6291460
  6.5 14.4 %copy-start.1 = (s32[4096]{0:T(1024)S(1)}, s32[4096]{0:T(1024)}, u32[]{:S(2)}) copy-start(s32[4096]{0:T(1024)} %param.11) | copy-start | bytes 49156
  6.5 65.5 %all-gather.3.cloned.1.call-start = ((), (), s32[]{:S(2)}) async-start(), calls=%async_computation.2 | async-start | bytes 4456448 | tf_op jit(solution)/shard_map/all_gather | solution.py:91
  10.9 64.2 %all-to-all-start = ((bf16[16,256,128]{2,1,0:T(8,128)(2,1)}), bf16[16,256,128]{2,1,0:T(8,128)(2,1)S(1)}, u32[]{:S(2)}, u32[]{:S(2)}) async-start(bf16[16,256,128]{2,1,0:T(8,128)(2,1)} %bitcast_bitcast_fusion), calls=%async_computation | async-start | bytes 2097152 | tf_op jit(solution)/shard_map/all_to_all | solution.py:88
  20.8 182.5 %all-gather.5.cloned.1.call-start = ((), (), s32[]{:S(2)}) async-start(), calls=%async_computation.3 | async-start | bytes 17825792 | tf_op jit(solution)/shard_map/all_gather | solution.py:94
  75.1 1.0 copy-start.2
  98.6 165.7 %reduce-scatter.2.cloned.1.call-start = ((), (), s32[]{:S(2)}) async-start(), calls=%async_computation.4 | async-start | bytes 5242880 | tf_op jit(solution)/shard_map/reduce_scatter | solution.py:95
  217.1 47.2 %copy-start.3 = (bf16[1024,512]{1,0:T(8,128)(2,1)S(1)}, bf16[1024,512]{1,0:T(8,128)(2,1)}, u32[]{:S(2)}) copy-start(bf16[1024,512]{1,0:T(8,128)(2,1)} %param.10) | copy-start | bytes 3145732
Sparse Core Ops, SparseCore 0:
  9.2 62.8 all-gather.2
  98.7 104.5 all-gather.4
  217.2 47.0 reduce-scatter.1

commit v5 on v4

--- a/solution.py
+++ b/solution.py
@@ -78,22 +78,26 @@
 
 
 def on_device(queries, keys_values, out_weight, residual, segments):
-    n_seq = lax.axis_size("seq")
-    seq_idx = lax.axis_index("seq")
+    n_core = lax.axis_size("core")
+    n_seq = lax.axis_size("z") * n_core
     tok_dev = queries.shape[0]
     heads_ten = queries.shape[1] // HD
-    assert heads_ten == n_seq
+    kv_ten = keys_values.shape[2] // HD
+    assert heads_ten == n_seq and kv_ten == n_core
     group_size = H // KVH
-    head_major = jnp.transpose(queries.reshape(tok_dev, heads_ten, HD), (1, 0, 2))
-    query_parts = lax.all_to_all(head_major, "seq", split_axis=0, concat_axis=0, tiled=True)
+    order = np.array([group_size * (j % n_core) + j // n_core for j in range(n_seq)], dtype=np.int32)
+    head_major = jnp.transpose(queries.reshape(tok_dev, heads_ten, HD), (1, 0, 2))[order]
+    query_parts = lax.all_to_all(head_major, ("z", "core"), split_axis=0, concat_axis=0, tiled=True)
     query_head = query_parts.reshape(n_seq * tok_dev, HD)
     assert query_head.shape[0] == L
-    pair_all = lax.all_gather(keys_values, "seq", axis=0, tiled=True)
-    pair_head = lax.dynamic_slice_in_dim(pair_all, (seq_idx // group_size) * HD, HD, axis=2)
+    pair_split = keys_values.reshape(tok_dev, 2, kv_ten, HD)
+    pair_core = lax.all_to_all(pair_split, "core", split_axis=2, concat_axis=0, tiled=True)
+    pair_head = lax.all_gather(pair_core, "z", axis=0, tiled=True).reshape(n_seq * tok_dev, 2, HD)
     heads_out = flash(query_head, pair_head[:, 0, :], pair_head[:, 1, :], segments)
-    gathered = lax.all_gather(heads_out, "seq", axis=1, tiled=True)
+    gathered = lax.all_gather(heads_out, ("z", "core"), axis=1, tiled=True)
+    weight_rows = out_weight.reshape(heads_ten, HD, out_weight.shape[1])[order].reshape(out_weight.shape)
     summed = lax.psum_scatter(
-        jnp.dot(gathered, out_weight, preferred_element_type=jnp.float32).astype(jnp.bfloat16),
+        jnp.dot(gathered, weight_rows, preferred_element_type=jnp.float32).astype(jnp.bfloat16),
         "tensor",
         scatter_dimension=0,
         tiled=True,
@@ -102,13 +106,21 @@
 
 
 def solution(mesh):
+    n_dp, n_seq, n_ten = (mesh.shape[name] for name in ("dp", "seq", "tensor"))
+    sub_mesh = jax.sharding.Mesh(
+        mesh.devices.reshape(n_dp, n_seq // 2, 2, n_ten), ("dp", "z", "core", "tensor")
+    )
     placed = (
-        P(("dp", "seq"), "tensor"),
-        P(("dp", "seq"), None, "tensor"),
-        P("tensor", "seq"),
-        P(("dp", "tensor"), "seq"),
+        P(("dp", "z", "core"), "tensor"),
+        P(("dp", "z", "core"), None, "tensor"),
+        P("tensor", ("z", "core")),
+        P(("dp", "tensor"), ("z", "core")),
         P("dp"),
     )
     return jax.shard_map(
-        on_device, mesh=mesh, in_specs=placed, out_specs=P(("dp", "tensor"), "seq"), check_vma=False
+        on_device,
+        mesh=sub_mesh,
+        in_specs=placed,
+        out_specs=P(("dp", "tensor"), ("z", "core")),
+        check_vma=False,
     )

time: 275 us -> 281 us (1.022)
  waiting for transfers between devices: 191 us -> 184 us
  blocking collectives: 0 us -> 6.78 us
  local copies, waits for them, and re-layouts: 18.7 us -> 24.8 us
  Pallas kernels: 22.5 us -> 26.4 us
  starting transfers between devices: 10.1 us -> 7.21 us
    all_gather x2, waiting for transfers between devices: 144 us -> 137 us  [the longest x1 101 us: on_device(): gathered = lax.all_gather(heads_out, ('z', 'core'), axis=1, tiled=True)]
    all_to_all x0 -> x1, blocking collectives: none -> 6.78 us  [on_device(): lax.all_to_all(pair_split, 'core', split_axis=2, concat_axis=0, tiled=True)]
    pallas_call x1, Pallas kernels: 22.5 us -> 26.4 us  [flash(): pl.pallas_call(kernel, out_shape=jax.ShapeDtypeStruct((rows, HD), jnp.bfl...]
    gather x0 -> x2, local copies, waits for them, and re-layouts: none -> 3.68 us  [the longest x1 2.03 us: on_device(): out_weight.reshape(heads_ten, HD, out_weight.shape[1])[order]]
    all_to_all x1, starting transfers between devices: 9.97 us -> 7.13 us  [on_device(): lax.all_to_all(head_major, ('z', 'core'), split_axis=0, concat_axis=0, ti...]
  transfers between devices with their start and end apart: 4 -> 4, of which waited for: 3 -> 3; matrix products, arithmetic and copies ran while one was open for 6% -> 7% of each run, Pallas kernels for 0% -> 0%
where the time goes in v5:
time: 281 us
  waiting for transfers between devices  184 us (65%)
  Pallas kernels  26.4 us (9%)
  local copies, waits for them, and re-layouts  24.8 us (9%)
  matrix products  14.4 us (5%)
  between operations  13.2 us (5%)
  starting transfers between devices  7.21 us (3%)
  blocking collectives  6.78 us (2%)
  other arithmetic  3.37 us (1%)
    all_gather x1, waiting for transfers between devices, on_device(): gathered = lax.all_gather(heads_out, ('z', 'core'), axis=1, tiled=True)  101 us
    reduce_scatter x1, waiting for transfers between devices, on_device(): lax.psum_scatter(jnp.dot(gathered, weight_rows, preferred_element_type=jn...  47.2 us
    all_gather x1, waiting for transfers between devices, on_device(): lax.all_gather(pair_core, 'z', axis=0, tiled=True)  36.4 us
    pallas_call x1, Pallas kernels, flash(): pl.pallas_call(kernel, out_shape=jax.ShapeDtypeStruct((rows, HD), jnp.bfl...  26.4 us
    dot_general x1, matrix products, on_device(): jnp.dot(gathered, weight_rows, preferred_element_type=jnp.float32)  14.4 us
    gather x13, local copies, waits for them, and re-layouts, flash(): jnp.searchsorted(segments, first_docs, side='left') // bk  8.27 us
    all_to_all x1, starting transfers between devices, on_device(): lax.all_to_all(head_major, ('z', 'core'), split_axis=0, concat_axis=0, ti...  7.13 us
    all_to_all x1, blocking collectives, on_device(): lax.all_to_all(pair_split, 'core', split_axis=2, concat_axis=0, tiled=True)  6.78 us
  transfers between devices with their start and end apart: 4, of which 3 were waited for; matrix products, arithmetic and copies ran while one was open for 7% of the time, Pallas kernels for 0%

profile of v5, /device:TPU:1, one launch (start us, length us, event | category | flops | bytes accessed | tf_op | source)
XLA Modules:
  0.0 280.8 jit_solution(18148622117936281628)
XLA Ops:
  6.5 0.0 copy-start
  6.5 0.0 copy-start.5
  6.5 0.0 copy-start.4
  6.5 0.0 all-gather.3.cloned.1.call-start
  6.5 2.0 copy.22
  8.5 1.1 copy.23
  9.6 6.8 %all_to_all.23 = bf16[256,2,2,128]{3,0,1,2:T(8,128)(2,1)S(1)} all-to-all(bf16[256,2,2,128]{3,0,1,2:T(8,128)(2,1)S(1)} %copy.23), channel_id=1, replica_groups=mesh['dp'=4,'z'=8,'core'=2,'tensor'=4] {'core'}, dimensions={2} | all-to-all | bytes 524288 | tf_op jit(solution)/shard_map/all_to_all | solution.py:94
  16.4 0.7 copy.24
  17.1 0.0 all-gather.3.cloned.1.call-update
  17.2 0.0 copy-done.5
  17.2 0.0 copy-done.4
  17.2 1.3 copy.20
  18.5 1.6 copy.21
  20.1 0.0 copy-start.1
  20.1 1.7 gather_fusion.1
  21.8 7.1 %all-to-all-start = ((bf16[16,256,128]{2,1,0:T(8,128)(2,1)}), bf16[16,256,128]{2,1,0:T(8,128)(2,1)S(1)}, u32[]{:S(2)}, u32[]{:S(2)}) async-start(bf16[16,256,128]{2,1,0:T(8,128)(2,1)} %gather_fusion.1), calls=%async_computation | async-start | bytes 2097152 | tf_op jit(solution)/shard_map/all_to_all | solution.py:90
  28.9 0.0 all-gather.5.cloned.1.call-start
  29.0 0.0 copy-done.1
  29.0 0.1 slice.9
  29.1 9.0 %while.24 = (s32[]{:T(128)}, u32[8]{0:T(128)S(1)}, u32[8]{0:T(128)S(1)}, s32[4096]{0:T(1024)S(1)}, s32[8]{0:T(128)S(1)}, /*index=5*/s32[]{:T(128)}, s32[]{:T(128)}, s32[]{}) while((s32[]{:T(128)}, u32[8]{0:T(128)S(1)}, u32[8]{0:T(128)S(1)}, s32[4096]{0:T(1024)S(1)}, s32[8]{0:T(128)S(1)}, /*index=5*/s32[]{:T(128)}, s32[]{:T(128)}, ...), condition=%wide.region_1.2_spmd.clone, body=%wide.region_0.1_spmd.clone.sunk | while | flops 1132 | bytes 4620 | solution.py:57
  29.1 0.6 gather_fusion
  29.8 0.6 gather_fusion
  30.5 0.6 gather_fusion
  31.2 0.6 gather_fusion
  31.9 0.6 gather_fusion
  32.6 0.6 gather_fusion
  33.3 0.6 gather_fusion
  34.0 0.6 gather_fusion
  34.7 0.6 gather_fusion
  35.4 0.6 gather_fusion
  36.1 0.6 gather_fusion
  36.7 0.6 gather_fusion
  37.4 0.6 gather_fusion
  38.1 2.0 copy.25.segq_ref
  40.1 0.5 and_select_fusion.starts_ref
  40.6 36.4 %all-gather.3.cloned.1.call-done = bf16[4096,2,1,128]{3,0,1,2:T(8,128)(2,1)} async-done(((bf16[512,2,1,128]{3,0,1,2:T(8,128)(2,1)}), bf16[4096,2,1,128]{3,0,1,2:T(8,128)(2,1)}) %all-gather.3.cloned.1.call-update) | async-done | bytes 2097168 | tf_op jit(solution)/shard_map/all_gather | solution.py:95
  77.0 3.0 %slice_bitcast_fusion = (bf16[4096,128]{1,0:T(8,128)(2,1)}, bf16[4096,128]{1,0:T(8,128)(2,1)}) fusion(bf16[4096,2,128]{2,0,1:T(8,128)(2,1)} %bitcast.25), kind=kLoop, calls=%fused_computation.11 | loop fusion | bytes 4194304 | tf_op jit(solution)/shard_map/squeeze | solution.py:96
  80.0 0.0 all-to-all-done
  80.0 0.0 copy-start.2
  80.0 1.0 copy-done.2
  81.0 26.4 %shard_map.82 = bf16[4096,128]{1,0:T(8,128)(2,1)} custom-call(s32[8]{0:T(128)} %and_select_fusion.starts_ref, bf16[4096,128]{1,0:T(8,128)(2,1)} %bitcast.22, bf16[4096,128]{1,0:T(8,128)(2,1)} %get-tuple-element.102.k_ref, bf16[4096,128]{1,0:T(8,128)(2,1)} %get-tuple-element.101.v_ref, s32[4096,1]{1,0:T(8,128)} %copy.25.segq_ref, s32[1,4096]{1,0:T(1,128)S(1)} %bitcast.21), custom_call_target="tpu_custom_call" | custom-call | tf_op jit(solution)/shard_map/pallas_call | solution.py:61
  107.4 0.0 all-gather.5.cloned.1.call-update
  107.4 0.0 reduce-scatter.2.cloned.1.call-start
  107.5 0.0 copy-done
  107.5 2.0 gather_fusion.2
  109.5 100.7 %all-gather.5.cloned.1.call-done = bf16[4096,2048]{1,0:T(8,128)(2,1)} async-done(((bf16[4096,128]{1,0:T(8,128)(2,1)}), bf16[4096,2048]{1,0:T(8,128)(2,1)}) %all-gather.5.cloned.1.call-update) | async-done | bytes 16777232 | tf_op jit(solution)/shard_map/all_gather | solution.py:97
  210.2 14.4 %convolution_convert_fusion = bf16[4096,512]{1,0:T(8,128)(2,1)} fusion(bf16[4096,2048]{1,0:T(8,128)(2,1)} %all-gather.5.cloned.1.call-done, bf16[2048,512]{1,0:T(8,128)(2,1)} %bitcast.26), kind=kOutput, calls=%fused_computation.9 | convolution fusion | flops 8592031744 | bytes 23068672 | tf_op jit(solution)/shard_map/dot_general | solution.py:100
  224.6 0.0 copy-start.3
  224.6 0.0 reduce-scatter.2.cloned.1.call-update
  224.6 47.2 %reduce-scatter.2.cloned.1.call-done = bf16[1024,512]{1,0:T(8,128)(2,1)} async-done(((bf16[4096,512]{1,0:T(8,128)(2,1)}), bf16[1024,512]{1,0:T(8,128)(2,1)}) %reduce-scatter.2.cloned.1.call-update) | async-done | bytes 1048592 | tf_op jit(solution)/shard_map/reduce_scatter | solution.py:99
  271.8 0.0 copy-done.3
  271.8 2.5 add_convert_fusion
  (42 shorter events, 0.4 us)
Async XLA Ops:
  6.5 100.9 %copy-start = (bf16[2048,512]{1,0:T(8,128)(2,1)S(1)}, bf16[2048,512]{1,0:T(8,128)(2,1)}, u32[]{:S(2)}) copy-start(bf16[2048,512]{1,0:T(8,128)(2,1)} %param.12) | copy-start | bytes 6291460
  6.5 10.6 %copy-start.5 = (s32[16]{0:T(128)S(1)}, s32[16]{0:T(128)}, u32[]{:S(2)}) copy-start(s32[16]{0:T(128)} %constant.55) | copy-start | bytes 196
  6.5 10.6 %copy-start.4 = (bf16[256,2048]{1,0:T(8,128)(2,1)S(1)}, bf16[256,2048]{1,0:T(8,128)(2,1)}, u32[]{:S(2)}) copy-start(bf16[256,2048]{1,0:T(8,128)(2,1)} %param.10) | copy-start | bytes 3145732
  6.5 70.4 %all-gather.3.cloned.1.call-start = ((), (), s32[]{:S(2)}) async-start(), calls=%async_computation.3 | async-start | bytes 2359296 | tf_op jit(solution)/shard_map/all_gather | solution.py:95
  20.1 8.9 %copy-start.1 = (s32[4096]{0:T(1024)S(1)}, s32[4096]{0:T(1024)}, u32[]{:S(2)}) copy-start(s32[4096]{0:T(1024)} %param.14) | copy-start | bytes 49156
  21.8 58.2 %all-to-all-start = ((bf16[16,256,128]{2,1,0:T(8,128)(2,1)}), bf16[16,256,128]{2,1,0:T(8,128)(2,1)S(1)}, u32[]{:S(2)}, u32[]{:S(2)}) async-start(bf16[16,256,128]{2,1,0:T(8,128)(2,1)} %gather_fusion.1), calls=%async_computation | async-start | bytes 2097152 | tf_op jit(solution)/shard_map/all_to_all | solution.py:90
  28.9 181.3 %all-gather.5.cloned.1.call-start = ((), (), s32[]{:S(2)}) async-start(), calls=%async_computation.4 | async-start | bytes 17825792 | tf_op jit(solution)/shard_map/all_gather | solution.py:97
  80.0 1.0 copy-start.2
  107.4 164.4 %reduce-scatter.2.cloned.1.call-start = ((), (), s32[]{:S(2)}) async-start(), calls=%async_computation.5 | async-start | bytes 5242880 | tf_op jit(solution)/shard_map/reduce_scatter | solution.py:99
  224.6 47.2 %copy-start.3 = (bf16[1024,512]{1,0:T(8,128)(2,1)S(1)}, bf16[1024,512]{1,0:T(8,128)(2,1)}, u32[]{:S(2)}) copy-start(bf16[1024,512]{1,0:T(8,128)(2,1)} %param.13) | copy-start | bytes 3145732
Sparse Core Ops, SparseCore 0:
  17.3 59.6 all-gather.2
  107.5 102.6 all-gather.4
  224.7 47.0 reduce-scatter.1

commit v6 on v4

--- a/solution.py
+++ b/solution.py
@@ -92,12 +92,16 @@
     pair_head = lax.dynamic_slice_in_dim(pair_all, (seq_idx // group_size) * HD, HD, axis=2)
     heads_out = flash(query_head, pair_head[:, 0, :], pair_head[:, 1, :], segments)
     gathered = lax.all_gather(heads_out, "seq", axis=1, tiled=True)
-    summed = lax.psum_scatter(
-        jnp.dot(gathered, out_weight, preferred_element_type=jnp.float32).astype(jnp.bfloat16),
+    n_ten = lax.axis_size("tensor")
+    projected = jnp.dot(gathered, out_weight, preferred_element_type=jnp.float32).astype(jnp.bfloat16)
+    blocks = lax.all_to_all(
+        projected.reshape(n_ten, projected.shape[0] // n_ten, projected.shape[1]),
         "tensor",
-        scatter_dimension=0,
+        split_axis=0,
+        concat_axis=0,
         tiled=True,
     )
+    summed = jnp.sum(blocks.astype(jnp.float32), axis=0)
     return (residual.astype(jnp.float32) + summed).astype(jnp.bfloat16)
 
 

time: 275 us -> 277 us (level)
  waiting for transfers between devices: 191 us -> 138 us
  blocking collectives: 0 us -> 52.1 us
  Pallas kernels: 22.5 us -> 28.3 us
    all_to_all x0 -> x1, blocking collectives: none -> 52.1 us  [on_device(): lax.all_to_all(projected.reshape(n_ten, projected.shape[0] // n_ten, proj...]
    reduce_scatter x1 -> x0, waiting for transfers between devices: 47.2 us -> none  [on_device(): lax.psum_scatter(jnp.dot(gathered, out_weight, preferred_element_type=jnp...]
    all_gather x1, waiting for transfers between devices: 105 us -> 98.2 us  [on_device(): gathered = lax.all_gather(heads_out, 'seq', axis=1, tiled=True)]
    pallas_call x1, Pallas kernels: 22.5 us -> 28.3 us  [flash(): pl.pallas_call(kernel, out_shape=jax.ShapeDtypeStruct((rows, HD), jnp.bfl...]
  transfers between devices with their start and end apart: 4 -> 3, of which waited for: 3 -> 2; matrix products, arithmetic and copies ran while one was open for 6% -> 6% of each run, Pallas kernels for 0% -> 0%
where the time goes in v6:
time: 277 us
  waiting for transfers between devices  138 us (50%)
  blocking collectives  52.1 us (19%)
  Pallas kernels  28.3 us (10%)
  local copies, waits for them, and re-layouts  19.2 us (7%)
  between operations  13.5 us (5%)
  matrix products  12.4 us (4%)
  starting transfers between devices  10 us (4%)
  other arithmetic  2.93 us (1%)
    all_gather x1, waiting for transfers between devices, on_device(): gathered = lax.all_gather(heads_out, 'seq', axis=1, tiled=True)  98.2 us
    all_to_all x1, blocking collectives, on_device(): lax.all_to_all(projected.reshape(n_ten, projected.shape[0] // n_ten, proj...  52.1 us
    all_gather x1, waiting for transfers between devices, on_device(): pair_all = lax.all_gather(keys_values, 'seq', axis=0, tiled=True)  39.5 us
    pallas_call x1, Pallas kernels, flash(): pl.pallas_call(kernel, out_shape=jax.ShapeDtypeStruct((rows, HD), jnp.bfl...  28.3 us
    dot_general x1, matrix products, on_device(): jnp.dot(gathered, out_weight, preferred_element_type=jnp.float32)  12.4 us
    all_to_all x1, starting transfers between devices, on_device(): lax.all_to_all(head_major, 'seq', split_axis=0, concat_axis=0, tiled=True)  9.97 us
    gather x13, local copies, waits for them, and re-layouts, flash(): jnp.searchsorted(segments, first_docs, side='left') // bk  8.27 us
  transfers between devices with their start and end apart: 3, of which 2 were waited for; matrix products, arithmetic and copies ran while one was open for 6% of the time, Pallas kernels for 0%

profile of v6, /device:TPU:1, one launch (start us, length us, event | category | flops | bytes accessed | tf_op | source)
XLA Modules:
  0.0 276.6 jit_solution(10229862734242949444)
XLA Ops:
  6.5 0.0 copy-start
  6.5 0.0 copy-start.1
  6.5 0.0 all-gather.3.cloned.1.call-start
  6.5 1.8 copy.9
  8.4 0.0 all-gather.3.cloned.1.call-update
  8.4 2.5 bitcast_bitcast_fusion
  10.9 10.0 %all-to-all-start = ((bf16[16,256,128]{2,1,0:T(8,128)(2,1)}), bf16[16,256,128]{2,1,0:T(8,128)(2,1)S(1)}, u32[]{:S(2)}, u32[]{:S(2)}) async-start(bf16[16,256,128]{2,1,0:T(8,128)(2,1)} %bitcast_bitcast_fusion), calls=%async_computation | async-start | bytes 2097152 | tf_op jit(solution)/shard_map/all_to_all | solution.py:88
  20.8 0.0 all-gather.5.cloned.1.call-start
  20.9 0.0 copy-done.1
  20.9 0.1 slice.9
  21.0 9.0 %while.24 = (s32[]{:T(128)}, u32[8]{0:T(128)S(1)}, u32[8]{0:T(128)S(1)}, s32[4096]{0:T(1024)S(1)}, s32[8]{0:T(128)S(1)}, /*index=5*/s32[]{:T(128)}, s32[]{:T(128)}, s32[]{}) while((s32[]{:T(128)}, u32[8]{0:T(128)S(1)}, u32[8]{0:T(128)S(1)}, s32[4096]{0:T(1024)S(1)}, s32[8]{0:T(128)S(1)}, /*index=5*/s32[]{:T(128)}, s32[]{:T(128)}, ...), condition=%wide.region_1.2_spmd.clone, body=%wide.region_0.1_spmd.clone.sunk | while | flops 1132 | bytes 4620 | solution.py:57
  21.0 0.6 gather_fusion
  21.7 0.6 gather_fusion
  22.4 0.6 gather_fusion
  23.1 0.6 gather_fusion
  23.8 0.6 gather_fusion
  24.5 0.6 gather_fusion
  25.2 0.6 gather_fusion
  25.9 0.6 gather_fusion
  26.6 0.6 gather_fusion
  27.3 0.6 gather_fusion
  28.0 0.6 gather_fusion
  28.7 0.6 gather_fusion
  29.4 0.6 gather_fusion
  30.1 2.0 copy.10.segq_ref
  32.0 0.6 and_select_fusion.starts_ref
  32.6 39.5 %all-gather.3.cloned.1.call-done = bf16[4096,2,256]{2,0,1:T(8,128)(2,1)} async-done(((bf16[256,2,256]{2,0,1:T(8,128)(2,1)}), bf16[4096,2,256]{2,0,1:T(8,128)(2,1)}) %all-gather.3.cloned.1.call-update) | async-done | bytes 4194320 | tf_op jit(solution)/shard_map/all_gather | solution.py:91
  72.1 3.0 %dynamic-slice_bitcast_fusion = (bf16[4096,128]{1,0:T(8,128)(2,1)}, bf16[4096,128]{1,0:T(8,128)(2,1)}) fusion(bf16[4096,2,256]{2,0,1:T(8,128)(2,1)} %all-gather.3.cloned.1.call-done, s32[]{:T(128)S(6)} %add.24, s32[]{:T(128)S(6)} %select_n.27), kind=kLoop, calls=%fused_computation.11 | loop fusion | bytes 4194312 | tf_op jit(solution)/shard_map/squeeze | solution.py:93
  75.1 0.0 all-to-all-done
  75.1 0.0 copy-start.2
  75.1 1.0 copy-done.2
  76.1 28.3 %shard_map.55 = bf16[4096,128]{1,0:T(8,128)(2,1)} custom-call(s32[8]{0:T(128)} %and_select_fusion.starts_ref, bf16[4096,128]{1,0:T(8,128)(2,1)} %bitcast.19, bf16[4096,128]{1,0:T(8,128)(2,1)} %get-tuple-element.102.k_ref, bf16[4096,128]{1,0:T(8,128)(2,1)} %get-tuple-element.101.v_ref, s32[4096,1]{1,0:T(8,128)} %copy.10.segq_ref, s32[1,4096]{1,0:T(1,128)S(1)} %bitcast.18), custom_call_target="tpu_custom_call" | custom-call | tf_op jit(solution)/shard_map/pallas_call | solution.py:61
  104.4 0.0 all-gather.5.cloned.1.call-update
  104.4 98.2 %all-gather.5.cloned.1.call-done = bf16[4096,2048]{1,0:T(8,128)(2,1)} async-done(((bf16[4096,128]{1,0:T(8,128)(2,1)}), bf16[4096,2048]{1,0:T(8,128)(2,1)}) %all-gather.5.cloned.1.call-update) | async-done | bytes 16777232 | tf_op jit(solution)/shard_map/all_gather | solution.py:94
  202.6 0.0 copy-done
  202.6 12.4 %convolution_convert_fusion = bf16[4096,512]{1,0:T(8,128)(2,1)S(1)} fusion(bf16[4096,2048]{1,0:T(8,128)(2,1)} %all-gather.5.cloned.1.call-done, bf16[2048,512]{1,0:T(8,128)(2,1)S(1)} %copy-done), kind=kOutput, calls=%fused_computation.8 | convolution fusion | flops 8592031744 | bytes 23068672 | tf_op jit(solution)/shard_map/dot_general | solution.py:96
  215.1 52.1 %all_to_all.10 = bf16[4,1024,512]{2,1,0:T(8,128)(2,1)S(1)} all-to-all(bf16[4,1024,512]{2,1,0:T(8,128)(2,1)S(1)} %bitcast.20), channel_id=1, replica_groups=mesh['dp'=4,'seq'=16,'tensor'=4] {'tensor'}, dimensions={0} | all-to-all | bytes 8388608 | tf_op jit(solution)/shard_map/all_to_all | solution.py:97
  267.2 0.0 copy-start.3
  267.2 0.7 convert_reduce_fusion
  267.9 0.6 copy-done.3
  268.4 1.3 add_convert_fusion
  (41 shorter events, 0.4 us)
Async XLA Ops:
  6.5 196.1 %copy-start = (bf16[2048,512]{1,0:T(8,128)(2,1)S(1)}, bf16[2048,512]{1,0:T(8,128)(2,1)}, u32[]{:S(2)}) copy-start(bf16[2048,512]{1,0:T(8,128)(2,1)} %param.9) | copy-start | bytes 6291460
  6.5 14.4 %copy-start.1 = (s32[4096]{0:T(1024)S(1)}, s32[4096]{0:T(1024)}, u32[]{:S(2)}) copy-start(s32[4096]{0:T(1024)} %param.11) | copy-start | bytes 49156
  6.5 65.5 %all-gather.3.cloned.1.call-start = ((), (), s32[]{:S(2)}) async-start(), calls=%async_computation.2 | async-start | bytes 4456448 | tf_op jit(solution)/shard_map/all_gather | solution.py:91
  10.9 64.2 %all-to-all-start = ((bf16[16,256,128]{2,1,0:T(8,128)(2,1)}), bf16[16,256,128]{2,1,0:T(8,128)(2,1)S(1)}, u32[]{:S(2)}, u32[]{:S(2)}) async-start(bf16[16,256,128]{2,1,0:T(8,128)(2,1)} %bitcast_bitcast_fusion), calls=%async_computation | async-start | bytes 2097152 | tf_op jit(solution)/shard_map/all_to_all | solution.py:88
  20.8 181.8 %all-gather.5.cloned.1.call-start = ((), (), s32[]{:S(2)}) async-start(), calls=%async_computation.3 | async-start | bytes 17825792 | tf_op jit(solution)/shard_map/all_gather | solution.py:94
  75.1 1.0 copy-start.2
  267.2 1.2 copy-start.3
Sparse Core Ops, SparseCore 0:
  9.2 62.8 all-gather.2
  104.5 98.0 all-gather.4

commit v7 on v4

--- a/solution.py
+++ b/solution.py
@@ -79,11 +79,22 @@
 
 def on_device(queries, keys_values, out_weight, residual, segments):
     n_seq = lax.axis_size("seq")
+    n_ten = lax.axis_size("tensor")
     seq_idx = lax.axis_index("seq")
+    ten_idx = lax.axis_index("tensor")
     tok_dev = queries.shape[0]
     heads_ten = queries.shape[1] // HD
     assert heads_ten == n_seq
     group_size = H // KVH
+    received = [out_weight] + [
+        lax.ppermute(out_weight, "tensor", [(j, (j + shift) % n_ten) for j in range(n_ten)])
+        for shift in range(1, n_ten)
+    ]
+    by_shift = jnp.stack(received).reshape(n_ten, n_seq, HD, out_weight.shape[1])
+    source = (ten_idx - jnp.arange(n_ten)) % n_ten
+    weight_all = jnp.transpose(jnp.take(by_shift, source, axis=0), (1, 0, 2, 3)).reshape(
+        n_ten * out_weight.shape[0], out_weight.shape[1]
+    )
     head_major = jnp.transpose(queries.reshape(tok_dev, heads_ten, HD), (1, 0, 2))
     query_parts = lax.all_to_all(head_major, "seq", split_axis=0, concat_axis=0, tiled=True)
     query_head = query_parts.reshape(n_seq * tok_dev, HD)
@@ -91,14 +102,12 @@
     pair_all = lax.all_gather(keys_values, "seq", axis=0, tiled=True)
     pair_head = lax.dynamic_slice_in_dim(pair_all, (seq_idx // group_size) * HD, HD, axis=2)
     heads_out = flash(query_head, pair_head[:, 0, :], pair_head[:, 1, :], segments)
-    gathered = lax.all_gather(heads_out, "seq", axis=1, tiled=True)
-    summed = lax.psum_scatter(
-        jnp.dot(gathered, out_weight, preferred_element_type=jnp.float32).astype(jnp.bfloat16),
-        "tensor",
-        scatter_dimension=0,
-        tiled=True,
-    )
-    return (residual.astype(jnp.float32) + summed).astype(jnp.bfloat16)
+    out_rows = heads_out.shape[0] // n_ten
+    row_parts = lax.all_to_all(heads_out.reshape(n_ten, out_rows, HD), "tensor", split_axis=0, concat_axis=0, tiled=True)
+    token_major = jnp.transpose(row_parts, (1, 0, 2))
+    gathered = lax.all_gather(token_major, "seq", axis=1, tiled=False).reshape(out_rows, n_seq * n_ten * HD)
+    projected = jnp.dot(gathered, weight_all, preferred_element_type=jnp.float32)
+    return (residual.astype(jnp.float32) + projected).astype(jnp.bfloat16)
 
 
 def solution(mesh):

time: 275 us -> 256 us (0.931); the launches traced: 273 us -> 251 us
  waiting for transfers between devices: 191 us -> 133 us
  blocking collectives: 0 us -> 19.2 us
  local copies, waits for them, and re-layouts: 18.7 us -> 31.1 us
    all_gather x1, waiting for transfers between devices: 105 us -> 0.01 us  [on_device(): lax.all_gather(token_major, 'seq', axis=1, tiled=False)]
    ppermute x0 -> x3, waiting for transfers between devices: none -> 93.1 us  [on_device(): lax.ppermute(out_weight, 'tensor', [(j, (j + shift) % n_ten) for j in ran...]
    reduce_scatter x1 -> x0, waiting for transfers between devices: 47.2 us -> none  [on_device(): lax.psum_scatter(jnp.dot(gathered, out_weight, preferred_element_type=jnp...]
    all_to_all x0 -> x1, blocking collectives: none -> 19.2 us  [on_device(): lax.all_to_all(heads_out.reshape(n_ten, out_rows, HD), 'tensor', split_ax...]
    gather x0 -> x3, local copies, waits for them, and re-layouts: none -> 13.7 us  [on_device(): jnp.take(by_shift, source, axis=0)]
    another operation x0 -> x1, other arithmetic: none -> 4.43 us  [on_device(): jnp.stack(received).reshape(n_ten, n_seq, HD, out_weight.shape[1])]
  transfers between devices with their start and end apart: 4 -> 6, of which waited for: 3 -> 4; matrix products, arithmetic and copies ran while one was open for 6% -> 13% of each run, Pallas kernels for 0% -> 0%
where the time goes in v7:
time: 256 us; the launch traced here: 251 us
  waiting for transfers between devices  133 us (52%)
  local copies, waits for them, and re-layouts  31.1 us (12%)
  Pallas kernels  22.5 us (9%)
  blocking collectives  19.2 us (8%)
  matrix products  14.2 us (6%)
  between operations  13.5 us (5%)
  starting transfers between devices  12.2 us (5%)
  other arithmetic  5.32 us (2%)
    ppermute x3, waiting for transfers between devices, on_device(): lax.ppermute(out_weight, 'tensor', [(j, (j + shift) % n_ten) for j in ran...  93.1 us
    all_gather x1, waiting for transfers between devices, on_device(): pair_all = lax.all_gather(keys_values, 'seq', axis=0, tiled=True)  39.7 us
    pallas_call x1, Pallas kernels, flash(): pl.pallas_call(kernel, out_shape=jax.ShapeDtypeStruct((rows, HD), jnp.bfl...  22.5 us
    all_to_all x1, blocking collectives, on_device(): lax.all_to_all(heads_out.reshape(n_ten, out_rows, HD), 'tensor', split_ax...  19.2 us
    dot_general x1, matrix products, on_device(): jnp.dot(gathered, weight_all, preferred_element_type=jnp.float32)  14.2 us
    gather x3, local copies, waits for them, and re-layouts, on_device(): jnp.take(by_shift, source, axis=0)  13.7 us
    all_to_all x1, starting transfers between devices, on_device(): lax.all_to_all(head_major, 'seq', split_axis=0, concat_axis=0, tiled=True)  9.97 us
    gather x13, local copies, waits for them, and re-layouts, flash(): jnp.searchsorted(segments, first_docs, side='left') // bk  8.27 us
  transfers between devices with their start and end apart: 6, of which 4 were waited for; matrix products, arithmetic and copies ran while one was open for 13% of the time, Pallas kernels for 0%

profile of v7, /device:TPU:1, one launch (start us, length us, event | category | flops | bytes accessed | tf_op | source)
XLA Modules:
  0.0 251.1 jit_solution(385163831083285731)
XLA Ops:
  6.5 0.0 copy-start
  6.5 0.0 copy-start.1
  6.5 0.0 all-gather.4.cloned.1.call-start
  6.5 1.8 copy.13
  8.3 0.0 all-gather.4.cloned.1.call-update
  8.3 0.0 copy-done
  8.4 1.2 bitcast_bitcast_fusion
  9.6 10.0 %all-to-all-start = ((bf16[16,256,128]{2,1,0:T(8,128)(2,1)}), bf16[16,256,128]{2,1,0:T(8,128)(2,1)S(1)}, u32[]{:S(2)}, u32[]{:S(2)}) async-start(bf16[16,256,128]{2,1,0:T(8,128)(2,1)} %bitcast_bitcast_fusion), calls=%async_computation | async-start | bytes 2097152 | tf_op jit(solution)/shard_map/all_to_all | solution.py:99
  19.6 0.0 all-gather.6.cloned.1.call-start
  19.6 0.0 copy-done.1
  19.6 0.1 slice.9
  19.7 9.0 %while.24 = (s32[]{:T(128)}, u32[8]{0:T(128)S(1)}, u32[8]{0:T(128)S(1)}, s32[4096]{0:T(1024)S(1)}, s32[8]{0:T(128)S(1)}, /*index=5*/s32[]{:T(128)}, s32[]{:T(128)}, s32[]{}) while((s32[]{:T(128)}, u32[8]{0:T(128)S(1)}, u32[8]{0:T(128)S(1)}, s32[4096]{0:T(1024)S(1)}, s32[8]{0:T(128)S(1)}, /*index=5*/s32[]{:T(128)}, s32[]{:T(128)}, ...), condition=%wide.region_1.2_spmd.clone, body=%wide.region_0.1_spmd.clone.sunk | while | flops 1132 | bytes 4628 | solution.py:57
  19.7 0.6 gather_fusion
  20.4 0.6 gather_fusion
  21.1 0.6 gather_fusion
  21.8 0.6 gather_fusion
  22.5 0.6 gather_fusion
  23.2 0.6 gather_fusion
  23.9 0.6 gather_fusion
  24.6 0.6 gather_fusion
  25.3 0.6 gather_fusion
  26.0 0.6 gather_fusion
  26.7 0.6 gather_fusion
  27.4 0.6 gather_fusion
  28.1 0.6 gather_fusion
  28.8 2.0 copy.14.segq_ref
  30.8 0.5 and_select_fusion.2.starts_ref
  31.3 39.7 %all-gather.4.cloned.1.call-done = bf16[4096,2,256]{2,0,1:T(8,128)(2,1)} async-done(((bf16[256,2,256]{2,0,1:T(8,128)(2,1)}), bf16[4096,2,256]{2,0,1:T(8,128)(2,1)}) %all-gather.4.cloned.1.call-update) | async-done | bytes 4194320 | tf_op jit(solution)/shard_map/all_gather | solution.py:102
  70.9 3.0 %dynamic-slice_bitcast_fusion = (bf16[4096,128]{1,0:T(8,128)(2,1)}, bf16[4096,128]{1,0:T(8,128)(2,1)}) fusion(bf16[4096,2,256]{2,0,1:T(8,128)(2,1)} %all-gather.4.cloned.1.call-done, s32[]{:T(128)S(6)} %add.60, s32[]{:T(128)S(6)} %select_n.68), kind=kLoop, calls=%fused_computation.17 | loop fusion | bytes 4194312 | tf_op jit(solution)/shard_map/squeeze | solution.py:104
  74.0 0.0 all-to-all-done
  74.0 0.0 copy-start.2
  74.0 1.0 copy-done.2
  74.9 22.5 %shard_map.55 = bf16[4096,128]{1,0:T(8,128)(2,1)} custom-call(s32[8]{0:T(128)} %and_select_fusion.2.starts_ref, bf16[4096,128]{1,0:T(8,128)(2,1)} %bitcast.36, bf16[4096,128]{1,0:T(8,128)(2,1)} %get-tuple-element.104.k_ref, bf16[4096,128]{1,0:T(8,128)(2,1)} %get-tuple-element.103.v_ref, s32[4096,1]{1,0:T(8,128)} %copy.14.segq_ref, s32[1,4096]{1,0:T(1,128)S(1)} %bitcast.35), custom_call_target="tpu_custom_call" | custom-call | tf_op jit(solution)/shard_map/pallas_call | solution.py:61
  97.4 19.2 %all_to_all.10 = bf16[4,1024,128]{2,1,0:T(8,128)(2,1)} all-to-all(bf16[4,1024,128]{2,1,0:T(8,128)(2,1)} %bitcast.37), channel_id=1, replica_groups=mesh['dp'=4,'seq'=16,'tensor'=4] {'tensor'}, dimensions={0} | all-to-all | bytes 2097152 | tf_op jit(solution)/shard_map/all_to_all | solution.py:106
  116.6 0.0 all-gather.6.cloned.1.call-update
  116.6 1.0 collective-permute-start.2
  117.6 1.2 collective-permute-start.1
  118.8 0.0 collective-permute-start
  118.8 44.2 %collective-permute-done.2 = bf16[2048,512]{1,0:T(8,128)(2,1)} collective-permute-done((bf16[2048,512]{1,0:T(8,128)(2,1)}, bf16[2048,512]{1,0:T(8,128)(2,1)}, u32[]{:S(2)}, u32[]{:S(2)}) %collective-permute-start.2) | collective-permute-done | bytes 2097184 | tf_op jit(solution)/shard_map/ppermute | solution.py:90
  163.0 2.2 collective-permute-done.1
  165.2 46.7 %collective-permute-done = bf16[2048,512]{1,0:T(8,128)(2,1)} collective-permute-done((bf16[2048,512]{1,0:T(8,128)(2,1)}, bf16[2048,512]{1,0:T(8,128)(2,1)}, u32[]{:S(2)}, u32[]{:S(2)}) %collective-permute-start) | collective-permute-done | bytes 2097184 | tf_op jit(solution)/shard_map/ppermute | solution.py:90
  211.9 4.4 %pad_maximum_fusion = bf16[4,16,128,512]{3,2,1,0:T(8,128)(2,1)S(1)} fusion(bf16[1,16,128,512]{3,2,1,0:T(8,128)(2,1)} %bitcast.12, bf16[1,16,128,512]{3,2,1,0:T(8,128)(2,1)} %bitcast.11, bf16[1,16,128,512]{3,2,1,0:T(8,128)(2,1)} %bitcast.10, bf16[1,16,128,512]{3,2,1,0:T(8,128)(2,1)} %bitcast.39), kind=kLoop, calls=%fused_computation.9 | loop fusion | flops 12582912 | bytes 16777216 | tf_op jit(solution)/shard_map/stack | solution.py:93
  216.4 3.7 %fusion.9 = (bf16[4,16,128,256]{3,2,1,0:T(8,128)(2,1)}, bf16[4,16,128,256]{3,2,1,0:T(8,128)(2,1)}) fusion(bf16[4,16,128,512]{3,2,1,0:T(8,128)(2,1)S(1)} %pad_maximum_fusion), kind=kLoop, calls=%fused_computation.36 | loop fusion | bytes 16777216 | tf_op jit(solution)/shard_map/jit(_take)/gather | solution.py:95
  220.0 5.0 %gather_fusion.2 = bf16[4,16,128,256]{3,2,1,0:T(8,128)(2,1)} fusion(bf16[4,16,128,256]{3,2,1,0:T(8,128)(2,1)} %get-tuple-element.102, s32[1024]{0:T(1024)S(1)} %pad_clamp_fusion.1), kind=kCustom, calls=%fused_computation.2 | custom fusion | bytes 8388624 | tf_op jit(solution)/shard_map/jit(_take)/gather | solution.py:95
  225.0 0.0 copy-start.3
  225.0 5.1 %gather_fusion.1 = bf16[4,16,128,256]{3,2,1,0:T(8,128)(2,1)} fusion(bf16[4,16,128,256]{3,2,1,0:T(8,128)(2,1)} %get-tuple-element.101, s32[1024]{0:T(1024)S(1)} %pad_clamp_fusion.1), kind=kCustom, calls=%fused_computation.1 | custom fusion | bytes 8388624 | tf_op jit(solution)/shard_map/jit(_take)/gather | solution.py:95
  230.0 0.0 all-gather.6.cloned.1.call-done
  230.0 0.0 copy-done.3
  230.0 14.2 %fusion.3 = bf16[1024,512]{1,0:T(8,128)(2,1)} fusion(bf16[1024,512]{1,0:T(8,128)(2,1)S(1)} %copy-done.3, bf16[1024,16,4,128]{3,0,2,1:T(8,128)(2,1)} %bitcast.40, bf16[4,16,128,256]{3,2,1,0:T(8,128)(2,1)} %gather_fusion.2, bf16[4,16,128,256]{3,2,1,0:T(8,128)(2,1)} %gather_fusion.1, pred[4]{0:T(512)(128)(4,1)S(1)} %compare_and_fusion), kind=kOutput, calls=%fused_computation.15 | convolution fusion | flops 8612478976 | bytes 27262980 | tf_op jit(solution)/shard_map/dot_general | solution.py:109
  (44 shorter events, 0.4 us)
Async XLA Ops:
  6.5 1.8 copy-start
  6.5 13.1 %copy-start.1 = (s32[4096]{0:T(1024)S(1)}, s32[4096]{0:T(1024)}, u32[]{:S(2)}) copy-start(s32[4096]{0:T(1024)} %param.11) | copy-start | bytes 49156
  6.5 64.4 %all-gather.4.cloned.1.call-start = ((), (), s32[]{:S(2)}) async-start(), calls=%async_computation.2 | async-start | bytes 4456448 | tf_op jit(solution)/shard_map/all_gather | solution.py:102
  9.6 64.4 %all-to-all-start = ((bf16[16,256,128]{2,1,0:T(8,128)(2,1)}), bf16[16,256,128]{2,1,0:T(8,128)(2,1)S(1)}, u32[]{:S(2)}, u32[]{:S(2)}) async-start(bf16[16,256,128]{2,1,0:T(8,128)(2,1)} %bitcast_bitcast_fusion), calls=%async_computation | async-start | bytes 2097152 | tf_op jit(solution)/shard_map/all_to_all | solution.py:99
  19.6 210.5 %all-gather.6.cloned.1.call-start = ((), (), s32[]{:S(2)}) async-start(), calls=%async_computation.3 | async-start | bytes 17825792 | tf_op jit(solution)/shard_map/all_gather | solution.py:108
  74.0 1.0 copy-start.2
  116.6 46.4 %collective-permute-start.2 = (bf16[2048,512]{1,0:T(8,128)(2,1)}, bf16[2048,512]{1,0:T(8,128)(2,1)}, u32[]{:S(2)}, u32[]{:S(2)}) collective-permute-start(bf16[2048,512]{1,0:T(8,128)(2,1)} %param.9), channel_id=1, source_target_pairs={{0,3},{1,0},{2,1},{3,2},{4,7},{5,4},{6,5},{7,6},{8,11},{9,8},{10,9... | collective-permute-start | bytes 6291464 | tf_op jit(solution)/shard_map/ppermute | solution.py:90
  117.6 47.6 %collective-permute-start.1 = (bf16[2048,512]{1,0:T(8,128)(2,1)}, bf16[2048,512]{1,0:T(8,128)(2,1)}, u32[]{:S(2)}, u32[]{:S(2)}) collective-permute-start(bf16[2048,512]{1,0:T(8,128)(2,1)} %param.9), channel_id=1, source_target_pairs={{0,2},{1,3},{2,0},{3,1},{4,6},{5,7},{6,4},{7,5},{8,10},{9,11},{10,... | collective-permute-start | bytes 6291464 | tf_op jit(solution)/shard_map/ppermute | solution.py:90
  118.8 93.1 %collective-permute-start = (bf16[2048,512]{1,0:T(8,128)(2,1)}, bf16[2048,512]{1,0:T(8,128)(2,1)}, u32[]{:S(2)}, u32[]{:S(2)}) collective-permute-start(bf16[2048,512]{1,0:T(8,128)(2,1)} %param.9), channel_id=1, source_target_pairs={{0,1},{1,2},{2,3},{3,0},{4,5},{5,6},{6,7},{7,4},{8,9},{9,10},{10,1... | collective-permute-start | bytes 6291464 | tf_op jit(solution)/shard_map/ppermute | solution.py:90
  225.0 5.1 %copy-start.3 = (bf16[1024,512]{1,0:T(8,128)(2,1)S(1)}, bf16[1024,512]{1,0:T(8,128)(2,1)}, u32[]{:S(2)}) copy-start(bf16[1024,512]{1,0:T(8,128)(2,1)} %param.10) | copy-start | bytes 3145732
Sparse Core Ops, SparseCore 0:
  9.2 61.6 all-gather.3
  116.8 97.6 all-gather.5

commit v8 on v7

v8 whole, which is shorter than its diff:
```python
import functools
import jax
import jax.numpy as jnp
from jax import lax
from jax.experimental import pallas as pl
from jax.experimental.pallas import tpu as pltpu
from jax.sharding import PartitionSpec as P

H = 64
KVH = 8
HD = 128
L = 4096


def flash_kernel(starts_ref, offset_ref, q_ref, k_ref, v_ref, segq_ref, segk_ref, o_ref, *, bq, bk):
    qi = offset_ref[0] + pl.program_id(0)
    q = q_ref[...]
    seg_q = segq_ref[...]
    row_pos = qi * bq + lax.broadcasted_iota(jnp.int32, (bq, bk), 0)

    def body(kb, carry):
        m_prev, l_prev, acc_prev = carry
        start = pl.multiple_of(kb * bk, bk)
        k_blk = k_ref[pl.ds(start, bk), :]
        v_blk = v_ref[pl.ds(start, bk), :]
        seg_k = segk_ref[:, pl.ds(start, bk)]
        scores = lax.dot_general(
            q, k_blk, (((1,), (1,)), ((), ())), preferred_element_type=jnp.float32
        ) * (HD ** -0.5)
        col_pos = start + lax.broadcasted_iota(jnp.int32, (bq, bk), 1)
        allowed = (col_pos <= row_pos) & (seg_q == seg_k)
        masked = jnp.where(allowed, scores, -1e30)
        m_new = jnp.maximum(m_prev, jnp.max(masked, axis=1, keepdims=True))
        alpha = jnp.exp(m_prev - m_new)
        probs = jnp.where(allowed, jnp.exp(masked - m_new), 0.0)
        l_new = alpha * l_prev + jnp.sum(probs, axis=1, keepdims=True)
        acc_new = alpha * acc_prev + jnp.dot(
            probs.astype(jnp.bfloat16), v_blk, preferred_element_type=jnp.float32
        )
        return m_new, l_new, acc_new

    init = (
        jnp.full((bq, 1), -1e30, jnp.float32),
        jnp.zeros((bq, 1), jnp.float32),
        jnp.zeros((bq, HD), jnp.float32),
    )
    last = (qi * bq + bq - 1) // bk
    _, l_fin, acc_fin = lax.fori_loop(starts_ref[qi], last + 1, body, init)
    o_ref[...] = (acc_fin / l_fin).astype(o_ref.dtype)


def block_starts(segments, bq, bk):
    first_docs = segments[::bq]
    return (jnp.searchsorted(segments, first_docs, side="left") // bk).astype(jnp.int32)


def flash(query_head, key_head, value_head, segments, starts, row_block, rows_out, bq=512, bk=512):
    rows = query_head.shape[0]
    seg_col = segments.reshape(rows, 1)
    seg_row = segments.reshape(1, rows)
    offset = (row_block * (rows_out // bq)).astype(jnp.int32).reshape(1)
    kernel = functools.partial(flash_kernel, bq=bq, bk=bk)
    return pl.pallas_call(
        kernel,
        out_shape=jax.ShapeDtypeStruct((rows_out, HD), jnp.bfloat16),
        grid_spec=pltpu.PrefetchScalarGridSpec(
            num_scalar_prefetch=2,
            grid=(rows_out // bq,),
            in_specs=[
                pl.BlockSpec((bq, HD), lambda i, s, o: (o[0] + i, 0)),
                pl.BlockSpec((rows, HD), lambda i, s, o: (0, 0)),
                pl.BlockSpec((rows, HD), lambda i, s, o: (0, 0)),
                pl.BlockSpec((bq, 1), lambda i, s, o: (o[0] + i, 0)),
                pl.BlockSpec((1, rows), lambda i, s, o: (0, 0)),
            ],
            out_specs=pl.BlockSpec((bq, HD), lambda i, s, o: (i, 0)),
        ),
        compiler_params=pltpu.CompilerParams(dimension_semantics=("arbitrary",)),
    )(starts, offset, query_head, key_head, value_head, seg_col, seg_row)


def layer(queries, keys_values, out_weight, residual, segments):
    n_seq = lax.axis_size("seq")
    n_ten = lax.axis_size("tensor")
    seq_idx = lax.axis_index("seq")
    ten_idx = lax.axis_index("tensor")
    tok_dev = queries.shape[0]
    heads_ten = queries.shape[1] // HD
    assert heads_ten == n_seq
    group_size = H // KVH
    received = [out_weight] + [
        lax.ppermute(out_weight, "tensor", [(j, (j + shift) % n_ten) for j in range(n_ten)])
        for shift in range(1, n_ten)
    ]
    weight_all = jnp.stack(received).reshape(n_ten * out_weight.shape[0], out_weight.shape[1])
    head_major = jnp.transpose(queries.reshape(tok_dev, heads_ten, HD), (1, 0, 2))
    query_parts = lax.all_to_all(head_major, "seq", split_axis=0, concat_axis=0, tiled=True)
    query_head = query_parts.reshape(n_seq * tok_dev, HD)
    assert query_head.shape[0] == L
    pair_all = lax.all_gather(keys_values, "seq", axis=0, tiled=True)
    pair_head = lax.dynamic_slice_in_dim(pair_all, (seq_idx // group_size) * HD, HD, axis=2)
    key_head = pair_head[:, 0, :]
    value_head = pair_head[:, 1, :]
    out_rows = query_head.shape[0] // n_ten
    starts = block_starts(segments, 512, 512)
    by_shift = [None] * n_ten
    for shift in list(range(1, n_ten)) + [0]:
        target = (ten_idx + shift) % n_ten
        block = flash(query_head, key_head, value_head, segments, starts, target, out_rows)
        if shift:
            block = lax.ppermute(block, "tensor", [(j, (j + shift) % n_ten) for j in range(n_ten)])
        by_shift[shift] = block
    token_major = jnp.stack(by_shift, axis=1)
    gathered = lax.all_gather(token_major, "seq", axis=2, tiled=False).reshape(out_rows, n_ten * n_seq * HD)
    projected = jnp.dot(gathered, weight_all, preferred_element_type=jnp.float32)
    return (residual.astype(jnp.float32) + projected).astype(jnp.bfloat16)


def solution(mesh):
    placed = (
        P(("dp", "seq"), "tensor"),
        P(("dp", "seq"), None, "tensor"),
        P("tensor", "seq"),
        P(("dp", "tensor"), "seq"),
        P("dp"),
    )
    return jax.shard_map(
        layer, mesh=mesh, in_specs=placed, out_specs=P(("dp", "tensor"), "seq"), check_vma=False
    )
```

time: 256 us -> 269 us (1.051); the launches traced: 251 us -> 268 us
  local copies, waits for them, and re-layouts: 31.1 us -> 50.8 us
  blocking collectives: 19.2 us -> 0 us
  Pallas kernels: 22.5 us -> 37.6 us
  waiting for transfers between devices: 133 us -> 126 us
  starting transfers between devices: 12.2 us -> 16.5 us
    all_gather x0 -> x1, local copies, waits for them, and re-layouts: none -> 22.6 us  [layer(): lax.all_gather(token_major, 'seq', axis=2, tiled=False)]
    all_to_all x1 -> x0, blocking collectives: 19.2 us -> none  [on_device(): lax.all_to_all(heads_out.reshape(n_ten, out_rows, HD), 'tensor', split_ax...]
    pallas_call x1 -> x4, Pallas kernels: 22.5 us -> 37.6 us  [flash(): pl.pallas_call(kernel, out_shape=jax.ShapeDtypeStruct((rows_out, HD), jnp...]
    all_gather x2, waiting for transfers between devices: 39.7 us -> 30.6 us  [the longest x1 28.8 us: layer(): pair_all = lax.all_gather(keys_values, 'seq', axis=0, tiled=True)]
    ppermute x3 -> x6, starting transfers between devices: 2.16 us -> 6.52 us  [the longest x3 3.73 us: layer(): lax.ppermute(out_weight, 'tensor', [(j, (j + shift) % n_ten) for j in ran...]
    gather x16 -> x13, local copies, waits for them, and re-layouts: 21.9 us -> 17.7 us  [block_starts(): jnp.searchsorted(segments, first_docs, side='left') // bk]
    ppermute x3 -> x6, waiting for transfers between devices: 93.1 us -> 95.6 us  [the longest x3 89.8 us: layer(): lax.ppermute(out_weight, 'tensor', [(j, (j + shift) % n_ten) for j in ran...]
    another operation x1 -> x2, other arithmetic: 4.43 us -> 5.91 us  [the longest x1 3.86 us: layer(): jnp.stack(received)]
  transfers between devices with their start and end apart: 6 -> 9, of which waited for: 4 -> 7; matrix products, arithmetic and copies ran while one was open for 13% -> 11% of each run, Pallas kernels for 0% -> 2%
where the time goes in v8:
time: 269 us; the launch traced here: 268 us
  waiting for transfers between devices  126 us (47%)
  local copies, waits for them, and re-layouts  50.8 us (19%)
  Pallas kernels  37.6 us (14%)
  starting transfers between devices  16.5 us (6%)
  matrix products  15.7 us (6%)
  between operations  13.5 us (5%)
  other arithmetic  6.81 us (3%)
    ppermute x3, waiting for transfers between devices, layer(): lax.ppermute(out_weight, 'tensor', [(j, (j + shift) % n_ten) for j in ran...  89.8 us
    pallas_call x4, Pallas kernels, flash(): pl.pallas_call(kernel, out_shape=jax.ShapeDtypeStruct((rows_out, HD), jnp...  37.6 us
    all_gather x1, waiting for transfers between devices, layer(): pair_all = lax.all_gather(keys_values, 'seq', axis=0, tiled=True)  28.8 us
    all_gather x1, local copies, waits for them, and re-layouts, layer(): lax.all_gather(token_major, 'seq', axis=2, tiled=False)  22.6 us
    gather x13, local copies, waits for them, and re-layouts, block_starts(): jnp.searchsorted(segments, first_docs, side='left') // bk  17.7 us
    dot_general x1, matrix products, layer(): jnp.dot(gathered, weight_all, preferred_element_type=jnp.float32)  15.7 us
    all_to_all x1, starting transfers between devices, layer(): lax.all_to_all(head_major, 'seq', split_axis=0, concat_axis=0, tiled=True)  9.97 us
    ppermute x3, waiting for transfers between devices, layer(): lax.ppermute(block, 'tensor', [(j, (j + shift) % n_ten) for j in range(n_...  5.82 us
  transfers between devices with their start and end apart: 9, of which 7 were waited for; matrix products, arithmetic and copies ran while one was open for 11% of the time, Pallas kernels for 2%

profile of v8, /device:TPU:1, one launch (start us, length us, event | category | flops | bytes accessed | tf_op | source)
XLA Modules:
  0.0 267.5 jit_solution(10480734789304254194)
XLA Ops:
  6.5 0.0 copy-start
  6.5 0.0 all-gather.4.cloned.1.call-start
  6.5 1.8 copy.9
  8.3 0.0 all-gather.4.cloned.1.call-update
  8.3 0.0 copy-done
  8.3 1.2 bitcast_bitcast_fusion
  9.6 10.0 %all-to-all-start = ((bf16[16,256,128]{2,1,0:T(8,128)(2,1)}), bf16[16,256,128]{2,1,0:T(8,128)(2,1)S(1)}, u32[]{:S(2)}, u32[]{:S(2)}) async-start(bf16[16,256,128]{2,1,0:T(8,128)(2,1)} %bitcast_bitcast_fusion), calls=%async_computation | async-start | bytes 2097152 | tf_op jit(solution)/shard_map/all_to_all | solution.py:97
  19.6 0.0 all-gather.6.cloned.1.call-start
  19.6 0.8 slice.9
  20.4 18.4 %while.24 = (s32[]{:T(128)}, u32[8]{0:T(128)S(1)}, u32[8]{0:T(128)S(1)}, s32[4096]{0:T(1024)}, s32[8]{0:T(128)S(1)}, /*index=5*/s32[]{:T(128)}, s32[]{:T(128)}, s32[]{}) while((s32[]{:T(128)}, u32[8]{0:T(128)S(1)}, u32[8]{0:T(128)S(1)}, s32[4096]{0:T(1024)}, s32[8]{0:T(128)S(1)}, /*index=5*/s32[]{:T(128)}, s32[]{:T(128)}, s32[]{}) %tuple.34), condition=%wide.region_1.2_spmd.clone, body=%wide.region_0.1_spmd.clone.sunk | while | flops 1132 | bytes 4620 | solution.py:54
  20.4 1.4 gather_fusion
  21.9 1.4 gather_fusion
  23.3 1.4 gather_fusion
  24.7 1.4 gather_fusion
  26.1 1.4 gather_fusion
  27.5 1.4 gather_fusion
  28.9 1.4 gather_fusion
  30.4 1.4 gather_fusion
  31.8 1.4 gather_fusion
  33.2 1.4 gather_fusion
  34.6 1.4 gather_fusion
  36.0 1.4 gather_fusion
  37.5 1.4 gather_fusion
  38.8 0.0 copy-start.2
  38.9 2.7 %copy.10.segq_ref = s32[4096,1]{1,0:T(8,128)} copy(s32[4096,1]{0,1:T(1,128)} %bitcast.30) | data formatting | bytes 32768 | tf_op jit(solution)/shard_map/reshape | solution.py:59
  41.6 0.5 and_select_fusion.starts_ref
  42.2 28.8 %all-gather.4.cloned.1.call-done = bf16[4096,2,256]{2,0,1:T(8,128)(2,1)} async-done(((bf16[256,2,256]{2,0,1:T(8,128)(2,1)}), bf16[4096,2,256]{2,0,1:T(8,128)(2,1)}) %all-gather.4.cloned.1.call-update) | async-done | bytes 4194320 | tf_op jit(solution)/shard_map/all_gather | solution.py:100
  70.9 3.1 %dynamic-slice_bitcast_fusion = (bf16[4096,128]{1,0:T(8,128)(2,1)}, bf16[4096,128]{1,0:T(8,128)(2,1)}) fusion(bf16[4096,2,256]{2,0,1:T(8,128)(2,1)} %all-gather.4.cloned.1.call-done, s32[]{:T(128)S(6)} %add.53, s32[]{:T(128)S(6)} %select_n.46), kind=kLoop, calls=%fused_computation.10 | loop fusion | bytes 4194312 | tf_op jit(solution)/shard_map/squeeze | solution.py:103
  74.0 0.0 all-to-all-done
  74.0 0.0 copy-start.3
  74.0 1.0 copy-done.3
  75.0 12.3 %shard_map.58 = bf16[1024,128]{1,0:T(8,128)(2,1)} custom-call(s32[8]{0:T(128)} %and_select_fusion.starts_ref, s32[1]{0:T(128)} %bitcast.12.offset_ref, bf16[4096,128]{1,0:T(8,128)(2,1)} %bitcast.35, bf16[4096,128]{1,0:T(8,128)(2,1)} %get-tuple-element.102.k_ref, bf16[4096,128]{1,0:T(8,128)(2,1)} %get-tuple-element.101.v_ref, s32[4096,1]{1,0:T(8,128)} %copy.10.segq_ref, ...), custom_call_target="tpu_custom_call" | custom-call | tf_op jit(solution)/shard_map/pallas_call | solution.py:63
  87.2 0.0 copy-start.5
  87.2 0.0 copy-done.2
  87.2 8.5 %shard_map.57 = bf16[1024,128]{1,0:T(8,128)(2,1)} custom-call(s32[8]{0:T(128)} %and_select_fusion.starts_ref, s32[1]{0:T(128)} %bitcast.10.offset_ref, bf16[4096,128]{1,0:T(8,128)(2,1)} %bitcast.36, bf16[4096,128]{1,0:T(8,128)(2,1)} %get-tuple-element.102.k_ref, bf16[4096,128]{1,0:T(8,128)(2,1)} %get-tuple-element.101.v_ref, s32[4096,1]{1,0:T(8,128)} %copy.10.segq_ref, ...), custom_call_target="tpu_custom_call" | custom-call | tf_op jit(solution)/shard_map/pallas_call | solution.py:63
  95.7 0.0 copy-start.4
  95.7 10.4 %shard_map.56 = bf16[1024,128]{1,0:T(8,128)(2,1)} custom-call(s32[8]{0:T(128)} %and_select_fusion.starts_ref, s32[1]{0:T(128)} %bitcast.8.offset_ref, bf16[4096,128]{1,0:T(8,128)(2,1)} %bitcast.37, bf16[4096,128]{1,0:T(8,128)(2,1)} %get-tuple-element.102.k_ref, bf16[4096,128]{1,0:T(8,128)(2,1)} %get-tuple-element.101.v_ref, s32[4096,1]{1,0:T(8,128)} %copy.10.segq_ref, ...), custom_call_target="tpu_custom_call" | custom-call | tf_op jit(solution)/shard_map/pallas_call | solution.py:63
  106.2 0.0 collective-permute-start
  106.2 0.7 collective-permute-start.1
  106.9 0.0 copy-done.5
  106.9 2.1 collective-permute-start.2
  109.0 6.4 %shard_map.55 = bf16[1024,128]{1,0:T(8,128)(2,1)} custom-call(s32[8]{0:T(128)} %and_select_fusion.starts_ref, s32[1]{0:T(128)} %bitcast.offset_ref, bf16[4096,128]{1,0:T(8,128)(2,1)} %bitcast.38, bf16[4096,128]{1,0:T(8,128)(2,1)} %get-tuple-element.102.k_ref, bf16[4096,128]{1,0:T(8,128)(2,1)} %get-tuple-element.101.v_ref, s32[4096,1]{1,0:T(8,128)} %copy.10.segq_ref, ...), custom_call_target="tpu_custom_call" | custom-call | tf_op jit(solution)/shard_map/pallas_call | solution.py:63
  115.3 5.4 %collective-permute-done = bf16[1024,128]{1,0:T(8,128)(2,1)S(1)} collective-permute-done((bf16[1024,128]{1,0:T(8,128)(2,1)}, bf16[1024,128]{1,0:T(8,128)(2,1)S(1)}, u32[]{:S(2)}, u32[]{:S(2)}) %collective-permute-start) | collective-permute-done | bytes 262176 | tf_op jit(solution)/shard_map/ppermute | solution.py:111
  120.8 0.0 collective-permute-done.1
  120.8 0.4 collective-permute-done.2
  121.2 2.1 pad_maximum_fusion.1
  123.2 0.0 all-gather.6.cloned.1.call-update
  123.2 0.0 copy-done.4
  123.2 1.0 collective-permute-start.3
  124.3 1.7 collective-permute-start.5
  126.0 1.0 collective-permute-start.4
  127.0 43.5 %collective-permute-done.3 = bf16[2048,512]{1,0:T(8,128)(2,1)S(1)} collective-permute-done((bf16[2048,512]{1,0:T(8,128)(2,1)S(1)}, bf16[2048,512]{1,0:T(8,128)(2,1)S(1)}, u32[]{:S(2)}, u32[]{:S(2)}) %collective-permute-start.3) | collective-permute-done | bytes 2097184 | tf_op jit(solution)/shard_map/ppermute | solution.py:92
  170.4 0.3 collective-permute-done.5
  170.8 46.0 %collective-permute-done.4 = bf16[2048,512]{1,0:T(8,128)(2,1)S(1)} collective-permute-done((bf16[2048,512]{1,0:T(8,128)(2,1)S(1)}, bf16[2048,512]{1,0:T(8,128)(2,1)S(1)}, u32[]{:S(2)}, u32[]{:S(2)}) %collective-permute-start.4) | collective-permute-done | bytes 2097184 | tf_op jit(solution)/shard_map/ppermute | solution.py:92
  216.8 3.9 %pad_maximum_fusion = bf16[4,2048,512]{2,1,0:T(8,128)(2,1)} fusion(bf16[1,2048,512]{2,1,0:T(8,128)(2,1)S(1)} %bitcast.43, bf16[1,2048,512]{2,1,0:T(8,128)(2,1)S(1)} %bitcast.44, bf16[1,2048,512]{2,1,0:T(8,128)(2,1)S(1)} %bitcast.42, bf16[1,2048,512]{2,1,0:T(8,128)(2,1)S(1)} %bitcast.41), kind=kLoop, calls=%fused_computation.7 | loop fusion | flops 12582912 | bytes 16777216 | tf_op jit(solution)/shard_map/stack | solution.py:95
  220.6 0.0 copy-start.6
  220.6 1.8 all-gather.6.cloned.1.call-done
  222.5 22.6 %copy.14 = bf16[1024,4,2048]{0,2,1:T(8,128)(2,1)} copy(bf16[1024,4,2048]{2,0,1:T(8,128)(2,1)} %all-gather.6.cloned.1.call-done) | data formatting | bytes 33554432 | tf_op jit(solution)/shard_map/all_gather | solution.py:114
  245.0 0.0 copy-done.6
  245.0 0.0 copy-start.1
  245.0 15.7 %add_convert_fusion = bf16[1024,512]{1,0:T(8,128)(2,1)} fusion(bf16[1024,512]{1,0:T(8,128)(2,1)S(1)} %copy-done.6, bf16[1024,8192]{0,1:T(8,128)(2,1)} %bitcast.39, bf16[8192,512]{1,0:T(8,128)(2,1)} %bitcast.40), kind=kOutput, calls=%fused_computation.8 | convolution fusion | flops 8591507456 | bytes 27262976 | tf_op jit(solution)/shard_map/dot_general | solution.py:115
  260.7 0.0 copy-done.1
  (41 shorter events, 0.4 us)
Async XLA Ops:
  6.5 1.8 copy-start
  6.5 64.4 %all-gather.4.cloned.1.call-start = ((), (), s32[]{:S(2)}) async-start(), calls=%async_computation.1 | async-start | bytes 4456448 | tf_op jit(solution)/shard_map/all_gather | solution.py:100
  9.6 64.4 %all-to-all-start = ((bf16[16,256,128]{2,1,0:T(8,128)(2,1)}), bf16[16,256,128]{2,1,0:T(8,128)(2,1)S(1)}, u32[]{:S(2)}, u32[]{:S(2)}) async-start(bf16[16,256,128]{2,1,0:T(8,128)(2,1)} %bitcast_bitcast_fusion), calls=%async_computation | async-start | bytes 2097152 | tf_op jit(solution)/shard_map/all_to_all | solution.py:97
  19.6 202.9 %all-gather.6.cloned.1.call-start = ((), (), s32[]{:S(2)}) async-start(), calls=%async_computation.2 | async-start | bytes 17825792 | tf_op jit(solution)/shard_map/all_gather | solution.py:114
  38.8 48.4 %copy-start.2 = (s32[4096]{0:T(1024)S(1)}, s32[4096]{0:T(1024)}, u32[]{:S(2)}) copy-start(s32[4096]{0:T(1024)} %get-tuple-element.164) | copy-start | bytes 49156
  74.0 1.0 copy-start.3
  87.2 19.7 %copy-start.5 = (bf16[1024,128]{1,0:T(8,128)(2,1)S(1)}, bf16[1024,128]{1,0:T(8,128)(2,1)}, u32[]{:S(2)}) copy-start(bf16[1024,128]{1,0:T(8,128)(2,1)} %shard_map.58) | copy-start | bytes 786436
  95.7 27.5 %copy-start.4 = (bf16[2048,512]{1,0:T(8,128)(2,1)S(1)}, bf16[2048,512]{1,0:T(8,128)(2,1)}, u32[]{:S(2)}) copy-start(bf16[2048,512]{1,0:T(8,128)(2,1)} %param.9) | copy-start | bytes 6291460
  106.2 14.6 %collective-permute-start = (bf16[1024,128]{1,0:T(8,128)(2,1)}, bf16[1024,128]{1,0:T(8,128)(2,1)S(1)}, u32[]{:S(2)}, u32[]{:S(2)}) collective-permute-start(bf16[1024,128]{1,0:T(8,128)(2,1)} %shard_map.56), channel_id=1, source_target_pairs={{0,1},{1,2},{2,3},{3,0},{4,5},{5,6},{6,7},{7,4},{8,9},{9,10},{10,1... | collective-permute-start | bytes 786440 | tf_op jit(solution)/shard_map/ppermute | solution.py:111
  106.2 14.6 %collective-permute-start.1 = (bf16[1024,128]{1,0:T(8,128)(2,1)}, bf16[1024,128]{1,0:T(8,128)(2,1)S(1)}, u32[]{:S(2)}, u32[]{:S(2)}) collective-permute-start(bf16[1024,128]{1,0:T(8,128)(2,1)} %shard_map.57), channel_id=1, source_target_pairs={{0,2},{1,3},{2,0},{3,1},{4,6},{5,7},{6,4},{7,5},{8,10},{9,11},{10,... | collective-permute-start | bytes 786440 | tf_op jit(solution)/shard_map/ppermute | solution.py:111
  106.9 14.3 %collective-permute-start.2 = (bf16[1024,128]{1,0:T(8,128)(2,1)S(1)}, bf16[1024,128]{1,0:T(8,128)(2,1)S(1)}, u32[]{:S(2)}, u32[]{:S(2)}) collective-permute-start(bf16[1024,128]{1,0:T(8,128)(2,1)S(1)} %copy-done.5), channel_id=1, source_target_pairs={{0,3},{1,0},{2,1},{3,2},{4,7},{5,4},{6,5},{7,6},{8,11},{9,8},{10,9... | collective-permute-start | bytes 786440 | tf_op jit(solution)/shard_map/ppermute | solution.py:111
  123.2 47.2 %collective-permute-start.3 = (bf16[2048,512]{1,0:T(8,128)(2,1)S(1)}, bf16[2048,512]{1,0:T(8,128)(2,1)S(1)}, u32[]{:S(2)}, u32[]{:S(2)}) collective-permute-start(bf16[2048,512]{1,0:T(8,128)(2,1)S(1)} %copy-done.4), channel_id=1, source_target_pairs={{0,1},{1,2},{2,3},{3,0},{4,5},{5,6},{6,7},{7,4},{8,9},{9,10},{10,1... | collective-permute-start | bytes 6291464 | tf_op jit(solution)/shard_map/ppermute | solution.py:92
  124.3 46.5 %collective-permute-start.5 = (bf16[2048,512]{1,0:T(8,128)(2,1)S(1)}, bf16[2048,512]{1,0:T(8,128)(2,1)S(1)}, u32[]{:S(2)}, u32[]{:S(2)}) collective-permute-start(bf16[2048,512]{1,0:T(8,128)(2,1)S(1)} %copy-done.4), channel_id=1, source_target_pairs={{0,3},{1,0},{2,1},{3,2},{4,7},{5,4},{6,5},{7,6},{8,11},{9,8},{10,9... | collective-permute-start | bytes 6291464 | tf_op jit(solution)/shard_map/ppermute | solution.py:92
  126.0 90.8 %collective-permute-start.4 = (bf16[2048,512]{1,0:T(8,128)(2,1)S(1)}, bf16[2048,512]{1,0:T(8,128)(2,1)S(1)}, u32[]{:S(2)}, u32[]{:S(2)}) collective-permute-start(bf16[2048,512]{1,0:T(8,128)(2,1)S(1)} %copy-done.4), channel_id=1, source_target_pairs={{0,2},{1,3},{2,0},{3,1},{4,6},{5,7},{6,4},{7,5},{8,10},{9,11},{10,... | collective-permute-start | bytes 6291464 | tf_op jit(solution)/shard_map/ppermute | solution.py:92
  220.6 24.4 %copy-start.6 = (bf16[1024,512]{1,0:T(8,128)(2,1)S(1)}, bf16[1024,512]{1,0:T(8,128)(2,1)}, u32[]{:S(2)}) copy-start(bf16[1024,512]{1,0:T(8,128)(2,1)} %param.10) | copy-start | bytes 3145732
  245.0 15.7 %copy-start.1 = (bf16[256,2048]{1,0:T(8,128)(2,1)S(1)}, bf16[256,2048]{1,0:T(8,128)(2,1)}, u32[]{:S(2)}) copy-start(bf16[256,2048]{1,0:T(8,128)(2,1)} %param.7) | copy-start | bytes 3145732
Sparse Core Ops, SparseCore 0:
  9.2 61.6 all-gather.3
  123.4 99.0 all-gather.5

commit v9 on v7

--- a/solution.py
+++ b/solution.py
@@ -1,7 +1,6 @@
 import functools
 import jax
 import jax.numpy as jnp
-import numpy as np
 from jax import lax
 from jax.experimental import pallas as pl
 from jax.experimental.pallas import tpu as pltpu
@@ -77,10 +76,13 @@
     )(starts, query_head, key_head, value_head, seg_col, seg_row)
 
 
-def on_device(queries, keys_values, out_weight, residual, segments):
-    n_seq = lax.axis_size("seq")
+def layer(queries, keys_values, out_weight, residual, segments):
+    n_core = lax.axis_size("core")
+    n_z = lax.axis_size("z")
+    n_seq = n_z * n_core
     n_ten = lax.axis_size("tensor")
-    seq_idx = lax.axis_index("seq")
+    core_idx = lax.axis_index("core")
+    seq_idx = lax.axis_index("z") * n_core + core_idx
     ten_idx = lax.axis_index("tensor")
     tok_dev = queries.shape[0]
     heads_ten = queries.shape[1] // HD
@@ -90,34 +92,49 @@
         lax.ppermute(out_weight, "tensor", [(j, (j + shift) % n_ten) for j in range(n_ten)])
         for shift in range(1, n_ten)
     ]
-    by_shift = jnp.stack(received).reshape(n_ten, n_seq, HD, out_weight.shape[1])
+    by_shift = jnp.stack(received)
     source = (ten_idx - jnp.arange(n_ten)) % n_ten
-    weight_all = jnp.transpose(jnp.take(by_shift, source, axis=0), (1, 0, 2, 3)).reshape(
-        n_ten * out_weight.shape[0], out_weight.shape[1]
-    )
+    weight_all = jnp.take(by_shift, source, axis=0).reshape(n_ten * out_weight.shape[0], out_weight.shape[1])
     head_major = jnp.transpose(queries.reshape(tok_dev, heads_ten, HD), (1, 0, 2))
-    query_parts = lax.all_to_all(head_major, "seq", split_axis=0, concat_axis=0, tiled=True)
+    query_parts = lax.all_to_all(head_major, ("z", "core"), split_axis=0, concat_axis=0, tiled=True)
     query_head = query_parts.reshape(n_seq * tok_dev, HD)
     assert query_head.shape[0] == L
-    pair_all = lax.all_gather(keys_values, "seq", axis=0, tiled=True)
+    pair_all = lax.all_gather(keys_values, ("z", "core"), axis=0, tiled=True)
     pair_head = lax.dynamic_slice_in_dim(pair_all, (seq_idx // group_size) * HD, HD, axis=2)
     heads_out = flash(query_head, pair_head[:, 0, :], pair_head[:, 1, :], segments)
     out_rows = heads_out.shape[0] // n_ten
     row_parts = lax.all_to_all(heads_out.reshape(n_ten, out_rows, HD), "tensor", split_axis=0, concat_axis=0, tiled=True)
     token_major = jnp.transpose(row_parts, (1, 0, 2))
-    gathered = lax.all_gather(token_major, "seq", axis=1, tiled=False).reshape(out_rows, n_seq * n_ten * HD)
-    projected = jnp.dot(gathered, weight_all, preferred_element_type=jnp.float32)
+    own = lax.all_gather(token_major, "z", axis=2, tiled=False)
+    sibling = lax.ppermute(own, "core", [(j, (j + 1) % n_core) for j in range(n_core)])
+    weight_parts = weight_all.reshape(n_ten, n_z, n_core, HD, weight_all.shape[1])
+    weight_own = lax.dynamic_index_in_dim(weight_parts, core_idx, axis=2, keepdims=False)
+    weight_sib = lax.dynamic_index_in_dim(weight_parts, (core_idx + 1) % n_core, axis=2, keepdims=False)
+    features = n_ten * n_z * HD
+    projected = jnp.dot(
+        own.reshape(out_rows, features), weight_own.reshape(features, -1), preferred_element_type=jnp.float32
+    ) + jnp.dot(
+        sibling.reshape(out_rows, features), weight_sib.reshape(features, -1), preferred_element_type=jnp.float32
+    )
     return (residual.astype(jnp.float32) + projected).astype(jnp.bfloat16)
 
 
 def solution(mesh):
+    n_dp, n_seq, n_ten = (mesh.shape[name] for name in ("dp", "seq", "tensor"))
+    sub_mesh = jax.sharding.Mesh(
+        mesh.devices.reshape(n_dp, n_seq // 2, 2, n_ten), ("dp", "z", "core", "tensor")
+    )
     placed = (
-        P(("dp", "seq"), "tensor"),
-        P(("dp", "seq"), None, "tensor"),
-        P("tensor", "seq"),
-        P(("dp", "tensor"), "seq"),
+        P(("dp", "z", "core"), "tensor"),
+        P(("dp", "z", "core"), None, "tensor"),
+        P("tensor", ("z", "core")),
+        P(("dp", "tensor"), ("z", "core")),
         P("dp"),
     )
     return jax.shard_map(
-        on_device, mesh=mesh, in_specs=placed, out_specs=P(("dp", "tensor"), "seq"), check_vma=False
+        layer,
+        mesh=sub_mesh,
+        in_specs=placed,
+        out_specs=P(("dp", "tensor"), ("z", "core")),
+        check_vma=False,
     )

time: 256 us -> 368 us (1.44); the launches traced: 251 us -> 368 us
  waiting for transfers between devices: 133 us -> 219 us
  other arithmetic: 5.32 us -> 19.5 us
  Pallas kernels: 22.5 us -> 28.4 us
  local copies, waits for them, and re-layouts: 31.1 us -> 36.6 us
    all_gather x2, waiting for transfers between devices: 39.7 us -> 130 us  [the longest x1 90 us: layer(): own = lax.all_gather(token_major, 'z', axis=2, tiled=False)]
    select_n x1 -> x2, other arithmetic: 0.01 us -> 7.49 us  [layer(): jnp.take(by_shift, source, axis=0)]
    unnamed x2 -> x3, other arithmetic: 0.01 us -> 7.26 us
    pallas_call x1, Pallas kernels: 22.5 us -> 28.4 us  [flash(): pl.pallas_call(kernel, out_shape=jax.ShapeDtypeStruct((rows, HD), jnp.bfl...]
    dynamic_slice x0 -> x1, local copies, waits for them, and re-layouts: none -> 4.08 us  [layer(): lax.dynamic_index_in_dim(weight_parts, (core_idx + 1) % n_core, axis=2, k...]
    ppermute x3 -> x4, waiting for transfers between devices: 93.1 us -> 89.5 us  [the longest x3 89.5 us: layer(): lax.ppermute(out_weight, 'tensor', [(j, (j + shift) % n_ten) for j in ran...]
    dot_general x1 -> x2, matrix products: 14.2 us -> 16 us  [the longest x1 8.97 us: layer(): jnp.dot(sibling.reshape(out_rows, features), weight_sib.reshape(features,...]
  transfers between devices with their start and end apart: 6 -> 7, of which waited for: 4 -> 4; matrix products, arithmetic and copies ran while one was open for 13% -> 16% of each run, Pallas kernels for 0% -> 0%
where the time goes in v9:
time: 368 us
  waiting for transfers between devices  219 us (60%)
  local copies, waits for them, and re-layouts  36.6 us (10%)
  Pallas kernels  28.4 us (8%)
  other arithmetic  19.5 us (5%)
  blocking collectives  18.5 us (5%)
  matrix products  16 us (4%)
  starting transfers between devices  15.6 us (4%)
  between operations  13.6 us (4%)
    all_gather x1, waiting for transfers between devices, layer(): own = lax.all_gather(token_major, 'z', axis=2, tiled=False)  90 us
    ppermute x3, waiting for transfers between devices, layer(): lax.ppermute(out_weight, 'tensor', [(j, (j + shift) % n_ten) for j in ran...  89.5 us
    all_gather x1, waiting for transfers between devices, layer(): pair_all = lax.all_gather(keys_values, ('z', 'core'), axis=0, tiled=True)  39.6 us
    pallas_call x1, Pallas kernels, flash(): pl.pallas_call(kernel, out_shape=jax.ShapeDtypeStruct((rows, HD), jnp.bfl...  28.4 us
    all_to_all x1, blocking collectives, layer(): lax.all_to_all(heads_out.reshape(n_ten, out_rows, HD), 'tensor', split_ax...  18.5 us
    gather x3, local copies, waits for them, and re-layouts, layer(): jnp.take(by_shift, source, axis=0)  13.5 us
    all_to_all x1, starting transfers between devices, layer(): lax.all_to_all(head_major, ('z', 'core'), split_axis=0, concat_axis=0, ti...  9.97 us
    dot_general x1, matrix products, layer(): jnp.dot(sibling.reshape(out_rows, features), weight_sib.reshape(features,...  8.97 us
  transfers between devices with their start and end apart: 7, of which 4 were waited for; matrix products, arithmetic and copies ran while one was open for 16% of the time, Pallas kernels for 0%

profile of v9, /device:TPU:1, one launch (start us, length us, event | category | flops | bytes accessed | tf_op | source)
XLA Modules:
  0.0 367.8 jit_solution(3646533414483984450)
XLA Ops:
  6.5 0.0 copy-start
  6.5 0.0 copy-start.2
  6.5 0.0 all-gather.4.cloned.1.call-start
  6.5 1.8 copy.9
  8.3 0.0 all-gather.4.cloned.1.call-update
  8.4 0.0 copy-done
  8.4 1.2 bitcast_bitcast_fusion
  9.6 10.0 %all-to-all-start = ((bf16[16,256,128]{2,1,0:T(8,128)(2,1)}), bf16[16,256,128]{2,1,0:T(8,128)(2,1)S(1)}, u32[]{:S(2)}, u32[]{:S(2)}) async-start(bf16[16,256,128]{2,1,0:T(8,128)(2,1)} %bitcast_bitcast_fusion), calls=%async_computation | async-start | bytes 2097152 | tf_op jit(solution)/shard_map/all_to_all | solution.py:99
  19.6 0.0 all-gather.6.cloned.1.call-start
  19.6 0.0 copy-done.2
  19.7 0.1 slice.9
  19.7 9.0 %while.24 = (s32[]{:T(128)}, u32[8]{0:T(128)S(1)}, u32[8]{0:T(128)S(1)}, s32[4096]{0:T(1024)S(1)}, s32[8]{0:T(128)S(1)}, /*index=5*/s32[]{:T(128)}, s32[]{:T(128)}, s32[]{}) while((s32[]{:T(128)}, u32[8]{0:T(128)S(1)}, u32[8]{0:T(128)S(1)}, s32[4096]{0:T(1024)S(1)}, s32[8]{0:T(128)S(1)}, /*index=5*/s32[]{:T(128)}, s32[]{:T(128)}, ...), condition=%wide.region_1.2_spmd.clone, body=%wide.region_0.1_spmd.clone.sunk | while | flops 1132 | bytes 4620 | solution.py:56
  19.8 0.6 gather_fusion
  20.5 0.6 gather_fusion
  21.2 0.6 gather_fusion
  21.8 0.6 gather_fusion
  22.5 0.6 gather_fusion
  23.2 0.6 gather_fusion
  23.9 0.6 gather_fusion
  24.6 0.6 gather_fusion
  25.3 0.6 gather_fusion
  26.0 0.6 gather_fusion
  26.7 0.6 gather_fusion
  27.4 0.6 gather_fusion
  28.1 0.6 gather_fusion
  28.8 2.0 copy.10.segq_ref
  30.8 0.5 and_select_fusion.2.starts_ref
  31.3 39.6 %all-gather.4.cloned.1.call-done = bf16[4096,2,256]{2,0,1:T(8,128)(2,1)} async-done(((bf16[256,2,256]{2,0,1:T(8,128)(2,1)}), bf16[4096,2,256]{2,0,1:T(8,128)(2,1)}) %all-gather.4.cloned.1.call-update) | async-done | bytes 4194320 | tf_op jit(solution)/shard_map/all_gather | solution.py:102
  70.9 3.0 dynamic-slice_bitcast_fusion
  74.0 0.0 all-to-all-done
  74.0 0.0 copy-start.3
  74.0 1.0 copy-done.3
  75.0 28.4 %shard_map.55 = bf16[4096,128]{1,0:T(8,128)(2,1)} custom-call(s32[8]{0:T(128)} %and_select_fusion.2.starts_ref, bf16[4096,128]{1,0:T(8,128)(2,1)} %bitcast.35, bf16[4096,128]{1,0:T(8,128)(2,1)} %get-tuple-element.106.k_ref, bf16[4096,128]{1,0:T(8,128)(2,1)} %get-tuple-element.105.v_ref, s32[4096,1]{1,0:T(8,128)} %copy.10.segq_ref, s32[1,4096]{1,0:T(1,128)S(1)} %bitcast.33), custom_call_target="tpu_custom_call" | custom-call | tf_op jit(solution)/shard_map/pallas_call | solution.py:60
  103.3 0.0 copy-start.4
  103.3 1.6 copy.11
  105.0 18.5 %all_to_all.10 = bf16[4,1024,128]{1,2,0:T(8,128)(2,1)} all-to-all(bf16[4,1024,128]{1,2,0:T(8,128)(2,1)S(1)} %copy.11), channel_id=1, replica_groups=mesh['dp'=4,'z'=8,'core'=2,'tensor'=4] {'tensor'}, dimensions={0} | all-to-all | bytes 2097152 | tf_op jit(solution)/shard_map/all_to_all | solution.py:106
  123.5 0.0 all-gather.6.cloned.1.call-update
  123.5 90.0 %all-gather.6.cloned.1.call-done = bf16[1024,4,1024]{0,2,1:T(8,128)(2,1)} async-done(((bf16[1024,4,128]{0,2,1:T(8,128)(2,1)}), bf16[1024,4,1024]{0,2,1:T(8,128)(2,1)}) %all-gather.6.cloned.1.call-update) | async-done | bytes 8388624 | tf_op jit(solution)/shard_map/all_gather | solution.py:108
  213.6 0.8 collective-permute-start.3
  214.4 0.0 copy-done.4
  214.4 1.2 collective-permute-start
  215.6 2.4 collective-permute-start.1
  218.0 1.2 collective-permute-start.2
  219.2 43.7 %collective-permute-done = bf16[2048,512]{1,0:T(8,128)(2,1)} collective-permute-done((bf16[2048,512]{1,0:T(8,128)(2,1)S(1)}, bf16[2048,512]{1,0:T(8,128)(2,1)}, u32[]{:S(2)}, u32[]{:S(2)}) %collective-permute-start) | collective-permute-done | bytes 2097184 | tf_op jit(solution)/shard_map/ppermute | solution.py:92
  262.9 45.9 %collective-permute-done.1 = bf16[2048,512]{1,0:T(8,128)(2,1)} collective-permute-done((bf16[2048,512]{1,0:T(8,128)(2,1)S(1)}, bf16[2048,512]{1,0:T(8,128)(2,1)}, u32[]{:S(2)}, u32[]{:S(2)}) %collective-permute-start.1) | collective-permute-done | bytes 2097184 | tf_op jit(solution)/shard_map/ppermute | solution.py:92
  308.8 0.0 collective-permute-done.2
  308.8 3.8 %pad_maximum_fusion = bf16[4,2048,512]{2,1,0:T(8,128)(2,1)S(1)} fusion(bf16[1,2048,512]{2,1,0:T(8,128)(2,1)} %bitcast.12, bf16[1,2048,512]{2,1,0:T(8,128)(2,1)} %bitcast.11, bf16[1,2048,512]{2,1,0:T(8,128)(2,1)} %bitcast.10, bf16[1,2048,512]{2,1,0:T(8,128)(2,1)S(1)} %bitcast.40), kind=kLoop, calls=%fused_computation.9 | loop fusion | flops 12582912 | bytes 16777216 | tf_op jit(solution)/shard_map/stack | solution.py:95
  312.6 3.6 fusion.3
  316.2 5.0 %gather_fusion.1 = bf16[4,1024,512]{2,1,0:T(8,128)(2,1)} fusion(bf16[4,1024,512]{2,1,0:T(8,128)(2,1)} %get-tuple-element.103, s32[1024]{0:T(1024)S(1)} %pad_clamp_fusion.1), kind=kCustom, calls=%fused_computation.1 | custom fusion | bytes 8388624 | tf_op jit(solution)/shard_map/jit(_take)/gather | solution.py:97
  321.2 4.9 %gather_fusion.2 = bf16[4,1024,512]{2,1,0:T(8,128)(2,1)} fusion(bf16[4,1024,512]{2,1,0:T(8,128)(2,1)} %get-tuple-element.104, s32[1024]{0:T(1024)S(1)} %pad_clamp_fusion.1), kind=kCustom, calls=%fused_computation.2 | custom fusion | bytes 8388624 | tf_op jit(solution)/shard_map/jit(_take)/gather | solution.py:97
  326.1 7.3 %pad_maximum_fusion.1 = bf16[4,2048,512]{2,1,0:T(8,128)(2,1)} fusion(bf16[4,1024,512]{2,1,0:T(8,128)(2,1)} %gather_fusion.2, bf16[4,1024,512]{2,1,0:T(8,128)(2,1)} %gather_fusion.1), kind=kLoop, calls=%fused_computation.10 | loop fusion | flops 16777216 | bytes 16777216
  333.4 7.5 %broadcast_select_fusion.2 = bf16[4,8,2,128,512]{4,3,2,1,0:T(8,128)(2,1)} fusion(bf16[4,8,2,128,512]{4,3,2,1,0:T(8,128)(2,1)} %bitcast.34, pred[4]{0:T(512)(128)(4,1)S(1)} %compare_and_fusion), kind=kLoop, calls=%fused_computation.11 | loop fusion | flops 4194304 | bytes 16777220 | tf_op jit(solution)/shard_map/jit(_take)/select_n | solution.py:97
  340.8 4.1 %constant_dynamic-slice_fusion = (bf16[4,8,1,128,512]{4,3,2,1,0:T(8,128)(2,1)S(1)}, bf16[4,8,1,128,512]{4,3,2,1,0:T(8,128)(2,1)S(1)}) fusion(bf16[4,8,2,128,512]{4,3,2,1,0:T(8,128)(2,1)} %broadcast_select_fusion.2, s32[]{:T(128)S(6)} %select_n.86, s32[]{:T(128)S(6)} %select_n.84), kind=kLoop, calls=%fused_computation.30 | loop fusion | bytes 16777224 | tf_op jit(solution)/shard_map/jit(dynamic_index_in_dim)/dynamic_slice | solution.py:112
  344.9 0.0 copy-start.5
  344.9 7.0 %fusion.4 = f32[1024,512]{1,0:T(8,128)S(1)} fusion(bf16[1024,4096]{0,1:T(8,128)(2,1)} %bitcast.42, bf16[4096,512]{1,0:T(8,128)(2,1)S(1)} %bitcast.39), kind=kOutput, calls=%fused_computation.36 | convolution fusion | flops 4294967296 | bytes 14680064 | tf_op jit(solution)/shard_map/dot_general | solution.py:114
  351.9 0.0 collective-permute-done.3
  351.9 0.0 copy-done.5
  352.0 0.0 copy-start.1
  352.0 9.0 %add_convert_fusion = bf16[1024,512]{1,0:T(8,128)(2,1)} fusion(f32[1024,512]{1,0:T(8,128)S(1)} %fusion.4, bf16[1024,512]{1,0:T(8,128)(2,1)S(1)} %copy-done.5, bf16[1024,4096]{0,1:T(8,128)(2,1)} %bitcast.17, bf16[4096,512]{1,0:T(8,128)(2,1)S(1)} %bitcast.38), kind=kOutput, calls=%fused_computation.12 | convolution fusion | flops 4297064448 | bytes 16777216 | tf_op jit(solution)/shard_map/dot_general | solution.py:116
  360.9 0.0 copy-done.1
  (44 shorter events, 0.4 us)
Async XLA Ops:
  6.5 1.8 copy-start
  6.5 13.1 %copy-start.2 = (s32[4096]{0:T(1024)S(1)}, s32[4096]{0:T(1024)}, u32[]{:S(2)}) copy-start(s32[4096]{0:T(1024)} %param.11) | copy-start | bytes 49156
  6.5 64.4 %all-gather.4.cloned.1.call-start = ((), (), s32[]{:S(2)}) async-start(), calls=%async_computation.2 | async-start | bytes 4456448 | tf_op jit(solution)/shard_map/all_gather | solution.py:102
  9.6 64.4 %all-to-all-start = ((bf16[16,256,128]{2,1,0:T(8,128)(2,1)}), bf16[16,256,128]{2,1,0:T(8,128)(2,1)S(1)}, u32[]{:S(2)}, u32[]{:S(2)}) async-start(bf16[16,256,128]{2,1,0:T(8,128)(2,1)} %bitcast_bitcast_fusion), calls=%async_computation | async-start | bytes 2097152 | tf_op jit(solution)/shard_map/all_to_all | solution.py:99
  19.6 194.0 %all-gather.6.cloned.1.call-start = ((), (), s32[]{:S(2)}) async-start(), calls=%async_computation.3 | async-start | bytes 9437184 | tf_op jit(solution)/shard_map/all_gather | solution.py:108
  74.0 1.0 copy-start.3
  103.3 111.1 %copy-start.4 = (bf16[2048,512]{1,0:T(8,128)(2,1)S(1)}, bf16[2048,512]{1,0:T(8,128)(2,1)}, u32[]{:S(2)}) copy-start(bf16[2048,512]{1,0:T(8,128)(2,1)} %param.9) | copy-start | bytes 6291460
  213.6 138.4 %collective-permute-start.3 = (bf16[1024,4,8,128]{0,3,2,1:T(8,128)(2,1)}, bf16[1024,4,8,128]{0,3,2,1:T(8,128)(2,1)}, u32[]{:S(2)}, u32[]{:S(2)}) collective-permute-start(bf16[1024,4,8,128]{0,3,2,1:T(8,128)(2,1)} %bitcast.41), channel_id=1, source_target_pairs={{0,4},{4,0},{1,5},{5,1},{2,6},{6,2},{3,7},{7,3},{8,12},{12,8},{9,1... | collective-permute-start | bytes 25165832 | tf_op jit(solution)/shard_map/ppermute | solution.py:109
  214.4 48.5 %collective-permute-start = (bf16[2048,512]{1,0:T(8,128)(2,1)S(1)}, bf16[2048,512]{1,0:T(8,128)(2,1)}, u32[]{:S(2)}, u32[]{:S(2)}) collective-permute-start(bf16[2048,512]{1,0:T(8,128)(2,1)S(1)} %copy-done.4), channel_id=1, source_target_pairs={{0,1},{1,2},{2,3},{3,0},{4,5},{5,6},{6,7},{7,4},{8,9},{9,10},{10,1... | collective-permute-start | bytes 6291464 | tf_op jit(solution)/shard_map/ppermute | solution.py:92
  215.6 93.2 %collective-permute-start.1 = (bf16[2048,512]{1,0:T(8,128)(2,1)S(1)}, bf16[2048,512]{1,0:T(8,128)(2,1)}, u32[]{:S(2)}, u32[]{:S(2)}) collective-permute-start(bf16[2048,512]{1,0:T(8,128)(2,1)S(1)} %copy-done.4), channel_id=1, source_target_pairs={{0,2},{1,3},{2,0},{3,1},{4,6},{5,7},{6,4},{7,5},{8,10},{9,11},{10,... | collective-permute-start | bytes 6291464 | tf_op jit(solution)/shard_map/ppermute | solution.py:92
  218.0 90.8 %collective-permute-start.2 = (bf16[2048,512]{1,0:T(8,128)(2,1)S(1)}, bf16[2048,512]{1,0:T(8,128)(2,1)}, u32[]{:S(2)}, u32[]{:S(2)}) collective-permute-start(bf16[2048,512]{1,0:T(8,128)(2,1)S(1)} %copy-done.4), channel_id=1, source_target_pairs={{0,3},{1,0},{2,1},{3,2},{4,7},{5,4},{6,5},{7,6},{8,11},{9,8},{10,9... | collective-permute-start | bytes 6291464 | tf_op jit(solution)/shard_map/ppermute | solution.py:92
  344.9 7.0 %copy-start.5 = (bf16[1024,512]{1,0:T(8,128)(2,1)S(1)}, bf16[1024,512]{1,0:T(8,128)(2,1)}, u32[]{:S(2)}) copy-start(bf16[1024,512]{1,0:T(8,128)(2,1)} %param.10) | copy-start | bytes 3145732
  352.0 9.0 %copy-start.1 = (bf16[256,2048]{1,0:T(8,128)(2,1)S(1)}, bf16[256,2048]{1,0:T(8,128)(2,1)}, u32[]{:S(2)}) copy-start(bf16[256,2048]{1,0:T(8,128)(2,1)} %param.7) | copy-start | bytes 3145732
Sparse Core Ops, SparseCore 0:
  9.2 61.7 all-gather.3
  123.6 89.8 all-gather.5

commit v10 on v7

--- a/solution.py
+++ b/solution.py
@@ -1,7 +1,6 @@
 import functools
 import jax
 import jax.numpy as jnp
-import numpy as np
 from jax import lax
 from jax.experimental import pallas as pl
 from jax.experimental.pallas import tpu as pltpu
@@ -50,7 +49,7 @@
     o_ref[...] = (acc_fin / l_fin).astype(o_ref.dtype)
 
 
-def flash(query_head, key_head, value_head, segments, bq=512, bk=512):
+def flash(query_head, key_head, value_head, segments, bq=512, bk=1024):
     rows = query_head.shape[0]
     n_q = rows // bq
     first_docs = segments[::bq]
@@ -77,7 +76,7 @@
     )(starts, query_head, key_head, value_head, seg_col, seg_row)
 
 
-def on_device(queries, keys_values, out_weight, residual, segments):
+def layer(queries, keys_values, out_weight, residual, segments):
     n_seq = lax.axis_size("seq")
     n_ten = lax.axis_size("tensor")
     seq_idx = lax.axis_index("seq")
@@ -90,11 +89,9 @@
         lax.ppermute(out_weight, "tensor", [(j, (j + shift) % n_ten) for j in range(n_ten)])
         for shift in range(1, n_ten)
     ]
-    by_shift = jnp.stack(received).reshape(n_ten, n_seq, HD, out_weight.shape[1])
+    by_shift = jnp.stack(received)
     source = (ten_idx - jnp.arange(n_ten)) % n_ten
-    weight_all = jnp.transpose(jnp.take(by_shift, source, axis=0), (1, 0, 2, 3)).reshape(
-        n_ten * out_weight.shape[0], out_weight.shape[1]
-    )
+    weight_all = jnp.take(by_shift, source, axis=0).reshape(n_ten * out_weight.shape[0], out_weight.shape[1])
     head_major = jnp.transpose(queries.reshape(tok_dev, heads_ten, HD), (1, 0, 2))
     query_parts = lax.all_to_all(head_major, "seq", split_axis=0, concat_axis=0, tiled=True)
     query_head = query_parts.reshape(n_seq * tok_dev, HD)
@@ -105,7 +102,7 @@
     out_rows = heads_out.shape[0] // n_ten
     row_parts = lax.all_to_all(heads_out.reshape(n_ten, out_rows, HD), "tensor", split_axis=0, concat_axis=0, tiled=True)
     token_major = jnp.transpose(row_parts, (1, 0, 2))
-    gathered = lax.all_gather(token_major, "seq", axis=1, tiled=False).reshape(out_rows, n_seq * n_ten * HD)
+    gathered = lax.all_gather(token_major, "seq", axis=2, tiled=False).reshape(out_rows, n_ten * n_seq * HD)
     projected = jnp.dot(gathered, weight_all, preferred_element_type=jnp.float32)
     return (residual.astype(jnp.float32) + projected).astype(jnp.bfloat16)
 
@@ -118,6 +115,4 @@
         P(("dp", "tensor"), "seq"),
         P("dp"),
     )
-    return jax.shard_map(
-        on_device, mesh=mesh, in_specs=placed, out_specs=P(("dp", "tensor"), "seq"), check_vma=False
-    )
+    return jax.shard_map(layer, mesh=mesh, in_specs=placed, out_specs=P(("dp", "tensor"), "seq"), check_vma=False)

time: 256 us -> 270 us (1.055); the launches traced: 251 us -> 269 us
  Pallas kernels: 22.5 us -> 31.4 us
  other arithmetic: 5.32 us -> 12.8 us
    pallas_call x1, Pallas kernels: 22.5 us -> 31.4 us  [flash(): pl.pallas_call(kernel, out_shape=jax.ShapeDtypeStruct((rows, HD), jnp.bfl...]
    select_n x1 -> x2, other arithmetic: 0.01 us -> 8.01 us  [layer(): jnp.take(by_shift, source, axis=0)]
  transfers between devices with their start and end apart: 6 -> 6, of which waited for: 4 -> 4; matrix products, arithmetic and copies ran while one was open for 13% -> 15% of each run, Pallas kernels for 0% -> 0%
where the time goes in v10:
time: 270 us; the launch traced here: 269 us
  waiting for transfers between devices  132 us (49%)
  local copies, waits for them, and re-layouts  32.5 us (12%)
  Pallas kernels  31.4 us (12%)
  blocking collectives  18.5 us (7%)
  matrix products  15.7 us (6%)
  between operations  13.5 us (5%)
  other arithmetic  12.8 us (5%)
  starting transfers between devices  12.2 us (5%)
    ppermute x3, waiting for transfers between devices, layer(): lax.ppermute(out_weight, 'tensor', [(j, (j + shift) % n_ten) for j in ran...  92.9 us
    all_gather x1, waiting for transfers between devices, layer(): pair_all = lax.all_gather(keys_values, 'seq', axis=0, tiled=True)  39.6 us
    pallas_call x1, Pallas kernels, flash(): pl.pallas_call(kernel, out_shape=jax.ShapeDtypeStruct((rows, HD), jnp.bfl...  31.4 us
    all_to_all x1, blocking collectives, layer(): lax.all_to_all(heads_out.reshape(n_ten, out_rows, HD), 'tensor', split_ax...  18.5 us
    dot_general x1, matrix products, layer(): jnp.dot(gathered, weight_all, preferred_element_type=jnp.float32)  15.7 us
    gather x3, local copies, waits for them, and re-layouts, layer(): jnp.take(by_shift, source, axis=0)  13.5 us
    all_to_all x1, starting transfers between devices, layer(): lax.all_to_all(head_major, 'seq', split_axis=0, concat_axis=0, tiled=True)  9.97 us
    gather x13, local copies, waits for them, and re-layouts, flash(): jnp.searchsorted(segments, first_docs, side='left') // bk  8.27 us
  transfers between devices with their start and end apart: 6, of which 4 were waited for; matrix products, arithmetic and copies ran while one was open for 15% of the time, Pallas kernels for 0%

profile of v10, /device:TPU:1, one launch (start us, length us, event | category | flops | bytes accessed | tf_op | source)
XLA Modules:
  0.0 269.4 jit_solution(12663990859727849172)
XLA Ops:
  6.5 0.0 copy-start
  6.5 0.0 copy-start.2
  6.5 0.0 all-gather.4.cloned.1.call-start
  6.5 1.8 copy.9
  8.3 0.0 all-gather.4.cloned.1.call-update
  8.4 0.0 copy-done
  8.4 1.2 bitcast_bitcast_fusion
  9.6 10.0 %all-to-all-start = ((bf16[16,256,128]{2,1,0:T(8,128)(2,1)}), bf16[16,256,128]{2,1,0:T(8,128)(2,1)S(1)}, u32[]{:S(2)}, u32[]{:S(2)}) async-start(bf16[16,256,128]{2,1,0:T(8,128)(2,1)} %bitcast_bitcast_fusion), calls=%async_computation | async-start | bytes 2097152 | tf_op jit(solution)/shard_map/all_to_all | solution.py:96
  19.6 0.0 all-gather.6.cloned.1.call-start
  19.6 0.0 copy-done.2
  19.6 0.1 slice.9
  19.7 9.0 %while.24 = (s32[]{:T(128)}, u32[8]{0:T(128)S(1)}, u32[8]{0:T(128)S(1)}, s32[4096]{0:T(1024)S(1)}, s32[8]{0:T(128)S(1)}, /*index=5*/s32[]{:T(128)}, s32[]{:T(128)}, s32[]{}) while((s32[]{:T(128)}, u32[8]{0:T(128)S(1)}, u32[8]{0:T(128)S(1)}, s32[4096]{0:T(1024)S(1)}, s32[8]{0:T(128)S(1)}, /*index=5*/s32[]{:T(128)}, s32[]{:T(128)}, ...), condition=%wide.region_1.2_spmd.clone, body=%wide.region_0.1_spmd.clone.sunk | while | flops 1132 | bytes 4628 | solution.py:56
  19.8 0.6 gather_fusion
  20.5 0.6 gather_fusion
  21.1 0.6 gather_fusion
  21.8 0.6 gather_fusion
  22.5 0.6 gather_fusion
  23.2 0.6 gather_fusion
  23.9 0.6 gather_fusion
  24.6 0.6 gather_fusion
  25.3 0.6 gather_fusion
  26.0 0.6 gather_fusion
  26.7 0.6 gather_fusion
  27.4 0.6 gather_fusion
  28.1 0.6 gather_fusion
  28.8 2.0 copy.10.segq_ref
  30.8 0.6 and_select_fusion.2.starts_ref
  31.4 39.6 %all-gather.4.cloned.1.call-done = bf16[4096,2,256]{2,0,1:T(8,128)(2,1)} async-done(((bf16[256,2,256]{2,0,1:T(8,128)(2,1)}), bf16[4096,2,256]{2,0,1:T(8,128)(2,1)}) %all-gather.4.cloned.1.call-update) | async-done | bytes 4194320 | tf_op jit(solution)/shard_map/all_gather | solution.py:99
  70.9 3.0 %dynamic-slice_bitcast_fusion = (bf16[4096,128]{1,0:T(8,128)(2,1)}, bf16[4096,128]{1,0:T(8,128)(2,1)}) fusion(bf16[4096,2,256]{2,0,1:T(8,128)(2,1)} %all-gather.4.cloned.1.call-done, s32[]{:T(128)S(6)} %add.60, s32[]{:T(128)S(6)} %select_n.74), kind=kLoop, calls=%fused_computation.13 | loop fusion | bytes 4194312 | tf_op jit(solution)/shard_map/squeeze | solution.py:101
  74.0 0.0 all-to-all-done
  74.0 0.0 copy-start.3
  74.0 1.0 copy-done.3
  74.9 31.4 %shard_map.55 = bf16[4096,128]{1,0:T(8,128)(2,1)} custom-call(s32[8]{0:T(128)} %and_select_fusion.2.starts_ref, bf16[4096,128]{1,0:T(8,128)(2,1)} %bitcast.29, bf16[4096,128]{1,0:T(8,128)(2,1)} %get-tuple-element.104.k_ref, bf16[4096,128]{1,0:T(8,128)(2,1)} %get-tuple-element.103.v_ref, s32[4096,1]{1,0:T(8,128)} %copy.10.segq_ref, s32[1,4096]{1,0:T(1,128)S(1)} %bitcast.27), custom_call_target="tpu_custom_call" | custom-call | tf_op jit(solution)/shard_map/pallas_call | solution.py:60
  106.4 0.0 copy-start.4
  106.4 1.6 copy.11
  108.0 18.5 %all_to_all.10 = bf16[4,1024,128]{1,2,0:T(8,128)(2,1)} all-to-all(bf16[4,1024,128]{1,2,0:T(8,128)(2,1)S(1)} %copy.11), channel_id=1, replica_groups=mesh['dp'=4,'seq'=16,'tensor'=4] {'tensor'}, dimensions={0} | all-to-all | bytes 2097152 | tf_op jit(solution)/shard_map/all_to_all | solution.py:103
  126.5 0.0 all-gather.6.cloned.1.call-update
  126.5 0.0 copy-done.4
  126.5 1.0 collective-permute-start.2
  127.5 1.2 collective-permute-start.1
  128.7 0.0 collective-permute-start
  128.7 43.7 %collective-permute-done.2 = bf16[2048,512]{1,0:T(8,128)(2,1)} collective-permute-done((bf16[2048,512]{1,0:T(8,128)(2,1)S(1)}, bf16[2048,512]{1,0:T(8,128)(2,1)}, u32[]{:S(2)}, u32[]{:S(2)}) %collective-permute-start.2) | collective-permute-done | bytes 2097184 | tf_op jit(solution)/shard_map/ppermute | solution.py:89
  172.5 2.2 collective-permute-done.1
  174.6 47.0 %collective-permute-done = bf16[2048,512]{1,0:T(8,128)(2,1)} collective-permute-done((bf16[2048,512]{1,0:T(8,128)(2,1)S(1)}, bf16[2048,512]{1,0:T(8,128)(2,1)}, u32[]{:S(2)}, u32[]{:S(2)}) %collective-permute-start) | collective-permute-done | bytes 2097184 | tf_op jit(solution)/shard_map/ppermute | solution.py:89
  221.6 3.8 %pad_maximum_fusion = bf16[4,2048,512]{2,1,0:T(8,128)(2,1)S(1)} fusion(bf16[1,2048,512]{2,1,0:T(8,128)(2,1)} %bitcast.12, bf16[1,2048,512]{2,1,0:T(8,128)(2,1)} %bitcast.11, bf16[1,2048,512]{2,1,0:T(8,128)(2,1)} %bitcast.10, bf16[1,2048,512]{2,1,0:T(8,128)(2,1)S(1)} %bitcast.32), kind=kLoop, calls=%fused_computation.9 | loop fusion | flops 12582912 | bytes 16777216 | tf_op jit(solution)/shard_map/stack | solution.py:92
  225.4 3.5 %fusion.3 = (bf16[4,1024,512]{2,1,0:T(8,128)(2,1)}, bf16[4,1024,512]{2,1,0:T(8,128)(2,1)}) fusion(bf16[4,2048,512]{2,1,0:T(8,128)(2,1)S(1)} %pad_maximum_fusion), kind=kLoop, calls=%fused_computation.32 | loop fusion | bytes 16777216 | tf_op jit(solution)/shard_map/jit(_take)/gather | solution.py:94
  229.0 5.0 %gather_fusion.2 = bf16[4,1024,512]{2,1,0:T(8,128)(2,1)} fusion(bf16[4,1024,512]{2,1,0:T(8,128)(2,1)} %get-tuple-element.102, s32[1024]{0:T(1024)S(1)} %pad_clamp_fusion.1), kind=kCustom, calls=%fused_computation.2 | custom fusion | bytes 8388624 | tf_op jit(solution)/shard_map/jit(_take)/gather | solution.py:94
  234.0 4.9 %gather_fusion.1 = bf16[4,1024,512]{2,1,0:T(8,128)(2,1)} fusion(bf16[4,1024,512]{2,1,0:T(8,128)(2,1)} %get-tuple-element.101, s32[1024]{0:T(1024)S(1)} %pad_clamp_fusion.1), kind=kCustom, calls=%fused_computation.1 | custom fusion | bytes 8388624 | tf_op jit(solution)/shard_map/jit(_take)/gather | solution.py:94
  238.9 0.0 copy-start.5
  238.9 8.0 %maximum_select_fusion = bf16[4,2048,512]{2,1,0:T(8,128)(2,1)} fusion(bf16[4,1024,512]{2,1,0:T(8,128)(2,1)} %gather_fusion.2, bf16[4,1024,512]{2,1,0:T(8,128)(2,1)} %gather_fusion.1, pred[4]{0:T(512)(128)(4,1)S(1)} %compare_and_fusion), kind=kLoop, calls=%fused_computation.10 | loop fusion | flops 20971520 | bytes 16777220 | tf_op jit(solution)/shard_map/jit(_take)/select_n | solution.py:94
  246.9 0.0 all-gather.6.cloned.1.call-done
  246.9 0.0 copy-done.5
  246.9 0.0 copy-start.1
  246.9 15.7 %add_convert_fusion = bf16[1024,512]{1,0:T(8,128)(2,1)} fusion(bf16[1024,512]{1,0:T(8,128)(2,1)S(1)} %copy-done.5, bf16[1024,8192]{0,1:T(8,128)(2,1)} %bitcast.33, bf16[8192,512]{1,0:T(8,128)(2,1)} %bitcast.28), kind=kOutput, calls=%fused_computation.11 | convolution fusion | flops 8591507456 | bytes 27262976 | tf_op jit(solution)/shard_map/dot_general | solution.py:106
  262.6 0.0 copy-done.1
  (44 shorter events, 0.4 us)
Async XLA Ops:
  6.5 1.8 copy-start
  6.5 13.1 %copy-start.2 = (s32[4096]{0:T(1024)S(1)}, s32[4096]{0:T(1024)}, u32[]{:S(2)}) copy-start(s32[4096]{0:T(1024)} %param.11) | copy-start | bytes 49156
  6.5 64.4 %all-gather.4.cloned.1.call-start = ((), (), s32[]{:S(2)}) async-start(), calls=%async_computation.2 | async-start | bytes 4456448 | tf_op jit(solution)/shard_map/all_gather | solution.py:99
  9.6 64.4 %all-to-all-start = ((bf16[16,256,128]{2,1,0:T(8,128)(2,1)}), bf16[16,256,128]{2,1,0:T(8,128)(2,1)S(1)}, u32[]{:S(2)}, u32[]{:S(2)}) async-start(bf16[16,256,128]{2,1,0:T(8,128)(2,1)} %bitcast_bitcast_fusion), calls=%async_computation | async-start | bytes 2097152 | tf_op jit(solution)/shard_map/all_to_all | solution.py:96
  19.6 227.3 %all-gather.6.cloned.1.call-start = ((), (), s32[]{:S(2)}) async-start(), calls=%async_computation.3 | async-start | bytes 17825792 | tf_op jit(solution)/shard_map/all_gather | solution.py:105
  74.0 1.0 copy-start.3
  106.4 20.2 %copy-start.4 = (bf16[2048,512]{1,0:T(8,128)(2,1)S(1)}, bf16[2048,512]{1,0:T(8,128)(2,1)}, u32[]{:S(2)}) copy-start(bf16[2048,512]{1,0:T(8,128)(2,1)} %param.9) | copy-start | bytes 6291460
  126.5 45.9 %collective-permute-start.2 = (bf16[2048,512]{1,0:T(8,128)(2,1)S(1)}, bf16[2048,512]{1,0:T(8,128)(2,1)}, u32[]{:S(2)}, u32[]{:S(2)}) collective-permute-start(bf16[2048,512]{1,0:T(8,128)(2,1)S(1)} %copy-done.4), channel_id=1, source_target_pairs={{0,3},{1,0},{2,1},{3,2},{4,7},{5,4},{6,5},{7,6},{8,11},{9,8},{10,9... | collective-permute-start | bytes 6291464 | tf_op jit(solution)/shard_map/ppermute | solution.py:89
  127.5 47.1 %collective-permute-start.1 = (bf16[2048,512]{1,0:T(8,128)(2,1)S(1)}, bf16[2048,512]{1,0:T(8,128)(2,1)}, u32[]{:S(2)}, u32[]{:S(2)}) collective-permute-start(bf16[2048,512]{1,0:T(8,128)(2,1)S(1)} %copy-done.4), channel_id=1, source_target_pairs={{0,2},{1,3},{2,0},{3,1},{4,6},{5,7},{6,4},{7,5},{8,10},{9,11},{10,... | collective-permute-start | bytes 6291464 | tf_op jit(solution)/shard_map/ppermute | solution.py:89
  128.7 92.9 %collective-permute-start = (bf16[2048,512]{1,0:T(8,128)(2,1)S(1)}, bf16[2048,512]{1,0:T(8,128)(2,1)}, u32[]{:S(2)}, u32[]{:S(2)}) collective-permute-start(bf16[2048,512]{1,0:T(8,128)(2,1)S(1)} %copy-done.4), channel_id=1, source_target_pairs={{0,1},{1,2},{2,3},{3,0},{4,5},{5,6},{6,7},{7,4},{8,9},{9,10},{10,1... | collective-permute-start | bytes 6291464 | tf_op jit(solution)/shard_map/ppermute | solution.py:89
  238.9 8.0 %copy-start.5 = (bf16[1024,512]{1,0:T(8,128)(2,1)S(1)}, bf16[1024,512]{1,0:T(8,128)(2,1)}, u32[]{:S(2)}) copy-start(bf16[1024,512]{1,0:T(8,128)(2,1)} %param.10) | copy-start | bytes 3145732
  246.9 15.7 %copy-start.1 = (bf16[256,2048]{1,0:T(8,128)(2,1)S(1)}, bf16[256,2048]{1,0:T(8,128)(2,1)}, u32[]{:S(2)}) copy-start(bf16[256,2048]{1,0:T(8,128)(2,1)} %param.7) | copy-start | bytes 3145732
Sparse Core Ops, SparseCore 0:
  9.2 61.7 all-gather.3
  126.6 93.7 all-gather.5

commit v11 on v10

--- a/solution.py
+++ b/solution.py
@@ -12,7 +12,7 @@
 L = 4096
 
 
-def flash_kernel(starts_ref, q_ref, k_ref, v_ref, segq_ref, segk_ref, o_ref, *, bq, bk):
+def flash_kernel(starts_ref, head_ref, q_ref, k_ref, v_ref, segq_ref, segk_ref, o_ref, *, bq, bk):
     qi = pl.program_id(0)
     q = q_ref[...]
     seg_q = segq_ref[...]
@@ -49,7 +49,7 @@
     o_ref[...] = (acc_fin / l_fin).astype(o_ref.dtype)
 
 
-def flash(query_head, key_head, value_head, segments, bq=512, bk=1024):
+def flash(query_head, pair_all, kv_head, segments, bq=512, bk=512):
     rows = query_head.shape[0]
     n_q = rows // bq
     first_docs = segments[::bq]
@@ -61,19 +61,19 @@
         kernel,
         out_shape=jax.ShapeDtypeStruct((rows, HD), jnp.bfloat16),
         grid_spec=pltpu.PrefetchScalarGridSpec(
-            num_scalar_prefetch=1,
+            num_scalar_prefetch=2,
             grid=(n_q,),
             in_specs=[
-                pl.BlockSpec((bq, HD), lambda i, s: (i, 0)),
-                pl.BlockSpec((rows, HD), lambda i, s: (0, 0)),
-                pl.BlockSpec((rows, HD), lambda i, s: (0, 0)),
-                pl.BlockSpec((bq, 1), lambda i, s: (i, 0)),
-                pl.BlockSpec((1, rows), lambda i, s: (0, 0)),
+                pl.BlockSpec((bq, HD), lambda i, s, h: (i, 0)),
+                pl.BlockSpec((None, rows, HD), lambda i, s, h: (0, 0, h[0])),
+                pl.BlockSpec((None, rows, HD), lambda i, s, h: (1, 0, h[0])),
+                pl.BlockSpec((bq, 1), lambda i, s, h: (i, 0)),
+                pl.BlockSpec((1, rows), lambda i, s, h: (0, 0)),
             ],
-            out_specs=pl.BlockSpec((bq, HD), lambda i, s: (i, 0)),
+            out_specs=pl.BlockSpec((bq, HD), lambda i, s, h: (i, 0)),
         ),
         compiler_params=pltpu.CompilerParams(dimension_semantics=("arbitrary",)),
-    )(starts, query_head, key_head, value_head, seg_col, seg_row)
+    )(starts, kv_head, query_head, pair_all, pair_all, seg_col, seg_row)
 
 
 def layer(queries, keys_values, out_weight, residual, segments):
@@ -96,9 +96,10 @@
     query_parts = lax.all_to_all(head_major, "seq", split_axis=0, concat_axis=0, tiled=True)
     query_head = query_parts.reshape(n_seq * tok_dev, HD)
     assert query_head.shape[0] == L
-    pair_all = lax.all_gather(keys_values, "seq", axis=0, tiled=True)
-    pair_head = lax.dynamic_slice_in_dim(pair_all, (seq_idx // group_size) * HD, HD, axis=2)
-    heads_out = flash(query_head, pair_head[:, 0, :], pair_head[:, 1, :], segments)
+    pair_major = jnp.transpose(keys_values, (1, 0, 2))
+    pair_all = lax.all_gather(pair_major, "seq", axis=1, tiled=True)
+    kv_head = (seq_idx // group_size).astype(jnp.int32).reshape(1)
+    heads_out = flash(query_head, pair_all, kv_head, segments)
     out_rows = heads_out.shape[0] // n_ten
     row_parts = lax.all_to_all(heads_out.reshape(n_ten, out_rows, HD), "tensor", split_axis=0, concat_axis=0, tiled=True)
     token_major = jnp.transpose(row_parts, (1, 0, 2))

time: 270 us -> 263 us (0.974)
  local copies, waits for them, and re-layouts: 32.5 us -> 28.5 us
  Pallas kernels: 31.4 us -> 28.3 us
    all_to_all x1, waiting for transfers between devices: 0.01 us -> 24.4 us  [layer(): lax.all_to_all(head_major, 'seq', split_axis=0, concat_axis=0, tiled=True)]
    all_gather x1, waiting for transfers between devices: 39.6 us -> 15.2 us  [layer(): pair_all = lax.all_gather(pair_major, 'seq', axis=1, tiled=True)]
    pallas_call x1, Pallas kernels: 31.4 us -> 28.3 us  [flash(): pl.pallas_call(kernel, out_shape=jax.ShapeDtypeStruct((rows, HD), jnp.bfl...]
    squeeze x1 -> x0, local copies, waits for them, and re-layouts: 3.03 us -> none  [layer(): pair_head[:, 1, :]]
  transfers between devices with their start and end apart: 6 -> 6, of which waited for: 4 -> 5; matrix products, arithmetic and copies ran while one was open for 15% -> 14% of each run, Pallas kernels for 0% -> 0%
where the time goes in v11:
time: 263 us; the launch traced here: 262 us
  waiting for transfers between devices  132 us (50%)
  local copies, waits for them, and re-layouts  28.5 us (11%)
  Pallas kernels  28.3 us (11%)
  blocking collectives  18.5 us (7%)
  matrix products  15.7 us (6%)
  between operations  13.5 us (5%)
  other arithmetic  12.8 us (5%)
  starting transfers between devices  12.2 us (5%)
    ppermute x3, waiting for transfers between devices, layer(): lax.ppermute(out_weight, 'tensor', [(j, (j + shift) % n_ten) for j in ran...  92.9 us
    pallas_call x1, Pallas kernels, flash(): pl.pallas_call(kernel, out_shape=jax.ShapeDtypeStruct((rows, HD), jnp.bfl...  28.3 us
    all_to_all x1, waiting for transfers between devices, layer(): lax.all_to_all(head_major, 'seq', split_axis=0, concat_axis=0, tiled=True)  24.4 us
    all_to_all x1, blocking collectives, layer(): lax.all_to_all(heads_out.reshape(n_ten, out_rows, HD), 'tensor', split_ax...  18.5 us
    dot_general x1, matrix products, layer(): jnp.dot(gathered, weight_all, preferred_element_type=jnp.float32)  15.7 us
    all_gather x1, waiting for transfers between devices, layer(): pair_all = lax.all_gather(pair_major, 'seq', axis=1, tiled=True)  15.2 us
    gather x3, local copies, waits for them, and re-layouts, layer(): jnp.take(by_shift, source, axis=0)  13.5 us
    all_to_all x1, starting transfers between devices, layer(): lax.all_to_all(head_major, 'seq', split_axis=0, concat_axis=0, tiled=True)  9.97 us
  transfers between devices with their start and end apart: 6, of which 5 were waited for; matrix products, arithmetic and copies ran while one was open for 14% of the time, Pallas kernels for 0%

profile of v11, /device:TPU:1, one launch (start us, length us, event | category | flops | bytes accessed | tf_op | source)
XLA Modules:
  0.0 262.4 jit_solution(12879382432726721136)
XLA Ops:
  6.5 0.0 copy-start
  6.5 0.0 copy-start.2
  6.5 0.0 all-gather.4.cloned.1.call-start
  6.5 1.8 copy.15
  8.3 0.0 all-gather.4.cloned.1.call-update
  8.3 0.0 copy-done
  8.3 1.2 bitcast_bitcast_fusion
  9.6 10.0 %all-to-all-start = ((bf16[16,256,128]{2,1,0:T(8,128)(2,1)}), bf16[16,256,128]{2,1,0:T(8,128)(2,1)S(1)}, u32[]{:S(2)}, u32[]{:S(2)}) async-start(bf16[16,256,128]{2,1,0:T(8,128)(2,1)} %bitcast_bitcast_fusion), calls=%async_computation | async-start | bytes 2097152 | tf_op jit(solution)/shard_map/all_to_all | solution.py:96
  19.6 0.0 all-gather.6.cloned.1.call-start
  19.6 0.0 copy-done.2
  19.6 0.1 slice.3
  19.7 9.0 %while.24 = (s32[]{:T(128)}, u32[8]{0:T(128)S(1)}, u32[8]{0:T(128)S(1)}, s32[4096]{0:T(1024)S(1)}, s32[8]{0:T(128)S(1)}, /*index=5*/s32[]{:T(128)}, s32[]{:T(128)}, s32[]{}) while((s32[]{:T(128)}, u32[8]{0:T(128)S(1)}, u32[8]{0:T(128)S(1)}, s32[4096]{0:T(1024)S(1)}, s32[8]{0:T(128)S(1)}, /*index=5*/s32[]{:T(128)}, s32[]{:T(128)}, ...), condition=%wide.region_1.2_spmd.clone, body=%wide.region_0.1_spmd.clone.sunk | while | flops 1132 | bytes 4628 | solution.py:56
  19.7 0.6 gather_fusion
  20.4 0.6 gather_fusion
  21.1 0.6 gather_fusion
  21.8 0.6 gather_fusion
  22.5 0.6 gather_fusion
  23.2 0.6 gather_fusion
  23.9 0.6 gather_fusion
  24.6 0.6 gather_fusion
  25.3 0.6 gather_fusion
  26.0 0.6 gather_fusion
  26.7 0.6 gather_fusion
  27.4 0.6 gather_fusion
  28.1 0.6 gather_fusion
  28.8 2.0 copy.10.segq_ref
  30.8 0.6 and_select_fusion.2.starts_ref
  31.3 24.4 %all-to-all-done = bf16[16,256,128]{2,1,0:T(8,128)(2,1)S(1)} async-done(((bf16[16,256,128]{2,1,0:T(8,128)(2,1)}), bf16[16,256,128]{2,1,0:T(8,128)(2,1)S(1)}, u32[]{:S(2)}, u32[]{:S(2)}) %all-to-all-start) | async-done | bytes 1048608 | tf_op jit(solution)/shard_map/all_to_all | solution.py:96
  55.7 0.0 copy-start.3
  55.7 15.2 %all-gather.4.cloned.1.call-done.k_ref.v_ref = bf16[2,4096,256]{2,1,0:T(8,128)(2,1)} async-done(((bf16[2,256,256]{2,1,0:T(8,128)(2,1)}), bf16[2,4096,256]{2,1,0:T(8,128)(2,1)}) %all-gather.4.cloned.1.call-update) | async-done | bytes 4194320 | tf_op jit(solution)/shard_map/all_gather | solution.py:100
  70.9 0.0 copy-done.3
  70.9 28.3 %shard_map.55 = bf16[4096,128]{1,0:T(8,128)(2,1)} custom-call(s32[8]{0:T(128)} %and_select_fusion.2.starts_ref, s32[1]{0:T(128)} %bitcast.head_ref, bf16[4096,128]{1,0:T(8,128)(2,1)} %bitcast.29, bf16[2,4096,256]{2,1,0:T(8,128)(2,1)} %all-gather.4.cloned.1.call-done.k_ref.v_ref, bf16[2,4096,256]{2,1,0:T(8,128)(2,1)} %all-gather.4.cloned.1.call-done.k_ref.v_ref, ...), custom_call_target="tpu_custom_call" | custom-call | tf_op jit(solution)/shard_map/pallas_call | solution.py:60
  99.3 0.0 copy-start.4
  99.3 1.6 copy.11
  100.9 18.5 %all_to_all.10 = bf16[4,1024,128]{1,2,0:T(8,128)(2,1)} all-to-all(bf16[4,1024,128]{1,2,0:T(8,128)(2,1)S(1)} %copy.11), channel_id=1, replica_groups=mesh['dp'=4,'seq'=16,'tensor'=4] {'tensor'}, dimensions={0} | all-to-all | bytes 2097152 | tf_op jit(solution)/shard_map/all_to_all | solution.py:104
  119.4 0.0 all-gather.6.cloned.1.call-update
  119.4 0.0 copy-done.4
  119.4 1.0 collective-permute-start.2
  120.4 1.2 collective-permute-start.1
  121.6 0.0 collective-permute-start
  121.6 43.7 %collective-permute-done.2 = bf16[2048,512]{1,0:T(8,128)(2,1)} collective-permute-done((bf16[2048,512]{1,0:T(8,128)(2,1)S(1)}, bf16[2048,512]{1,0:T(8,128)(2,1)}, u32[]{:S(2)}, u32[]{:S(2)}) %collective-permute-start.2) | collective-permute-done | bytes 2097184 | tf_op jit(solution)/shard_map/ppermute | solution.py:89
  165.4 2.2 collective-permute-done.1
  167.5 47.0 %collective-permute-done = bf16[2048,512]{1,0:T(8,128)(2,1)} collective-permute-done((bf16[2048,512]{1,0:T(8,128)(2,1)S(1)}, bf16[2048,512]{1,0:T(8,128)(2,1)}, u32[]{:S(2)}, u32[]{:S(2)}) %collective-permute-start) | collective-permute-done | bytes 2097184 | tf_op jit(solution)/shard_map/ppermute | solution.py:89
  214.5 3.8 %pad_maximum_fusion = bf16[4,2048,512]{2,1,0:T(8,128)(2,1)S(1)} fusion(bf16[1,2048,512]{2,1,0:T(8,128)(2,1)} %bitcast.12, bf16[1,2048,512]{2,1,0:T(8,128)(2,1)} %bitcast.11, bf16[1,2048,512]{2,1,0:T(8,128)(2,1)} %bitcast.10, bf16[1,2048,512]{2,1,0:T(8,128)(2,1)S(1)} %bitcast.32), kind=kLoop, calls=%fused_computation.9 | loop fusion | flops 12582912 | bytes 16777216 | tf_op jit(solution)/shard_map/stack | solution.py:92
  218.3 3.5 %fusion.3 = (bf16[4,1024,512]{2,1,0:T(8,128)(2,1)}, bf16[4,1024,512]{2,1,0:T(8,128)(2,1)}) fusion(bf16[4,2048,512]{2,1,0:T(8,128)(2,1)S(1)} %pad_maximum_fusion), kind=kLoop, calls=%fused_computation.31 | loop fusion | bytes 16777216 | tf_op jit(solution)/shard_map/jit(_take)/gather | solution.py:94
  221.9 5.0 %gather_fusion.2 = bf16[4,1024,512]{2,1,0:T(8,128)(2,1)} fusion(bf16[4,1024,512]{2,1,0:T(8,128)(2,1)} %get-tuple-element.102, s32[1024]{0:T(1024)S(1)} %pad_clamp_fusion.1), kind=kCustom, calls=%fused_computation.2 | custom fusion | bytes 8388624 | tf_op jit(solution)/shard_map/jit(_take)/gather | solution.py:94
  226.9 4.9 %gather_fusion.1 = bf16[4,1024,512]{2,1,0:T(8,128)(2,1)} fusion(bf16[4,1024,512]{2,1,0:T(8,128)(2,1)} %get-tuple-element.101, s32[1024]{0:T(1024)S(1)} %pad_clamp_fusion.1), kind=kCustom, calls=%fused_computation.1 | custom fusion | bytes 8388624 | tf_op jit(solution)/shard_map/jit(_take)/gather | solution.py:94
  231.8 0.0 copy-start.5
  231.8 8.0 %maximum_select_fusion = bf16[4,2048,512]{2,1,0:T(8,128)(2,1)} fusion(bf16[4,1024,512]{2,1,0:T(8,128)(2,1)} %gather_fusion.2, bf16[4,1024,512]{2,1,0:T(8,128)(2,1)} %gather_fusion.1, pred[4]{0:T(512)(128)(4,1)S(1)} %compare_and_fusion), kind=kLoop, calls=%fused_computation.10 | loop fusion | flops 20971520 | bytes 16777220 | tf_op jit(solution)/shard_map/jit(_take)/select_n | solution.py:94
  239.8 0.0 all-gather.6.cloned.1.call-done
  239.8 0.0 copy-done.5
  239.8 0.0 copy-start.1
  239.8 15.7 %add_convert_fusion = bf16[1024,512]{1,0:T(8,128)(2,1)} fusion(bf16[1024,512]{1,0:T(8,128)(2,1)S(1)} %copy-done.5, bf16[1024,8192]{0,1:T(8,128)(2,1)} %bitcast.34, bf16[8192,512]{1,0:T(8,128)(2,1)} %bitcast.28), kind=kOutput, calls=%fused_computation.11 | convolution fusion | flops 8591507456 | bytes 27262976 | tf_op jit(solution)/shard_map/dot_general | solution.py:107
  255.5 0.0 copy-done.1
  (44 shorter events, 0.4 us)
Async XLA Ops:
  6.5 1.8 copy-start
  6.5 13.1 %copy-start.2 = (s32[4096]{0:T(1024)S(1)}, s32[4096]{0:T(1024)}, u32[]{:S(2)}) copy-start(s32[4096]{0:T(1024)} %param.11) | copy-start | bytes 49156
  6.5 64.4 %all-gather.4.cloned.1.call-start = ((), (), s32[]{:S(2)}) async-start(), calls=%async_computation.2 | async-start | bytes 4456448 | tf_op jit(solution)/shard_map/all_gather | solution.py:100
  9.6 46.1 %all-to-all-start = ((bf16[16,256,128]{2,1,0:T(8,128)(2,1)}), bf16[16,256,128]{2,1,0:T(8,128)(2,1)S(1)}, u32[]{:S(2)}, u32[]{:S(2)}) async-start(bf16[16,256,128]{2,1,0:T(8,128)(2,1)} %bitcast_bitcast_fusion), calls=%async_computation | async-start | bytes 2097152 | tf_op jit(solution)/shard_map/all_to_all | solution.py:96
  19.6 220.3 %all-gather.6.cloned.1.call-start = ((), (), s32[]{:S(2)}) async-start(), calls=%async_computation.3 | async-start | bytes 17825792 | tf_op jit(solution)/shard_map/all_gather | solution.py:106
  55.7 15.2 %copy-start.3 = (bf16[16,256,128]{2,1,0:T(8,128)(2,1)}, bf16[16,256,128]{2,1,0:T(8,128)(2,1)S(1)}, u32[]{:S(2)}) copy-start(bf16[16,256,128]{2,1,0:T(8,128)(2,1)S(1)} %all-to-all-done) | copy-start | bytes 3145732
  99.3 20.2 %copy-start.4 = (bf16[2048,512]{1,0:T(8,128)(2,1)S(1)}, bf16[2048,512]{1,0:T(8,128)(2,1)}, u32[]{:S(2)}) copy-start(bf16[2048,512]{1,0:T(8,128)(2,1)} %param.9) | copy-start | bytes 6291460
  119.4 45.9 %collective-permute-start.2 = (bf16[2048,512]{1,0:T(8,128)(2,1)S(1)}, bf16[2048,512]{1,0:T(8,128)(2,1)}, u32[]{:S(2)}, u32[]{:S(2)}) collective-permute-start(bf16[2048,512]{1,0:T(8,128)(2,1)S(1)} %copy-done.4), channel_id=1, source_target_pairs={{0,3},{1,0},{2,1},{3,2},{4,7},{5,4},{6,5},{7,6},{8,11},{9,8},{10,9... | collective-permute-start | bytes 6291464 | tf_op jit(solution)/shard_map/ppermute | solution.py:89
  120.4 47.1 %collective-permute-start.1 = (bf16[2048,512]{1,0:T(8,128)(2,1)S(1)}, bf16[2048,512]{1,0:T(8,128)(2,1)}, u32[]{:S(2)}, u32[]{:S(2)}) collective-permute-start(bf16[2048,512]{1,0:T(8,128)(2,1)S(1)} %copy-done.4), channel_id=1, source_target_pairs={{0,2},{1,3},{2,0},{3,1},{4,6},{5,7},{6,4},{7,5},{8,10},{9,11},{10,... | collective-permute-start | bytes 6291464 | tf_op jit(solution)/shard_map/ppermute | solution.py:89
  121.6 92.9 %collective-permute-start = (bf16[2048,512]{1,0:T(8,128)(2,1)S(1)}, bf16[2048,512]{1,0:T(8,128)(2,1)}, u32[]{:S(2)}, u32[]{:S(2)}) collective-permute-start(bf16[2048,512]{1,0:T(8,128)(2,1)S(1)} %copy-done.4), channel_id=1, source_target_pairs={{0,1},{1,2},{2,3},{3,0},{4,5},{5,6},{6,7},{7,4},{8,9},{9,10},{10,1... | collective-permute-start | bytes 6291464 | tf_op jit(solution)/shard_map/ppermute | solution.py:89
  231.8 8.0 %copy-start.5 = (bf16[1024,512]{1,0:T(8,128)(2,1)S(1)}, bf16[1024,512]{1,0:T(8,128)(2,1)}, u32[]{:S(2)}) copy-start(bf16[1024,512]{1,0:T(8,128)(2,1)} %param.10) | copy-start | bytes 3145732
  239.8 15.7 %copy-start.1 = (bf16[256,2048]{1,0:T(8,128)(2,1)S(1)}, bf16[256,2048]{1,0:T(8,128)(2,1)}, u32[]{:S(2)}) copy-start(bf16[256,2048]{1,0:T(8,128)(2,1)} %param.7) | copy-start | bytes 3145732
Sparse Core Ops, SparseCore 0:
  9.2 61.6 all-gather.3
  119.5 91.7 all-gather.5

commit v12 on v11

--- a/solution.py
+++ b/solution.py
@@ -18,7 +18,7 @@
     seg_q = segq_ref[...]
     row_pos = qi * bq + lax.broadcasted_iota(jnp.int32, (bq, bk), 0)
 
-    def body(kb, carry):
+    def body(kb, carry, causal=False):
         m_prev, l_prev, acc_prev = carry
         start = pl.multiple_of(kb * bk, bk)
         k_blk = k_ref[pl.ds(start, bk), :]
@@ -27,8 +27,10 @@
         scores = lax.dot_general(
             q, k_blk, (((1,), (1,)), ((), ())), preferred_element_type=jnp.float32
         ) * (HD ** -0.5)
-        col_pos = start + lax.broadcasted_iota(jnp.int32, (bq, bk), 1)
-        allowed = (col_pos <= row_pos) & (seg_q == seg_k)
+        allowed = seg_q == seg_k
+        if causal:
+            col_pos = start + lax.broadcasted_iota(jnp.int32, (bq, bk), 1)
+            allowed = allowed & (col_pos <= row_pos)
         masked = jnp.where(allowed, scores, -1e30)
         m_new = jnp.maximum(m_prev, jnp.max(masked, axis=1, keepdims=True))
         alpha = jnp.exp(m_prev - m_new)
@@ -44,8 +46,9 @@
         jnp.zeros((bq, 1), jnp.float32),
         jnp.zeros((bq, HD), jnp.float32),
     )
-    last = (qi * bq + bq - 1) // bk
-    _, l_fin, acc_fin = lax.fori_loop(starts_ref[qi], last + 1, body, init)
+    assert bq == bk
+    carry = lax.fori_loop(starts_ref[qi], qi, body, init)
+    _, l_fin, acc_fin = body(qi, carry, causal=True)
     o_ref[...] = (acc_fin / l_fin).astype(o_ref.dtype)
 
 

time: 263 us -> 261 us (level)
  transfers between devices with their start and end apart: 6 -> 6, of which waited for: 5 -> 5; matrix products, arithmetic and copies ran while one was open for 14% -> 15% of each run, Pallas kernels for 0% -> 0%
where the time goes in v12:
time: 261 us; the launch traced here: 260 us
  waiting for transfers between devices  132 us (51%)
  local copies, waits for them, and re-layouts  28.5 us (11%)
  Pallas kernels  26.3 us (10%)
  blocking collectives  18.5 us (7%)
  matrix products  15.7 us (6%)
  between operations  13.5 us (5%)
  other arithmetic  12.8 us (5%)
  starting transfers between devices  12.2 us (5%)
    ppermute x3, waiting for transfers between devices, layer(): lax.ppermute(out_weight, 'tensor', [(j, (j + shift) % n_ten) for j in ran...  92.9 us
    pallas_call x1, Pallas kernels, flash(): pl.pallas_call(kernel, out_shape=jax.ShapeDtypeStruct((rows, HD), jnp.bfl...  26.3 us
    all_to_all x1, waiting for transfers between devices, layer(): lax.all_to_all(head_major, 'seq', split_axis=0, concat_axis=0, tiled=True)  24.4 us
    all_to_all x1, blocking collectives, layer(): lax.all_to_all(heads_out.reshape(n_ten, out_rows, HD), 'tensor', split_ax...  18.5 us
    dot_general x1, matrix products, layer(): jnp.dot(gathered, weight_all, preferred_element_type=jnp.float32)  15.7 us
    all_gather x1, waiting for transfers between devices, layer(): pair_all = lax.all_gather(pair_major, 'seq', axis=1, tiled=True)  15.2 us
    gather x3, local copies, waits for them, and re-layouts, layer(): jnp.take(by_shift, source, axis=0)  13.5 us
    all_to_all x1, starting transfers between devices, layer(): lax.all_to_all(head_major, 'seq', split_axis=0, concat_axis=0, tiled=True)  9.97 us
  transfers between devices with their start and end apart: 6, of which 5 were waited for; matrix products, arithmetic and copies ran while one was open for 15% of the time, Pallas kernels for 0%

profile of v12, /device:TPU:1, one launch (start us, length us, event | category | flops | bytes accessed | tf_op | source)
XLA Modules:
  0.0 260.4 jit_solution(12182369045797473654)
XLA Ops:
  6.5 0.0 copy-start
  6.5 0.0 copy-start.2
  6.5 0.0 all-gather.4.cloned.1.call-start
  6.5 1.8 copy.15
  8.3 0.0 all-gather.4.cloned.1.call-update
  8.3 0.0 copy-done
  8.3 1.2 bitcast_bitcast_fusion
  9.6 10.0 %all-to-all-start = ((bf16[16,256,128]{2,1,0:T(8,128)(2,1)}), bf16[16,256,128]{2,1,0:T(8,128)(2,1)S(1)}, u32[]{:S(2)}, u32[]{:S(2)}) async-start(bf16[16,256,128]{2,1,0:T(8,128)(2,1)} %bitcast_bitcast_fusion), calls=%async_computation | async-start | bytes 2097152 | tf_op jit(solution)/shard_map/all_to_all | solution.py:99
  19.6 0.0 all-gather.6.cloned.1.call-start
  19.6 0.0 copy-done.2
  19.6 0.1 slice.3
  19.7 9.0 %while.24 = (s32[]{:T(128)}, u32[8]{0:T(128)S(1)}, u32[8]{0:T(128)S(1)}, s32[4096]{0:T(1024)S(1)}, s32[8]{0:T(128)S(1)}, /*index=5*/s32[]{:T(128)}, s32[]{:T(128)}, s32[]{}) while((s32[]{:T(128)}, u32[8]{0:T(128)S(1)}, u32[8]{0:T(128)S(1)}, s32[4096]{0:T(1024)S(1)}, s32[8]{0:T(128)S(1)}, /*index=5*/s32[]{:T(128)}, s32[]{:T(128)}, ...), condition=%wide.region_1.2_spmd.clone, body=%wide.region_0.1_spmd.clone.sunk | while | flops 1132 | bytes 4628 | solution.py:59
  19.7 0.6 gather_fusion
  20.4 0.6 gather_fusion
  21.1 0.6 gather_fusion
  21.8 0.6 gather_fusion
  22.5 0.6 gather_fusion
  23.2 0.6 gather_fusion
  23.9 0.6 gather_fusion
  24.6 0.6 gather_fusion
  25.3 0.6 gather_fusion
  26.0 0.6 gather_fusion
  26.7 0.6 gather_fusion
  27.4 0.6 gather_fusion
  28.1 0.6 gather_fusion
  28.8 2.0 copy.10.segq_ref
  30.8 0.6 and_select_fusion.2.starts_ref
  31.3 24.4 %all-to-all-done = bf16[16,256,128]{2,1,0:T(8,128)(2,1)S(1)} async-done(((bf16[16,256,128]{2,1,0:T(8,128)(2,1)}), bf16[16,256,128]{2,1,0:T(8,128)(2,1)S(1)}, u32[]{:S(2)}, u32[]{:S(2)}) %all-to-all-start) | async-done | bytes 1048608 | tf_op jit(solution)/shard_map/all_to_all | solution.py:99
  55.7 0.0 copy-start.3
  55.7 15.2 %all-gather.4.cloned.1.call-done.k_ref.v_ref = bf16[2,4096,256]{2,1,0:T(8,128)(2,1)} async-done(((bf16[2,256,256]{2,1,0:T(8,128)(2,1)}), bf16[2,4096,256]{2,1,0:T(8,128)(2,1)}) %all-gather.4.cloned.1.call-update) | async-done | bytes 4194320 | tf_op jit(solution)/shard_map/all_gather | solution.py:103
  70.9 0.0 copy-done.3
  70.9 26.3 %shard_map.55 = bf16[4096,128]{1,0:T(8,128)(2,1)} custom-call(s32[8]{0:T(128)} %and_select_fusion.2.starts_ref, s32[1]{0:T(128)} %bitcast.head_ref, bf16[4096,128]{1,0:T(8,128)(2,1)} %bitcast.29, bf16[2,4096,256]{2,1,0:T(8,128)(2,1)} %all-gather.4.cloned.1.call-done.k_ref.v_ref, bf16[2,4096,256]{2,1,0:T(8,128)(2,1)} %all-gather.4.cloned.1.call-done.k_ref.v_ref, ...), custom_call_target="tpu_custom_call" | custom-call | tf_op jit(solution)/shard_map/pallas_call | solution.py:63
  97.3 0.0 copy-start.4
  97.3 1.6 copy.11
  98.9 18.5 %all_to_all.10 = bf16[4,1024,128]{1,2,0:T(8,128)(2,1)} all-to-all(bf16[4,1024,128]{1,2,0:T(8,128)(2,1)S(1)} %copy.11), channel_id=1, replica_groups=mesh['dp'=4,'seq'=16,'tensor'=4] {'tensor'}, dimensions={0} | all-to-all | bytes 2097152 | tf_op jit(solution)/shard_map/all_to_all | solution.py:107
  117.4 0.0 all-gather.6.cloned.1.call-update
  117.4 0.0 copy-done.4
  117.4 1.0 collective-permute-start.2
  118.4 1.2 collective-permute-start.1
  119.6 0.0 collective-permute-start
  119.6 43.7 %collective-permute-done.2 = bf16[2048,512]{1,0:T(8,128)(2,1)} collective-permute-done((bf16[2048,512]{1,0:T(8,128)(2,1)S(1)}, bf16[2048,512]{1,0:T(8,128)(2,1)}, u32[]{:S(2)}, u32[]{:S(2)}) %collective-permute-start.2) | collective-permute-done | bytes 2097184 | tf_op jit(solution)/shard_map/ppermute | solution.py:92
  163.4 2.2 collective-permute-done.1
  165.5 47.0 %collective-permute-done = bf16[2048,512]{1,0:T(8,128)(2,1)} collective-permute-done((bf16[2048,512]{1,0:T(8,128)(2,1)S(1)}, bf16[2048,512]{1,0:T(8,128)(2,1)}, u32[]{:S(2)}, u32[]{:S(2)}) %collective-permute-start) | collective-permute-done | bytes 2097184 | tf_op jit(solution)/shard_map/ppermute | solution.py:92
  212.5 3.8 %pad_maximum_fusion = bf16[4,2048,512]{2,1,0:T(8,128)(2,1)S(1)} fusion(bf16[1,2048,512]{2,1,0:T(8,128)(2,1)} %bitcast.12, bf16[1,2048,512]{2,1,0:T(8,128)(2,1)} %bitcast.11, bf16[1,2048,512]{2,1,0:T(8,128)(2,1)} %bitcast.10, bf16[1,2048,512]{2,1,0:T(8,128)(2,1)S(1)} %bitcast.32), kind=kLoop, calls=%fused_computation.9 | loop fusion | flops 12582912 | bytes 16777216 | tf_op jit(solution)/shard_map/stack | solution.py:95
  216.4 3.5 %fusion.3 = (bf16[4,1024,512]{2,1,0:T(8,128)(2,1)}, bf16[4,1024,512]{2,1,0:T(8,128)(2,1)}) fusion(bf16[4,2048,512]{2,1,0:T(8,128)(2,1)S(1)} %pad_maximum_fusion), kind=kLoop, calls=%fused_computation.31 | loop fusion | bytes 16777216 | tf_op jit(solution)/shard_map/jit(_take)/gather | solution.py:97
  219.9 5.0 %gather_fusion.2 = bf16[4,1024,512]{2,1,0:T(8,128)(2,1)} fusion(bf16[4,1024,512]{2,1,0:T(8,128)(2,1)} %get-tuple-element.102, s32[1024]{0:T(1024)S(1)} %pad_clamp_fusion.1), kind=kCustom, calls=%fused_computation.2 | custom fusion | bytes 8388624 | tf_op jit(solution)/shard_map/jit(_take)/gather | solution.py:97
  224.9 4.9 %gather_fusion.1 = bf16[4,1024,512]{2,1,0:T(8,128)(2,1)} fusion(bf16[4,1024,512]{2,1,0:T(8,128)(2,1)} %get-tuple-element.101, s32[1024]{0:T(1024)S(1)} %pad_clamp_fusion.1), kind=kCustom, calls=%fused_computation.1 | custom fusion | bytes 8388624 | tf_op jit(solution)/shard_map/jit(_take)/gather | solution.py:97
  229.8 0.0 copy-start.5
  229.8 8.0 %maximum_select_fusion = bf16[4,2048,512]{2,1,0:T(8,128)(2,1)} fusion(bf16[4,1024,512]{2,1,0:T(8,128)(2,1)} %gather_fusion.2, bf16[4,1024,512]{2,1,0:T(8,128)(2,1)} %gather_fusion.1, pred[4]{0:T(512)(128)(4,1)S(1)} %compare_and_fusion), kind=kLoop, calls=%fused_computation.10 | loop fusion | flops 20971520 | bytes 16777220 | tf_op jit(solution)/shard_map/jit(_take)/select_n | solution.py:97
  237.8 0.0 all-gather.6.cloned.1.call-done
  237.8 0.0 copy-done.5
  237.8 0.0 copy-start.1
  237.8 15.7 %add_convert_fusion = bf16[1024,512]{1,0:T(8,128)(2,1)} fusion(bf16[1024,512]{1,0:T(8,128)(2,1)S(1)} %copy-done.5, bf16[1024,8192]{0,1:T(8,128)(2,1)} %bitcast.34, bf16[8192,512]{1,0:T(8,128)(2,1)} %bitcast.28), kind=kOutput, calls=%fused_computation.11 | convolution fusion | flops 8591507456 | bytes 27262976 | tf_op jit(solution)/shard_map/dot_general | solution.py:110
  253.5 0.0 copy-done.1
  (44 shorter events, 0.4 us)
Async XLA Ops:
  6.5 1.8 copy-start
  6.5 13.1 %copy-start.2 = (s32[4096]{0:T(1024)S(1)}, s32[4096]{0:T(1024)}, u32[]{:S(2)}) copy-start(s32[4096]{0:T(1024)} %param.11) | copy-start | bytes 49156
  6.5 64.4 %all-gather.4.cloned.1.call-start = ((), (), s32[]{:S(2)}) async-start(), calls=%async_computation.2 | async-start | bytes 4456448 | tf_op jit(solution)/shard_map/all_gather | solution.py:103
  9.6 46.1 %all-to-all-start = ((bf16[16,256,128]{2,1,0:T(8,128)(2,1)}), bf16[16,256,128]{2,1,0:T(8,128)(2,1)S(1)}, u32[]{:S(2)}, u32[]{:S(2)}) async-start(bf16[16,256,128]{2,1,0:T(8,128)(2,1)} %bitcast_bitcast_fusion), calls=%async_computation | async-start | bytes 2097152 | tf_op jit(solution)/shard_map/all_to_all | solution.py:99
  19.6 218.3 %all-gather.6.cloned.1.call-start = ((), (), s32[]{:S(2)}) async-start(), calls=%async_computation.3 | async-start | bytes 17825792 | tf_op jit(solution)/shard_map/all_gather | solution.py:109
  55.7 15.2 %copy-start.3 = (bf16[16,256,128]{2,1,0:T(8,128)(2,1)}, bf16[16,256,128]{2,1,0:T(8,128)(2,1)S(1)}, u32[]{:S(2)}) copy-start(bf16[16,256,128]{2,1,0:T(8,128)(2,1)S(1)} %all-to-all-done) | copy-start | bytes 3145732
  97.3 20.2 %copy-start.4 = (bf16[2048,512]{1,0:T(8,128)(2,1)S(1)}, bf16[2048,512]{1,0:T(8,128)(2,1)}, u32[]{:S(2)}) copy-start(bf16[2048,512]{1,0:T(8,128)(2,1)} %param.9) | copy-start | bytes 6291460
  117.4 45.9 %collective-permute-start.2 = (bf16[2048,512]{1,0:T(8,128)(2,1)S(1)}, bf16[2048,512]{1,0:T(8,128)(2,1)}, u32[]{:S(2)}, u32[]{:S(2)}) collective-permute-start(bf16[2048,512]{1,0:T(8,128)(2,1)S(1)} %copy-done.4), channel_id=1, source_target_pairs={{0,3},{1,0},{2,1},{3,2},{4,7},{5,4},{6,5},{7,6},{8,11},{9,8},{10,9... | collective-permute-start | bytes 6291464 | tf_op jit(solution)/shard_map/ppermute | solution.py:92
  118.4 47.1 %collective-permute-start.1 = (bf16[2048,512]{1,0:T(8,128)(2,1)S(1)}, bf16[2048,512]{1,0:T(8,128)(2,1)}, u32[]{:S(2)}, u32[]{:S(2)}) collective-permute-start(bf16[2048,512]{1,0:T(8,128)(2,1)S(1)} %copy-done.4), channel_id=1, source_target_pairs={{0,2},{1,3},{2,0},{3,1},{4,6},{5,7},{6,4},{7,5},{8,10},{9,11},{10,... | collective-permute-start | bytes 6291464 | tf_op jit(solution)/shard_map/ppermute | solution.py:92
  119.6 92.9 %collective-permute-start = (bf16[2048,512]{1,0:T(8,128)(2,1)S(1)}, bf16[2048,512]{1,0:T(8,128)(2,1)}, u32[]{:S(2)}, u32[]{:S(2)}) collective-permute-start(bf16[2048,512]{1,0:T(8,128)(2,1)S(1)} %copy-done.4), channel_id=1, source_target_pairs={{0,1},{1,2},{2,3},{3,0},{4,5},{5,6},{6,7},{7,4},{8,9},{9,10},{10,1... | collective-permute-start | bytes 6291464 | tf_op jit(solution)/shard_map/ppermute | solution.py:92
  229.8 8.0 %copy-start.5 = (bf16[1024,512]{1,0:T(8,128)(2,1)S(1)}, bf16[1024,512]{1,0:T(8,128)(2,1)}, u32[]{:S(2)}) copy-start(bf16[1024,512]{1,0:T(8,128)(2,1)} %param.10) | copy-start | bytes 3145732
  237.8 15.7 %copy-start.1 = (bf16[256,2048]{1,0:T(8,128)(2,1)S(1)}, bf16[256,2048]{1,0:T(8,128)(2,1)}, u32[]{:S(2)}) copy-start(bf16[256,2048]{1,0:T(8,128)(2,1)} %param.7) | copy-start | bytes 3145732
Sparse Core Ops, SparseCore 0:
  9.2 61.6 all-gather.3
  117.5 91.9 all-gather.5
